TPU v7x, 128 devices: a whole 4x4x4 slice. The times are simulated.
128 devices in a mesh: ha: 64 (over y, z, x), ta: 2 (over core).
Axes of the slice: x: 4, y: 4, z: 4, core: 2. Of those that a mesh axis runs over, the one named last changes fastest.
Arguments:
- features: bfloat16 [8, 64, 640, 128], P('ta', 'ha'), may hold values from -6 to 6
- cotangent: bfloat16 [8, 64, 640, 128], P('ta', 'ha'), may hold values from -6 to 6
- kernel: bfloat16 [3, 3, 3, 128, 128], replicated, may hold values from -0.109375 to 0.109375
Outputs:
- grad_features: bfloat16 [8, 64, 640, 128], P('ta', 'ha')
- grad_kernel: float32 [3456, 128], P(('ha', 'ta'))
All inputs are finite; a program needn't handle non-finite values.
Results may differ from a plain program's by a relative error of at most 0.003.
Values may be sent and summed in bfloat16 or wider, within the bound.
No kernel may reach another device: no remote copies, remote signals or barrier semaphores. Data moves between devices by JAX's collectives and lax.ppermute only.
A program may use at most 128 MiB of HBM per device.

v0:
```python
import jax
import jax.numpy as jnp
from jax import lax
from jax.sharding import PartitionSpec as P


def passed_along(block, axis, distance):
    devices = range(lax.axis_size(axis))
    route = [(i - distance, i) for i in devices if i - distance in devices]
    return lax.ppermute(block, axis, route)


def with_halo(x, sides, width):
    for axis, dim in sides:
        count, length = (lax.axis_size(axis), x.shape[dim])
        up = [(i, (i + 1) % count) for i in range(count - 1)]
        down = [(j, i) for i, j in up]
        last = lax.slice_in_dim(x, length - width, length, axis=dim)
        leading = lax.slice_in_dim(x, 0, width, axis=dim)
        before = lax.ppermute(last, axis, up)
        after = lax.ppermute(leading, axis, down)
        x = jnp.concatenate([before, x, after], axis=dim)
    return x


def body(features, cotangent, kernel):
    frames, height, breadth, channels = features.shape
    values = features.astype(jnp.float32)
    active = jax.nn.silu(values).astype(jnp.bfloat16)
    future = passed_along(cotangent[:2], "ta", -1)
    cot_ext = jnp.concatenate([cotangent, future], axis=0)
    cot_rows = with_halo(cot_ext, (("ha", 1),), 1)
    cot_pad = jnp.pad(cot_rows, ((0, 0), (0, 0), (1, 1), (0, 0)))
    cot_flat = cotangent.reshape(-1, channels)
    past = passed_along(active[-2:], "ta", 1)
    act_ext = jnp.concatenate([past, active], axis=0)
    act_rows = with_halo(act_ext, (("ha", 1),), 1)
    act_pad = jnp.pad(act_rows, ((0, 0), (0, 0), (1, 1), (0, 0)))
    grad_input = jnp.zeros((frames * height * breadth, channels), jnp.float32)
    blocks = []
    for t_tap in range(3):
        for h_tap in range(3):
            cot_slab = jnp.concatenate(
                [
                    cot_pad[
                        2 - t_tap : 2 - t_tap + frames,
                        2 - h_tap : 2 - h_tap + height,
                        2 - w_tap : 2 - w_tap + breadth,
                    ]
                    for w_tap in range(3)
                ],
                axis=-1,
            ).reshape(-1, 3 * channels)
            stacked = jnp.transpose(kernel[t_tap, h_tap], (0, 2, 1)).reshape(3 * channels, channels)
            grad_input = grad_input + jnp.dot(cot_slab, stacked, preferred_element_type=jnp.float32)
            act_slab = jnp.concatenate(
                [
                    act_pad[t_tap : t_tap + frames, h_tap : h_tap + height, w_tap : w_tap + breadth]
                    for w_tap in range(3)
                ],
                axis=-1,
            ).reshape(-1, 3 * channels)
            blocks.append(
                lax.dot_general(
                    act_slab, cot_flat, (((0,), (0,)), ((), ())), preferred_element_type=jnp.float32
                )
            )
    total_cells = frames * height * breadth * lax.axis_size("ha") * lax.axis_size("ta")
    factor = float(total_cells) ** (-0.5)
    term = jnp.concatenate(blocks, axis=0) * factor
    grad_kernel = lax.psum_scatter(term, ("ha", "ta"), scatter_dimension=0, tiled=True)
    sigmoid_part = jax.nn.sigmoid(values)
    derivative = sigmoid_part * (1.0 + values * (1.0 - sigmoid_part))
    grad_features = (
        cotangent.astype(jnp.float32) + derivative * grad_input.reshape(features.shape)
    ).astype(jnp.bfloat16)
    return (grad_features, grad_kernel)


def solution(mesh):
    placed = (P("ta", "ha", None, None), P("ta", "ha", None, None), P())
    return jax.shard_map(
        body,
        mesh=mesh,
        in_specs=placed,
        out_specs=(P("ta", "ha", None, None), P(("ha", "ta"), None)),
        check_vma=False,
    )
```

profile of v0, /device:TPU:0, one launch (start us, length us, event | category | flops | bytes accessed | tf_op | source)
XLA Modules:
  0.0 501.0 jit_solution(15857602657229989308)
XLA Ops:
  1.6 1.3 collective-permute-start
  2.9 1.1 constant_dynamic-update-slice_fusion.1
  4.1 1.1 collective-permute-done
  5.2 3.6 collective-permute-start.1
  8.8 1.3 collective-permute-start.2
  10.1 2.2 copy.22
  12.2 2.0 fusion.110
  15.3 1.6 copy.36
  16.9 1.6 copy.37
  18.6 1.6 copy.38
  22.7 2.2 copy.23
  25.1 4.9 collective-permute-done.1
  30.0 4.2 collective-permute-done.2
  34.2 1.1 fusion.10
  35.3 3.3 fusion.104
  50.5 1.9 fusion.64
  52.4 1.3 collective-permute-start.3
  53.7 1.2 collective-permute-done.3
  55.0 3.4 collective-permute-start.4
  58.4 1.5 collective-permute-start.5
  60.1 19.8 %collective-permute-done.4 = bf16[6,1,640,128]{2,3,0,1:T(8,128)(2,1)S(1)} collective-permute-done((bf16[6,1,640,128]{2,3,0,1:T(8,128)(2,1)S(1)}, bf16[6,1,640,128]{2,3,0,1:T(8,128)(2,1)S(1)}, u32[]{:S(2)}, u32[]{:S(2)}) %collective-permute-start.4) | collective-permute-done | bytes 983072 | tf_op jit(solution)/shard_map/ppermute | solution.py:20
  79.9 4.2 collective-permute-done.5
  84.1 3.0 select_maximum_fusion
  87.1 3.9 fusion.103
  97.7 329.7 %fusion = f32[32,128]{1,0:T(8,128)S(1)} fusion(f32[3456,128]{1,0:T(8,128)S(1)} %broadcast_multiply_fusion), kind=kCustom, calls=%all-reduce-scatter | all-reduce-scatter fusion | flops 524289 | bytes 1785856
  427.4 1.3 collective-permute-start.10
  428.7 1.3 collective-permute-start.11
  430.0 1.3 collective-permute-start.12
  431.3 1.3 collective-permute-start.13
  432.6 1.3 collective-permute-start.25
  433.9 1.4 collective-permute-done.25
  435.4 1.3 collective-permute-start.14
  436.6 1.3 collective-permute-start.15
  438.0 8.4 %collective-permute-start.16 = (f32[32,128]{1,0:T(8,128)S(1)}, f32[32,128]{1,0:T(8,128)S(1)}, u32[]{:S(2)}, u32[]{:S(2)}) collective-permute-start(f32[32,128]{1,0:T(8,128)S(1)} %fusion), channel_id=1, source_target_pairs={{0,11},{1,12},{2,13},{3,14},{4,15},{5,16},{6,17},{7,18},{8,19},{9,... | collective-permute-start | bytes 49160
  446.4 1.3 collective-permute-start.17
  447.7 1.3 collective-permute-start.18
  449.0 1.3 collective-permute-start.19
  450.3 9.7 %collective-permute-start.20 = (f32[32,128]{1,0:T(8,128)S(1)}, f32[32,128]{1,0:T(8,128)S(1)}, u32[]{:S(2)}, u32[]{:S(2)}) collective-permute-start(f32[32,128]{1,0:T(8,128)S(1)} %fusion), channel_id=1, source_target_pairs={{0,15},{1,16},{2,17},{3,18},{4,19},{5,20},{6,21},{7,22},{8,23},{9,... | collective-permute-start | bytes 49160
  460.0 15.5 %collective-permute-start.21 = (f32[32,128]{1,0:T(8,128)S(1)}, f32[32,128]{1,0:T(8,128)S(1)}, u32[]{:S(2)}, u32[]{:S(2)}) collective-permute-start(f32[32,128]{1,0:T(8,128)S(1)} %fusion), channel_id=1, source_target_pairs={{0,16},{1,17},{2,18},{3,19},{4,20},{5,21},{6,22},{7,23},{8,24},{9,... | collective-permute-start | bytes 49160
  475.5 4.8 collective-permute-start.22
  480.4 1.6 collective-permute-start.23
  482.0 1.7 collective-permute-start.24
  483.7 3.1 collective-permute-start.6
  486.9 3.1 collective-permute-start.7
  490.0 2.4 collective-permute-start.8
  492.4 4.0 collective-permute-start.9
  496.4 1.1 copy.34
  497.9 2.5 concatenate.92
  (76 shorter events, 24.4 us)
Async XLA Ops:
  1.6 3.5 collective-permute-start
  5.2 24.8 %collective-permute-start.1 = (bf16[6,1,640,128]{3,2,1,0:T(8,128)(2,1)S(1)}, bf16[6,1,640,128]{3,2,1,0:T(8,128)(2,1)S(1)}, u32[]{:S(2)}, u32[]{:S(2)}) collective-permute-start(bf16[6,1,640,128]{3,2,1,0:T(8,128)(2,1)S(1)} %constant_dynamic-update-slice_fusion), channel_id=1, source_target_pairs={{0,2},{2,4},{4,6},{6,8},{8,10},{10,12},{12,14},{14,16},{16,18},{18... | collective-permute-start | bytes 2949128 | tf_op jit(solution)/shard_map/ppermute | solution.py:20
  8.8 25.4 %collective-permute-start.2 = (bf16[6,1,640,128]{3,2,1,0:T(8,128)(2,1)S(1)}, bf16[6,1,640,128]{3,2,1,0:T(8,128)(2,1)S(1)}, u32[]{:S(2)}, u32[]{:S(2)}) collective-permute-start(bf16[6,1,640,128]{3,2,1,0:T(8,128)(2,1)S(1)} %constant_dynamic-update-slice_fusion), channel_id=1, source_target_pairs={{2,0},{4,2},{6,4},{8,6},{10,8},{12,10},{14,12},{16,14},{18,16},{20... | collective-permute-start | bytes 2949128 | tf_op jit(solution)/shard_map/ppermute | solution.py:21
  39.4 0.9 copy-start.6
  41.4 0.9 copy-start.5
  42.3 0.9 copy-start.4
  43.9 0.9 copy-start.3
  44.8 0.9 copy-start.2
  45.7 1.1 copy-start
  46.8 0.9 copy-start.1
  52.4 2.5 collective-permute-start.3
  55.0 24.9 %collective-permute-start.4 = (bf16[6,1,640,128]{2,3,0,1:T(8,128)(2,1)S(1)}, bf16[6,1,640,128]{2,3,0,1:T(8,128)(2,1)S(1)}, u32[]{:S(2)}, u32[]{:S(2)}) collective-permute-start(bf16[6,1,640,128]{2,3,0,1:T(8,128)(2,1)S(1)} %pad_maximum_fusion.9), channel_id=1, source_target_pairs={{0,2},{2,4},{4,6},{6,8},{8,10},{10,12},{12,14},{14,16},{16,18},{18... | collective-permute-start | bytes 2949128 | tf_op jit(solution)/shard_map/ppermute | solution.py:20
  58.4 25.6 %collective-permute-start.5 = (bf16[6,1,640,128]{2,3,0,1:T(8,128)(2,1)S(1)}, bf16[6,1,640,128]{2,3,0,1:T(8,128)(2,1)S(1)}, u32[]{:S(2)}, u32[]{:S(2)}) collective-permute-start(bf16[6,1,640,128]{2,3,0,1:T(8,128)(2,1)S(1)} %pad_maximum_fusion.9), channel_id=1, source_target_pairs={{2,0},{4,2},{6,4},{8,6},{10,8},{12,10},{14,12},{16,14},{18,16},{20... | collective-permute-start | bytes 2949128 | tf_op jit(solution)/shard_map/ppermute | solution.py:21
  427.4 9.2 %collective-permute-start.10 = (f32[32,128]{1,0:T(8,128)S(1)}, f32[32,128]{1,0:T(8,128)S(1)}, u32[]{:S(2)}, u32[]{:S(2)}) collective-permute-start(f32[32,128]{1,0:T(8,128)S(1)} %fusion), channel_id=1, source_target_pairs={{0,5},{1,6},{2,7},{3,8},{4,9},{5,10},{6,11},{7,12},{8,13},{9,14},{... | collective-permute-start | bytes 49160
  428.7 9.2 %collective-permute-start.11 = (f32[32,128]{1,0:T(8,128)S(1)}, f32[32,128]{1,0:T(8,128)S(1)}, u32[]{:S(2)}, u32[]{:S(2)}) collective-permute-start(f32[32,128]{1,0:T(8,128)S(1)} %fusion), channel_id=1, source_target_pairs={{0,6},{1,7},{2,8},{3,9},{4,10},{5,11},{6,12},{7,13},{8,14},{9,15},... | collective-permute-start | bytes 49160
  430.0 16.4 %collective-permute-start.12 = (f32[32,128]{1,0:T(8,128)S(1)}, f32[32,128]{1,0:T(8,128)S(1)}, u32[]{:S(2)}, u32[]{:S(2)}) collective-permute-start(f32[32,128]{1,0:T(8,128)S(1)} %fusion), channel_id=1, source_target_pairs={{0,7},{1,8},{2,9},{3,10},{4,11},{5,12},{6,13},{7,14},{8,15},{9,16}... | collective-permute-start | bytes 49160
  431.3 16.4 %collective-permute-start.13 = (f32[32,128]{1,0:T(8,128)S(1)}, f32[32,128]{1,0:T(8,128)S(1)}, u32[]{:S(2)}, u32[]{:S(2)}) collective-permute-start(f32[32,128]{1,0:T(8,128)S(1)} %fusion), channel_id=1, source_target_pairs={{0,8},{1,9},{2,10},{3,11},{4,12},{5,13},{6,14},{7,15},{8,16},{9,17... | collective-permute-start | bytes 49160
  432.6 2.7 collective-permute-start.25
  435.4 13.7 %collective-permute-start.14 = (f32[32,128]{1,0:T(8,128)S(1)}, f32[32,128]{1,0:T(8,128)S(1)}, u32[]{:S(2)}, u32[]{:S(2)}) collective-permute-start(f32[32,128]{1,0:T(8,128)S(1)} %fusion), channel_id=1, source_target_pairs={{0,9},{1,10},{2,11},{3,12},{4,13},{5,14},{6,15},{7,16},{8,17},{9,1... | collective-permute-start | bytes 49160
  436.6 13.7 %collective-permute-start.15 = (f32[32,128]{1,0:T(8,128)S(1)}, f32[32,128]{1,0:T(8,128)S(1)}, u32[]{:S(2)}, u32[]{:S(2)}) collective-permute-start(f32[32,128]{1,0:T(8,128)S(1)} %fusion), channel_id=1, source_target_pairs={{0,10},{1,11},{2,12},{3,13},{4,14},{5,15},{6,16},{7,17},{8,18},{9,... | collective-permute-start | bytes 49160
  438.0 22.1 %collective-permute-start.16 = (f32[32,128]{1,0:T(8,128)S(1)}, f32[32,128]{1,0:T(8,128)S(1)}, u32[]{:S(2)}, u32[]{:S(2)}) collective-permute-start(f32[32,128]{1,0:T(8,128)S(1)} %fusion), channel_id=1, source_target_pairs={{0,11},{1,12},{2,13},{3,14},{4,15},{5,16},{6,17},{7,18},{8,19},{9,... | collective-permute-start | bytes 49160
  446.4 29.1 %collective-permute-start.17 = (f32[32,128]{1,0:T(8,128)S(1)}, f32[32,128]{1,0:T(8,128)S(1)}, u32[]{:S(2)}, u32[]{:S(2)}) collective-permute-start(f32[32,128]{1,0:T(8,128)S(1)} %fusion), channel_id=1, source_target_pairs={{0,12},{1,13},{2,14},{3,15},{4,16},{5,17},{6,18},{7,19},{8,20},{9,... | collective-permute-start | bytes 49160
  447.7 32.6 %collective-permute-start.18 = (f32[32,128]{1,0:T(8,128)S(1)}, f32[32,128]{1,0:T(8,128)S(1)}, u32[]{:S(2)}, u32[]{:S(2)}) collective-permute-start(f32[32,128]{1,0:T(8,128)S(1)} %fusion), channel_id=1, source_target_pairs={{0,13},{1,14},{2,15},{3,16},{4,17},{5,18},{6,19},{7,20},{8,21},{9,... | collective-permute-start | bytes 49160
  449.0 32.9 %collective-permute-start.19 = (f32[32,128]{1,0:T(8,128)S(1)}, f32[32,128]{1,0:T(8,128)S(1)}, u32[]{:S(2)}, u32[]{:S(2)}) collective-permute-start(f32[32,128]{1,0:T(8,128)S(1)} %fusion), channel_id=1, source_target_pairs={{0,14},{1,15},{2,16},{3,17},{4,18},{5,19},{6,20},{7,21},{8,22},{9,... | collective-permute-start | bytes 49160
  450.3 33.4 %collective-permute-start.20 = (f32[32,128]{1,0:T(8,128)S(1)}, f32[32,128]{1,0:T(8,128)S(1)}, u32[]{:S(2)}, u32[]{:S(2)}) collective-permute-start(f32[32,128]{1,0:T(8,128)S(1)} %fusion), channel_id=1, source_target_pairs={{0,15},{1,16},{2,17},{3,18},{4,19},{5,20},{6,21},{7,22},{8,23},{9,... | collective-permute-start | bytes 49160
  460.0 26.8 %collective-permute-start.21 = (f32[32,128]{1,0:T(8,128)S(1)}, f32[32,128]{1,0:T(8,128)S(1)}, u32[]{:S(2)}, u32[]{:S(2)}) collective-permute-start(f32[32,128]{1,0:T(8,128)S(1)} %fusion), channel_id=1, source_target_pairs={{0,16},{1,17},{2,18},{3,19},{4,20},{5,21},{6,22},{7,23},{8,24},{9,... | collective-permute-start | bytes 49160
  475.5 14.4 %collective-permute-start.22 = (f32[32,128]{1,0:T(8,128)S(1)}, f32[32,128]{1,0:T(8,128)S(1)}, u32[]{:S(2)}, u32[]{:S(2)}) collective-permute-start(f32[32,128]{1,0:T(8,128)S(1)} %fusion), channel_id=1, source_target_pairs={{0,17},{1,18},{2,19},{3,20},{4,21},{5,22},{6,23},{7,24},{8,25},{9,... | collective-permute-start | bytes 49160
  480.4 12.0 %collective-permute-start.23 = (f32[32,128]{1,0:T(8,128)S(1)}, f32[32,128]{1,0:T(8,128)S(1)}, u32[]{:S(2)}, u32[]{:S(2)}) collective-permute-start(f32[32,128]{1,0:T(8,128)S(1)} %fusion), channel_id=1, source_target_pairs={{0,18},{1,19},{2,20},{3,21},{4,22},{5,23},{6,24},{7,25},{8,26},{9,... | collective-permute-start | bytes 49160
  482.0 15.6 %collective-permute-start.24 = (f32[32,128]{1,0:T(8,128)S(1)}, f32[32,128]{1,0:T(8,128)S(1)}, u32[]{:S(2)}, u32[]{:S(2)}) collective-permute-start(f32[32,128]{1,0:T(8,128)S(1)} %fusion), channel_id=1, source_target_pairs={{0,19},{1,20},{2,21},{3,22},{4,23},{5,24},{6,25},{7,26},{8,27},{9,... | collective-permute-start | bytes 49160
  483.7 13.8 %collective-permute-start.6 = (f32[32,128]{1,0:T(8,128)S(1)}, f32[32,128]{1,0:T(8,128)S(1)}, u32[]{:S(2)}, u32[]{:S(2)}) collective-permute-start(f32[32,128]{1,0:T(8,128)S(1)} %fusion), channel_id=1, source_target_pairs={{0,1},{1,2},{2,3},{3,4},{4,5},{5,6},{6,7},{7,8},{8,9},{9,10},{10,1... | collective-permute-start | bytes 49160
  486.9 10.7 %collective-permute-start.7 = (f32[32,128]{1,0:T(8,128)S(1)}, f32[32,128]{1,0:T(8,128)S(1)}, u32[]{:S(2)}, u32[]{:S(2)}) collective-permute-start(f32[32,128]{1,0:T(8,128)S(1)} %fusion), channel_id=1, source_target_pairs={{0,2},{1,3},{2,4},{3,5},{4,6},{5,7},{6,8},{7,9},{8,10},{9,11},{10,... | collective-permute-start | bytes 49160
  490.0 7.6 %collective-permute-start.8 = (f32[32,128]{1,0:T(8,128)S(1)}, f32[32,128]{1,0:T(8,128)S(1)}, u32[]{:S(2)}, u32[]{:S(2)}) collective-permute-start(f32[32,128]{1,0:T(8,128)S(1)} %fusion), channel_id=1, source_target_pairs={{0,3},{1,4},{2,5},{3,6},{4,7},{5,8},{6,9},{7,10},{8,11},{9,12},{10... | collective-permute-start | bytes 49160
  492.4 5.5 %collective-permute-start.9 = (f32[32,128]{1,0:T(8,128)S(1)}, f32[32,128]{1,0:T(8,128)S(1)}, u32[]{:S(2)}, u32[]{:S(2)}) collective-permute-start(f32[32,128]{1,0:T(8,128)S(1)} %fusion), channel_id=1, source_target_pairs={{0,4},{1,5},{2,6},{3,7},{4,8},{5,9},{6,10},{7,11},{8,12},{9,13},{1... | collective-permute-start | bytes 49160
where the time goes:
time: 503 us; the launch traced here: 501 us
  blocking collectives  330 us (66%)
  starting transfers between devices  79.6 us (16%)
  waiting for transfers between devices  37.2 us (7%)
  local copies, waits for them, and re-layouts  31.9 us (6%)
  matrix products  12.4 us (2%)
  other arithmetic  8.87 us (2%)
    unnamed x1, blocking collectives  330 us
    unnamed x20, starting transfers between devices  67.3 us
    ppermute x2, waiting for transfers between devices, with_halo(): before = lax.ppermute(last, axis, up)  24.8 us
    unnamed x30, local copies, waits for them, and re-layouts  20 us
  transfers between devices with their start and end apart: 26, of which 8 were waited for; matrix products, arithmetic and copies ran while one was open for 3% of the time, Pallas kernels for 0%

commit v1 on v0

--- a/solution.py
+++ b/solution.py
@@ -68,7 +68,13 @@
     total_cells = frames * height * breadth * lax.axis_size("ha") * lax.axis_size("ta")
     factor = float(total_cells) ** (-0.5)
     term = jnp.concatenate(blocks, axis=0) * factor
-    grad_kernel = lax.psum_scatter(term, ("ha", "ta"), scatter_dimension=0, tiled=True)
+    owners = lax.axis_size("ha") * lax.axis_size("ta")
+    rows = term.shape[0] // owners
+    padded = -(-rows // 8) * 8
+    term = jnp.pad(term.reshape(owners, rows, channels), ((0, 0), (0, padded - rows), (0, 0)))
+    grad_kernel = lax.psum_scatter(
+        term.reshape(owners * padded, channels), ("ha", "ta"), scatter_dimension=0, tiled=True
+    )[:rows]
     sigmoid_part = jax.nn.sigmoid(values)
     derivative = sigmoid_part * (1.0 + values * (1.0 - sigmoid_part))
     grad_features = (

time: 503 us -> 772 us (1.53)
  waiting for transfers between devices: 37.2 us -> 690 us
  blocking collectives: 330 us -> 0 us
  starting transfers between devices: 79.6 us -> 12.4 us
  between operations: 1.33 us -> 14.4 us
    reduce_scatter x0 -> x1, waiting for transfers between devices: none -> 654 us  [body(): lax.psum_scatter(term.reshape(owners * padded, channels), ('ha', 'ta'), s...]
    unnamed x1 -> x0, blocking collectives: 330 us -> none
    unnamed x20 -> x0, starting transfers between devices: 67.3 us -> none
    unnamed x30 -> x27, local copies, waits for them, and re-layouts: 20 us -> 16.9 us
  transfers between devices with their start and end apart: 26 -> 7, of which waited for: 8 -> 7; matrix products, arithmetic and copies ran while one was open for 3% -> 2% of each run, Pallas kernels for 0% -> 0%
where the time goes in v1:
time: 772 us; the launch traced here: 771 us
  waiting for transfers between devices  690 us (89%)
  local copies, waits for them, and re-layouts  31.8 us (4%)
  between operations  14.4 us (2%)
  starting transfers between devices  12.4 us (2%)
  matrix products  12.3 us (2%)
  other arithmetic  10.1 us (1%)
    reduce_scatter x1, waiting for transfers between devices, body(): lax.psum_scatter(term.reshape(owners * padded, channels), ('ha', 'ta'), s...  654 us
    ppermute x2, waiting for transfers between devices, with_halo(): before = lax.ppermute(last, axis, up)  24.8 us
    unnamed x27, local copies, waits for them, and re-layouts  16.9 us
  transfers between devices with their start and end apart: 7, of which 7 were waited for; matrix products, arithmetic and copies ran while one was open for 2% of the time, Pallas kernels for 0%

profile of v1, /device:TPU:0, one launch (start us, length us, event | category | flops | bytes accessed | tf_op | source)
XLA Modules:
  0.0 770.8 jit_solution(12778964203199178777)
XLA Ops:
  7.2 1.0 slice.230
  8.2 1.3 collective-permute-start
  9.5 1.1 constant_dynamic-update-slice_fusion.1
  10.6 1.1 collective-permute-done
  11.8 3.6 collective-permute-start.1
  15.4 1.3 collective-permute-start.2
  16.7 2.2 copy.9
  18.8 2.0 fusion.109
  20.8 1.0 copy.22
  21.9 1.6 copy.23
  23.5 1.6 copy.24
  25.1 1.6 copy.25
  26.7 0.7 copy.26
  27.5 0.7 copy.27
  28.2 0.7 copy.28
  29.2 2.2 copy.10
  31.6 5.0 collective-permute-done.1
  36.6 4.2 collective-permute-done.2
  40.8 1.1 fusion.9
  41.8 3.3 fusion.103
  46.9 0.7 convolution_add_fusion.7
  48.9 0.7 convolution_add_fusion.6
  49.8 0.7 convolution_add_fusion.5
  51.4 0.7 convolution_add_fusion.4
  52.3 0.7 convolution_add_fusion.3
  54.2 0.7 convolution_add_fusion.2
  54.9 0.7 convolution_add_fusion.1
  55.9 0.7 convolution_add_fusion
  57.0 1.9 fusion.63
  59.0 1.3 collective-permute-start.3
  60.3 1.2 collective-permute-done.3
  61.6 3.4 collective-permute-start.4
  65.0 1.5 collective-permute-start.5
  66.7 19.8 %collective-permute-done.4 = bf16[6,1,640,128]{2,3,0,1:T(8,128)(2,1)S(1)} collective-permute-done((bf16[6,1,640,128]{2,3,0,1:T(8,128)(2,1)S(1)}, bf16[6,1,640,128]{2,3,0,1:T(8,128)(2,1)S(1)}, u32[]{:S(2)}, u32[]{:S(2)}) %collective-permute-start.4) | collective-permute-done | bytes 983072 | tf_op jit(solution)/shard_map/ppermute | solution.py:20
  86.5 4.2 collective-permute-done.5
  90.7 3.0 select_maximum_fusion
  93.7 3.9 fusion.102
  97.8 0.7 fusion.81
  98.5 0.7 fusion.79
  99.4 0.7 fusion.77
  100.0 0.7 fusion.75
  101.4 0.7 fusion.71
  102.1 0.7 fusion.69
  104.1 1.4 broadcast_multiply_fusion
  105.5 1.5 mul.29
  107.1 1.5 pad.13
  108.6 1.1 copy.21
  109.7 654.2 %reduce-scatter.2.cloned.1.call-done = f32[32,128]{1,0:T(8,128)} async-done(((f32[4096,128]{1,0:T(8,128)}), f32[32,128]{1,0:T(8,128)}) %reduce-scatter.2.cloned.1.call-update) | async-done | bytes 16400 | tf_op jit(solution)/shard_map/reduce_scatter | solution.py:75
  (37 shorter events, 9.4 us)
Async XLA Ops:
  7.2 756.8 %reduce-scatter.2.cloned.1.call-start = ((), (), s32[]{:S(2)}) async-start(), calls=%async_computation.1 | async-start | bytes 2113536 | tf_op jit(solution)/shard_map/reduce_scatter | solution.py:75
  8.2 3.5 collective-permute-start
  11.8 24.8 %collective-permute-start.1 = (bf16[6,1,640,128]{3,2,1,0:T(8,128)(2,1)S(1)}, bf16[6,1,640,128]{3,2,1,0:T(8,128)(2,1)S(1)}, u32[]{:S(2)}, u32[]{:S(2)}) collective-permute-start(bf16[6,1,640,128]{3,2,1,0:T(8,128)(2,1)S(1)} %constant_dynamic-update-slice_fusion), channel_id=1, source_target_pairs={{0,2},{2,4},{4,6},{6,8},{8,10},{10,12},{12,14},{14,16},{16,18},{18... | collective-permute-start | bytes 2949128 | tf_op jit(solution)/shard_map/ppermute | solution.py:20
  15.4 25.4 %collective-permute-start.2 = (bf16[6,1,640,128]{3,2,1,0:T(8,128)(2,1)S(1)}, bf16[6,1,640,128]{3,2,1,0:T(8,128)(2,1)S(1)}, u32[]{:S(2)}, u32[]{:S(2)}) collective-permute-start(bf16[6,1,640,128]{3,2,1,0:T(8,128)(2,1)S(1)} %constant_dynamic-update-slice_fusion), channel_id=1, source_target_pairs={{2,0},{4,2},{6,4},{8,6},{10,8},{12,10},{14,12},{16,14},{18,16},{20... | collective-permute-start | bytes 2949128 | tf_op jit(solution)/shard_map/ppermute | solution.py:21
  46.0 0.9 copy-start.6
  48.0 0.9 copy-start.5
  48.9 0.9 copy-start.4
  50.5 0.9 copy-start.3
  51.4 0.9 copy-start.2
  52.3 1.1 copy-start
  53.3 0.9 copy-start.1
  59.0 2.5 collective-permute-start.3
  61.6 24.9 %collective-permute-start.4 = (bf16[6,1,640,128]{2,3,0,1:T(8,128)(2,1)S(1)}, bf16[6,1,640,128]{2,3,0,1:T(8,128)(2,1)S(1)}, u32[]{:S(2)}, u32[]{:S(2)}) collective-permute-start(bf16[6,1,640,128]{2,3,0,1:T(8,128)(2,1)S(1)} %pad_maximum_fusion.9), channel_id=1, source_target_pairs={{0,2},{2,4},{4,6},{6,8},{8,10},{10,12},{12,14},{14,16},{16,18},{18... | collective-permute-start | bytes 2949128 | tf_op jit(solution)/shard_map/ppermute | solution.py:20
  65.0 25.6 %collective-permute-start.5 = (bf16[6,1,640,128]{2,3,0,1:T(8,128)(2,1)S(1)}, bf16[6,1,640,128]{2,3,0,1:T(8,128)(2,1)S(1)}, u32[]{:S(2)}, u32[]{:S(2)}) collective-permute-start(bf16[6,1,640,128]{2,3,0,1:T(8,128)(2,1)S(1)} %pad_maximum_fusion.9), channel_id=1, source_target_pairs={{2,0},{4,2},{6,4},{8,6},{10,8},{12,10},{14,12},{16,14},{18,16},{20... | collective-permute-start | bytes 2949128 | tf_op jit(solution)/shard_map/ppermute | solution.py:21
Sparse Core Ops, SparseCore 0:
  108.7 655.1 reduce-scatter.1

commit v2 on v1

--- a/solution.py
+++ b/solution.py
@@ -1,7 +1,11 @@
 import jax
 import jax.numpy as jnp
+import numpy as np
 from jax import lax
+from jax.sharding import Mesh, NamedSharding
 from jax.sharding import PartitionSpec as P
+
+PHYSICAL = ("y", "z", "x")
 
 
 def passed_along(block, axis, distance):
@@ -72,23 +76,77 @@
     rows = term.shape[0] // owners
     padded = -(-rows // 8) * 8
     term = jnp.pad(term.reshape(owners, rows, channels), ((0, 0), (0, padded - rows), (0, 0)))
-    grad_kernel = lax.psum_scatter(
-        term.reshape(owners * padded, channels), ("ha", "ta"), scatter_dimension=0, tiled=True
-    )[:rows]
     sigmoid_part = jax.nn.sigmoid(values)
     derivative = sigmoid_part * (1.0 + values * (1.0 - sigmoid_part))
     grad_features = (
         cotangent.astype(jnp.float32) + derivative * grad_input.reshape(features.shape)
     ).astype(jnp.bfloat16)
-    return (grad_features, grad_kernel)
+    return (grad_features, term[None])
+
+
+def physical_mesh(mesh):
+    devices = mesh.devices
+    coords = np.array([d.coords for d in devices.reshape(-1)])
+    sizes = {"x": len(set(coords[:, 0])), "y": len(set(coords[:, 1])), "z": len(set(coords[:, 2]))}
+    shape = tuple(sizes[a] for a in PHYSICAL) + (devices.shape[1],)
+    grid = devices.reshape(shape)
+    flat = np.array([d.coords for d in grid.reshape(-1)]).reshape(shape + (3,))
+    want = np.stack(np.meshgrid(*[np.arange(n) for n in shape[:3]], indexing="ij"), -1)
+    got = flat[..., 0, :][..., [1, 2, 0]]
+    assert (got == want).all()
+    return Mesh(grid, PHYSICAL + ("core",))
+
+
+def reduce_blocks(term, order):
+    rows = term.shape[2]
+    part = term[0]
+    for axis in order:
+        part = lax.psum_scatter(part, axis, scatter_dimension=0, tiled=True)
+    return part[0]
 
 
 def solution(mesh):
     placed = (P("ta", "ha", None, None), P("ta", "ha", None, None), P())
-    return jax.shard_map(
+    local = jax.shard_map(
         body,
         mesh=mesh,
         in_specs=placed,
-        out_specs=(P("ta", "ha", None, None), P(("ha", "ta"), None)),
+        out_specs=(P("ta", "ha", None, None), P(("ha", "ta"))),
         check_vma=False,
     )
+    grid = physical_mesh(mesh)
+    order = ("core", "x", "z", "y")
+    names = PHYSICAL + ("core",)
+    sizes = [grid.shape[a] for a in names]
+
+    def reorder(term):
+        n, owners, padded, channels = term.shape
+        t = term.reshape((n,) + tuple(sizes) + (padded, channels))
+        perm = [0] + [1 + names.index(a) for a in order] + [5, 6]
+        return t.transpose(perm).reshape(n, owners, padded, channels)
+
+    def reduce_fn(term):
+        rows = 27
+        return reduce_blocks(term, order)
+
+    rows_per = None
+
+    def run(features, cotangent, kernel):
+        grad_features, term = local(features, cotangent, kernel)
+        channels = kernel.shape[-1]
+        owners = term.shape[1]
+        taps_rows = kernel.shape[0] * kernel.shape[1] * kernel.shape[2] * kernel.shape[3]
+        rows = taps_rows // owners
+        term = reorder(term)
+        spec = P(names)
+        part = jax.shard_map(
+            lambda t: reduce_blocks(t, order)[:rows],
+            mesh=grid,
+            in_specs=spec,
+            out_specs=P(names),
+            check_vma=False,
+        )(term)
+        part = lax.with_sharding_constraint(part, NamedSharding(mesh, P(("ha", "ta"), None)))
+        return grad_features, part
+
+    return run

time: 772 us -> 212 us (0.27)
  waiting for transfers between devices: 690 us -> 128 us
    reduce_scatter x1 -> x4, waiting for transfers between devices: 654 us -> 92.7 us  [reduce_blocks(): part = lax.psum_scatter(part, axis, scatter_dimension=0, tiled=True)]
  transfers between devices with their start and end apart: 7 -> 10, of which waited for: 7 -> 10; matrix products, arithmetic and copies ran while one was open for 2% -> 8% of each run, Pallas kernels for 0% -> 0%
where the time goes in v2:
time: 212 us; the launch traced here: 211 us
  waiting for transfers between devices  128 us (60%)
  local copies, waits for them, and re-layouts  33.3 us (16%)
  between operations  14.2 us (7%)
  starting transfers between devices  12.5 us (6%)
  matrix products  12.3 us (6%)
  other arithmetic  10.1 us (5%)
    reduce_scatter x4, waiting for transfers between devices, reduce_blocks(): part = lax.psum_scatter(part, axis, scatter_dimension=0, tiled=True)  92.7 us
    ppermute x2, waiting for transfers between devices, with_halo(): before = lax.ppermute(last, axis, up)  24.8 us
    unnamed x27, local copies, waits for them, and re-layouts  16.9 us
    ppermute x2, waiting for transfers between devices, with_halo(): after = lax.ppermute(leading, axis, down)  8.35 us
    ppermute x2, starting transfers between devices, with_halo(): before = lax.ppermute(last, axis, up)  6.97 us
    dot_general x9, matrix products, body(): jnp.dot(cot_slab, stacked, preferred_element_type=jnp.float32)  6.25 us
    dot_general x9, matrix products, body(): lax.dot_general(act_slab, cot_flat, (((0,), (0,)), ((), ())), preferred_e...  6.08 us
    slice x3, local copies, waits for them, and re-layouts, body(): act_pad[t_tap:t_tap + frames, h_tap:h_tap + height, w_tap:w_tap + breadth]  4.31 us
  transfers between devices with their start and end apart: 10, of which 10 were waited for; matrix products, arithmetic and copies ran while one was open for 8% of the time, Pallas kernels for 0%

profile of v2, /device:TPU:0, one launch (start us, length us, event | category | flops | bytes accessed | tf_op | source)
XLA Modules:
  0.0 210.7 jit_solution(7997188344664616470)
XLA Ops:
  7.2 1.0 slice.233
  8.2 1.3 collective-permute-start
  9.5 1.1 constant_dynamic-update-slice_fusion.1
  10.7 1.1 collective-permute-done
  11.8 3.6 %collective-permute-start.1 = (bf16[6,1,640,128]{3,2,1,0:T(8,128)(2,1)S(1)}, bf16[6,1,640,128]{3,2,1,0:T(8,128)(2,1)S(1)}, u32[]{:S(2)}, u32[]{:S(2)}) collective-permute-start(bf16[6,1,640,128]{3,2,1,0:T(8,128)(2,1)S(1)} %constant_dynamic-update-slice_fusion), channel_id=1, source_target_pairs={{0,2},{2,4},{4,6},{6,8},{8,10},{10,12},{12,14},{14,16},{16,18},{18... | collective-permute-start | bytes 2949128 | tf_op jit(solution)/shard_map/ppermute | solution.py:24
  15.4 1.3 collective-permute-start.2
  16.7 2.2 %copy.12 = bf16[4,1,640,128]{2,3,0,1:T(8,128)(2,1)} copy(bf16[4,1,640,128]{3,2,1,0:T(8,128)(2,1)} %param.5) | data formatting | bytes 1310720 | tf_op args[1]
  18.8 2.0 fusion.109
  20.8 1.0 copy.26
  21.9 1.6 copy.27
  23.5 1.6 copy.28
  25.1 1.6 copy.29
  26.7 0.7 copy.30
  27.5 0.7 copy.31
  28.2 0.7 copy.32
  29.2 2.2 %copy.13 = bf16[4,1,640,128]{2,3,0,1:T(8,128)(2,1)} copy(bf16[4,1,640,128]{3,2,1,0:T(8,128)(2,1)} %param.4) | data formatting | bytes 1310720 | tf_op args[0]
  31.6 5.0 %collective-permute-done.1 = bf16[6,1,640,128]{3,2,1,0:T(8,128)(2,1)S(1)} collective-permute-done((bf16[6,1,640,128]{3,2,1,0:T(8,128)(2,1)S(1)}, bf16[6,1,640,128]{3,2,1,0:T(8,128)(2,1)S(1)}, u32[]{:S(2)}, u32[]{:S(2)}) %collective-permute-start.1) | collective-permute-done | bytes 983072 | tf_op jit(solution)/shard_map/ppermute | solution.py:24
  36.6 4.2 %collective-permute-done.2 = bf16[6,1,640,128]{3,2,1,0:T(8,128)(2,1)S(1)} collective-permute-done((bf16[6,1,640,128]{3,2,1,0:T(8,128)(2,1)S(1)}, bf16[6,1,640,128]{3,2,1,0:T(8,128)(2,1)S(1)}, u32[]{:S(2)}, u32[]{:S(2)}) %collective-permute-start.2) | collective-permute-done | bytes 983072 | tf_op jit(solution)/shard_map/ppermute | solution.py:25
  40.8 1.1 fusion.9
  41.8 3.3 %fusion.103 = (bf16[4,1,640,128]{3,2,1,0:T(8,128)(2,1)S(1)}, bf16[4,1,640,128]{3,2,1,0:T(8,128)(2,1)S(1)}, bf16[4,1,640,128]{3,2,1,0:T(8,128)(2,1)S(1)}, bf16[4,...) fusion(bf16[6,3,642,128]{3,2,1,0:T(8,128)(2,1)S(1)} %fusion.9), kind=kLoop, calls=%fused_computation.147 | loop fusion | bytes 23592960 | tf_op jit(solution)/shard_map/slice | solution.py:49
  46.9 0.7 convolution_add_fusion.7
  48.9 0.7 convolution_add_fusion.6
  49.8 0.7 convolution_add_fusion.5
  51.4 0.7 convolution_add_fusion.4
  52.3 0.7 convolution_add_fusion.3
  54.2 0.7 convolution_add_fusion.2
  54.9 0.7 convolution_add_fusion.1
  55.9 0.7 convolution_add_fusion
  57.0 1.9 fusion.63
  59.0 1.3 collective-permute-start.3
  60.3 1.2 collective-permute-done.3
  61.6 3.4 %collective-permute-start.4 = (bf16[6,1,640,128]{2,3,0,1:T(8,128)(2,1)S(1)}, bf16[6,1,640,128]{2,3,0,1:T(8,128)(2,1)S(1)}, u32[]{:S(2)}, u32[]{:S(2)}) collective-permute-start(bf16[6,1,640,128]{2,3,0,1:T(8,128)(2,1)S(1)} %pad_maximum_fusion.9), channel_id=1, source_target_pairs={{0,2},{2,4},{4,6},{6,8},{8,10},{10,12},{12,14},{14,16},{16,18},{18... | collective-permute-start | bytes 2949128 | tf_op jit(solution)/shard_map/ppermute | solution.py:24
  65.0 1.5 collective-permute-start.5
  66.7 19.8 %collective-permute-done.4 = bf16[6,1,640,128]{2,3,0,1:T(8,128)(2,1)S(1)} collective-permute-done((bf16[6,1,640,128]{2,3,0,1:T(8,128)(2,1)S(1)}, bf16[6,1,640,128]{2,3,0,1:T(8,128)(2,1)S(1)}, u32[]{:S(2)}, u32[]{:S(2)}) %collective-permute-start.4) | collective-permute-done | bytes 983072 | tf_op jit(solution)/shard_map/ppermute | solution.py:24
  86.5 4.2 %collective-permute-done.5 = bf16[6,1,640,128]{2,3,0,1:T(8,128)(2,1)S(1)} collective-permute-done((bf16[6,1,640,128]{2,3,0,1:T(8,128)(2,1)S(1)}, bf16[6,1,640,128]{2,3,0,1:T(8,128)(2,1)S(1)}, u32[]{:S(2)}, u32[]{:S(2)}) %collective-permute-start.5) | collective-permute-done | bytes 983072 | tf_op jit(solution)/shard_map/ppermute | solution.py:25
  90.7 3.0 %select_maximum_fusion = bf16[6,3,642,128]{2,3,0,1:T(8,128)(2,1)S(1)} fusion(bf16[6,1,640,128]{2,3,0,1:T(8,128)(2,1)S(1)} %collective-permute-done.5, bf16[6,1,640,128]{2,3,0,1:T(8,128)(2,1)S(1)} %collective-permute-done.4, bf16[4,1,640,128]{2,3,0,1:T(8,128)(2,1)S(1)} %get-tuple-element.68, bf16[2,1,640,128]{2,3,0,1:T(8,128)(2,1)S(1)} %collective-permute-done.3), kind=kLoop, calls=%fused_computation.14 | loop fusion | flops 22187520 | bytes 5907456 | tf_op jit(solution)/shard_map/concatenate | solution.py:26
  93.7 3.9 %fusion.102 = (bf16[4,1,640,128]{2,3,0,1:T(8,128)(2,1)S(1)}, bf16[4,1,640,128]{2,3,0,1:T(8,128)(2,1)S(1)}, bf16[4,1,640,128]{2,3,0,1:T(8,128)(2,1)S(1)}, bf16[4,...) fusion(bf16[6,3,642,128]{2,3,0,1:T(8,128)(2,1)S(1)} %select_max, ...), kind=kLoop, calls=%fused_computation.146 | loop fusion | bytes 23592960 | tf_op jit(solution)/shard_map/slice | solution.py:62
  99.4 0.7 fusion.77
  101.4 0.7 fusion.71
  104.1 1.4 broadcast_multiply_fusion
  105.5 1.5 mul.29
  107.2 1.5 copy.24
  108.9 20.8 %reduce-scatter.5.cloned.1.call-done = f32[64,32,128]{2,1,0:T(8,128)} async-done(((f32[128,32,128]{2,1,0:T(8,128)}), f32[64,32,128]{2,1,0:T(8,128)}) %reduce-scatter.5.cloned.1.call-update) | async-done | bytes 1048592 | tf_op jit(solution)/shard_map/reduce_scatter | solution.py:104
  129.7 27.5 %reduce-scatter.7.cloned.1.call-done = f32[16,32,128]{2,1,0:T(8,128)} async-done(((f32[64,32,128]{2,1,0:T(8,128)}), f32[16,32,128]{2,1,0:T(8,128)}) %reduce-scatter.7.cloned.1.call-update) | async-done | bytes 262160 | tf_op jit(solution)/shard_map/reduce_scatter | solution.py:104
  157.2 23.2 %reduce-scatter.9.cloned.1.call-done = f32[4,32,128]{2,1,0:T(8,128)} async-done(((f32[16,32,128]{2,1,0:T(8,128)}), f32[4,32,128]{2,1,0:T(8,128)}) %reduce-scatter.9.cloned.1.call-update) | async-done | bytes 65552 | tf_op jit(solution)/shard_map/reduce_scatter | solution.py:104
  180.5 1.1 copy.25
  181.6 21.3 %reduce-scatter.11.cloned.1.call-done = f32[1,32,128]{2,1,0:T(8,128)} async-done(((f32[4,32,128]{2,1,0:T(8,128)}), f32[1,32,128]{2,1,0:T(8,128)}) %reduce-scatter.11.cloned.1.call-update) | async-done | bytes 16400 | tf_op jit(solution)/shard_map/reduce_scatter | solution.py:104
  202.8 1.3 slice_bitcast_fusion
  (48 shorter events, 12.5 us)
Async XLA Ops:
  7.2 122.5 %reduce-scatter.5.cloned.1.call-start = ((), (), s32[]{:S(2)}) async-start(), calls=%async_computation.4 | async-start | bytes 3145728 | tf_op jit(solution)/shard_map/reduce_scatter | solution.py:104
  8.2 3.5 %collective-permute-start = (bf16[2,1,640,128]{3,2,1,0:T(8,128)(2,1)S(1)}, bf16[2,1,640,128]{3,2,1,0:T(8,128)(2,1)S(1)}, u32[]{:S(2)}, u32[]{:S(2)}) collective-permute-start(bf16[2,1,640,128]{3,2,1,0:T(8,128)(2,1)S(1)} %slice.233), channel_id=1, source_target_pairs={{1,0},{3,2},{5,4},{7,6},{9,8},{11,10},{13,12},{15,14},{17,16},{19,... | collective-permute-start | bytes 983048 | tf_op jit(solution)/shard_map/ppermute | solution.py:14
  11.8 24.8 %collective-permute-start.1 = (bf16[6,1,640,128]{3,2,1,0:T(8,128)(2,1)S(1)}, bf16[6,1,640,128]{3,2,1,0:T(8,128)(2,1)S(1)}, u32[]{:S(2)}, u32[]{:S(2)}) collective-permute-start(bf16[6,1,640,128]{3,2,1,0:T(8,128)(2,1)S(1)} %constant_dynamic-update-slice_fusion), channel_id=1, source_target_pairs={{0,2},{2,4},{4,6},{6,8},{8,10},{10,12},{12,14},{14,16},{16,18},{18... | collective-permute-start | bytes 2949128 | tf_op jit(solution)/shard_map/ppermute | solution.py:24
  15.4 25.4 %collective-permute-start.2 = (bf16[6,1,640,128]{3,2,1,0:T(8,128)(2,1)S(1)}, bf16[6,1,640,128]{3,2,1,0:T(8,128)(2,1)S(1)}, u32[]{:S(2)}, u32[]{:S(2)}) collective-permute-start(bf16[6,1,640,128]{3,2,1,0:T(8,128)(2,1)S(1)} %constant_dynamic-update-slice_fusion), channel_id=1, source_target_pairs={{2,0},{4,2},{6,4},{8,6},{10,8},{12,10},{14,12},{16,14},{18,16},{20... | collective-permute-start | bytes 2949128 | tf_op jit(solution)/shard_map/ppermute | solution.py:25
  46.0 0.9 copy-start.6
  48.0 0.9 copy-start.5
  48.9 0.9 copy-start.4
  50.5 0.9 copy-start.3
  51.4 0.9 copy-start.2
  52.3 1.1 copy-start
  53.3 0.9 copy-start.1
  59.0 2.5 %collective-permute-start.3 = (bf16[2,1,640,128]{2,3,0,1:T(8,128)(2,1)S(1)}, bf16[2,1,640,128]{2,3,0,1:T(8,128)(2,1)S(1)}, u32[]{:S(2)}, u32[]{:S(2)}) collective-permute-start(bf16[2,1,640,128]{2,3,0,1:T(8,128)(2,1)S(1)} %slice.324), channel_id=1, source_target_pairs={{0,1},{2,3},{4,5},{6,7},{8,9},{10,11},{12,13},{14,15},{16,17},{18,... | collective-permute-start | bytes 983048 | tf_op jit(solution)/shard_map/ppermute | solution.py:14
  61.6 24.9 %collective-permute-start.4 = (bf16[6,1,640,128]{2,3,0,1:T(8,128)(2,1)S(1)}, bf16[6,1,640,128]{2,3,0,1:T(8,128)(2,1)S(1)}, u32[]{:S(2)}, u32[]{:S(2)}) collective-permute-start(bf16[6,1,640,128]{2,3,0,1:T(8,128)(2,1)S(1)} %pad_maximum_fusion.9), channel_id=1, source_target_pairs={{0,2},{2,4},{4,6},{6,8},{8,10},{10,12},{12,14},{14,16},{16,18},{18... | collective-permute-start | bytes 2949128 | tf_op jit(solution)/shard_map/ppermute | solution.py:24
  65.0 25.6 %collective-permute-start.5 = (bf16[6,1,640,128]{2,3,0,1:T(8,128)(2,1)S(1)}, bf16[6,1,640,128]{2,3,0,1:T(8,128)(2,1)S(1)}, u32[]{:S(2)}, u32[]{:S(2)}) collective-permute-start(bf16[6,1,640,128]{2,3,0,1:T(8,128)(2,1)S(1)} %pad_maximum_fusion.9), channel_id=1, source_target_pairs={{2,0},{4,2},{6,4},{8,6},{10,8},{12,10},{14,12},{16,14},{18,16},{20... | collective-permute-start | bytes 2949128 | tf_op jit(solution)/shard_map/ppermute | solution.py:25
  108.8 48.3 %reduce-scatter.7.cloned.1.call-start = ((), (), s32[]{:S(2)}) async-start(), calls=%async_computation.5 | async-start | bytes 1310720 | tf_op jit(solution)/shard_map/reduce_scatter | solution.py:104
  129.6 50.8 %reduce-scatter.9.cloned.1.call-start = ((), (), s32[]{:S(2)}) async-start(), calls=%async_computation.6 | async-start | bytes 327680 | tf_op jit(solution)/shard_map/reduce_scatter | solution.py:104
  157.2 45.6 %reduce-scatter.11.cloned.1.call-start = ((), (), s32[]{:S(2)}) async-start(), calls=%async_computation.7 | async-start | bytes 81920 | tf_op jit(solution)/shard_map/reduce_scatter | solution.py:104
Sparse Core Ops, SparseCore 0:
  108.9 20.6 reduce-scatter.4
  132.0 25.0 reduce-scatter.6
  159.5 20.8 reduce-scatter.8
  182.7 20.1 reduce-scatter.10

commit v3 on v0

--- a/solution.py
+++ b/solution.py
@@ -68,7 +68,10 @@
     total_cells = frames * height * breadth * lax.axis_size("ha") * lax.axis_size("ta")
     factor = float(total_cells) ** (-0.5)
     term = jnp.concatenate(blocks, axis=0) * factor
-    grad_kernel = lax.psum_scatter(term, ("ha", "ta"), scatter_dimension=0, tiled=True)
+    total = lax.psum(term, ("ha", "ta"))
+    rows = term.shape[0] // (lax.axis_size("ha") * lax.axis_size("ta"))
+    owner = lax.axis_index("ha") * lax.axis_size("ta") + lax.axis_index("ta")
+    grad_kernel = lax.dynamic_slice_in_dim(total, owner * rows, rows, axis=0)
     sigmoid_part = jax.nn.sigmoid(values)
     derivative = sigmoid_part * (1.0 + values * (1.0 - sigmoid_part))
     grad_features = (

time: 503 us -> 273 us (0.54)
  blocking collectives: 330 us -> 0 us
  waiting for transfers between devices: 37.2 us -> 195 us
  starting transfers between devices: 79.6 us -> 12.4 us
  between operations: 1.33 us -> 14.4 us
    unnamed x1 -> x0, blocking collectives: 330 us -> none
    psum x0 -> x1, waiting for transfers between devices: none -> 158 us  [body(): total = lax.psum(term, ('ha', 'ta'))]
    unnamed x20 -> x0, starting transfers between devices: 67.3 us -> none
    unnamed x30 -> x23, local copies, waits for them, and re-layouts: 20 us -> 15.1 us
  transfers between devices with their start and end apart: 26 -> 7, of which waited for: 8 -> 7; matrix products, arithmetic and copies ran while one was open for 3% -> 6% of each run, Pallas kernels for 0% -> 0%
where the time goes in v3:
time: 273 us; the launch traced here: 272 us
  waiting for transfers between devices  195 us (71%)
  local copies, waits for them, and re-layouts  28.4 us (10%)
  between operations  14.4 us (5%)
  starting transfers between devices  12.4 us (5%)
  matrix products  12.3 us (5%)
  other arithmetic  10.1 us (4%)
    psum x1, waiting for transfers between devices, body(): total = lax.psum(term, ('ha', 'ta'))  158 us
    ppermute x2, waiting for transfers between devices, with_halo(): before = lax.ppermute(last, axis, up)  26.1 us
    unnamed x23, local copies, waits for them, and re-layouts  15.1 us
    ppermute x2, waiting for transfers between devices, with_halo(): after = lax.ppermute(leading, axis, down)  8.35 us
    ppermute x2, starting transfers between devices, with_halo(): before = lax.ppermute(last, axis, up)  6.97 us
    dot_general x9, matrix products, body(): jnp.dot(cot_slab, stacked, preferred_element_type=jnp.float32)  6.25 us
    dot_general x9, matrix products, body(): lax.dot_general(act_slab, cot_flat, (((0,), (0,)), ((), ())), preferred_e...  6.09 us
  transfers between devices with their start and end apart: 7, of which 7 were waited for; matrix products, arithmetic and copies ran while one was open for 6% of the time, Pallas kernels for 0%

profile of v3, /device:TPU:0, one launch (start us, length us, event | category | flops | bytes accessed | tf_op | source)
XLA Modules:
  0.0 272.2 jit_solution(1772013093454288054)
XLA Ops:
  7.2 1.0 slice.227
  8.2 1.3 collective-permute-start
  9.5 1.1 constant_dynamic-update-slice_fusion.1
  10.7 1.1 collective-permute-done
  11.8 3.6 %collective-permute-start.1 = (bf16[6,1,640,128]{3,2,1,0:T(8,128)(2,1)S(1)}, bf16[6,1,640,128]{3,2,1,0:T(8,128)(2,1)S(1)}, u32[]{:S(2)}, u32[]{:S(2)}) collective-permute-start(bf16[6,1,640,128]{3,2,1,0:T(8,128)(2,1)S(1)} %constant_dynamic-update-slice_fusion), channel_id=1, source_target_pairs={{0,2},{2,4},{4,6},{6,8},{8,10},{10,12},{12,14},{14,16},{16,18},{18... | collective-permute-start | bytes 2949128 | tf_op jit(solution)/shard_map/ppermute | solution.py:20
  15.4 1.3 collective-permute-start.2
  16.7 2.2 copy.9
  18.8 2.0 fusion.109
  20.8 1.0 copy.22
  21.9 1.6 copy.23
  23.5 1.6 copy.24
  25.1 1.6 copy.25
  26.7 0.7 copy.26
  28.0 2.2 copy.10
  30.4 6.2 %collective-permute-done.1 = bf16[6,1,640,128]{3,2,1,0:T(8,128)(2,1)S(1)} collective-permute-done((bf16[6,1,640,128]{3,2,1,0:T(8,128)(2,1)S(1)}, bf16[6,1,640,128]{3,2,1,0:T(8,128)(2,1)S(1)}, u32[]{:S(2)}, u32[]{:S(2)}) %collective-permute-start.1) | collective-permute-done | bytes 983072 | tf_op jit(solution)/shard_map/ppermute | solution.py:20
  36.6 4.2 %collective-permute-done.2 = bf16[6,1,640,128]{3,2,1,0:T(8,128)(2,1)S(1)} collective-permute-done((bf16[6,1,640,128]{3,2,1,0:T(8,128)(2,1)S(1)}, bf16[6,1,640,128]{3,2,1,0:T(8,128)(2,1)S(1)}, u32[]{:S(2)}, u32[]{:S(2)}) %collective-permute-start.2) | collective-permute-done | bytes 983072 | tf_op jit(solution)/shard_map/ppermute | solution.py:21
  40.8 1.1 fusion.9
  41.8 3.2 %fusion.103 = (bf16[4,1,640,128]{3,2,1,0:T(8,128)(2,1)S(1)}, bf16[4,1,640,128]{3,2,1,0:T(8,128)(2,1)S(1)}, bf16[4,1,640,128]{3,2,1,0:T(8,128)(2,1)S(1)}, bf16[4,...) fusion(bf16[6,3,642,128]{3,2,1,0:T(8,128)(2,1)S(1)} %fusion.9), kind=kLoop, calls=%fused_computation.147 | loop fusion | bytes 23592960 | tf_op jit(solution)/shard_map/slice | solution.py:45
  46.0 0.7 fusion.110
  46.9 0.7 convolution_add_fusion.7
  48.9 0.7 convolution_add_fusion.6
  49.8 0.7 convolution_add_fusion.5
  51.4 0.7 convolution_add_fusion.4
  52.1 0.7 convolution_add_fusion.3
  53.7 0.7 convolution_add_fusion.2
  54.4 0.7 convolution_add_fusion.1
  55.4 0.7 convolution_add_fusion
  56.5 1.9 fusion.63
  58.4 1.3 collective-permute-start.3
  59.7 1.2 collective-permute-done.3
  61.1 3.4 %collective-permute-start.4 = (bf16[6,1,640,128]{2,3,0,1:T(8,128)(2,1)S(1)}, bf16[6,1,640,128]{2,3,0,1:T(8,128)(2,1)S(1)}, u32[]{:S(2)}, u32[]{:S(2)}) collective-permute-start(bf16[6,1,640,128]{2,3,0,1:T(8,128)(2,1)S(1)} %pad_maximum_fusion.9), channel_id=1, source_target_pairs={{0,2},{2,4},{4,6},{6,8},{8,10},{10,12},{12,14},{14,16},{16,18},{18... | collective-permute-start | bytes 2949128 | tf_op jit(solution)/shard_map/ppermute | solution.py:20
  64.5 1.5 collective-permute-start.5
  66.1 19.8 %collective-permute-done.4 = bf16[6,1,640,128]{2,3,0,1:T(8,128)(2,1)S(1)} collective-permute-done((bf16[6,1,640,128]{2,3,0,1:T(8,128)(2,1)S(1)}, bf16[6,1,640,128]{2,3,0,1:T(8,128)(2,1)S(1)}, u32[]{:S(2)}, u32[]{:S(2)}) %collective-permute-start.4) | collective-permute-done | bytes 983072 | tf_op jit(solution)/shard_map/ppermute | solution.py:20
  85.9 4.2 %collective-permute-done.5 = bf16[6,1,640,128]{2,3,0,1:T(8,128)(2,1)S(1)} collective-permute-done((bf16[6,1,640,128]{2,3,0,1:T(8,128)(2,1)S(1)}, bf16[6,1,640,128]{2,3,0,1:T(8,128)(2,1)S(1)}, u32[]{:S(2)}, u32[]{:S(2)}) %collective-permute-start.5) | collective-permute-done | bytes 983072 | tf_op jit(solution)/shard_map/ppermute | solution.py:21
  90.1 3.0 %select_maximum_fusion = bf16[6,3,642,128]{2,3,0,1:T(8,128)(2,1)S(1)} fusion(bf16[6,1,640,128]{2,3,0,1:T(8,128)(2,1)S(1)} %collective-permute-done.5, bf16[6,1,640,128]{2,3,0,1:T(8,128)(2,1)S(1)} %collective-permute-done.4, bf16[4,1,640,128]{2,3,0,1:T(8,128)(2,1)S(1)} %get-tuple-element.67, bf16[2,1,640,128]{2,3,0,1:T(8,128)(2,1)S(1)} %collective-permute-done.3), kind=kLoop, calls=%fused_computation.14 | loop fusion | flops 22187520 | bytes 5907456 | tf_op jit(solution)/shard_map/concatenate | solution.py:22
  93.1 4.0 %fusion.102 = (bf16[4,1,640,128]{2,3,0,1:T(8,128)(2,1)S(1)}, bf16[4,1,640,128]{2,3,0,1:T(8,128)(2,1)S(1)}, bf16[4,1,640,128]{2,3,0,1:T(8,128)(2,1)S(1)}, bf16[4,...) fusion(bf16[6,3,642,128]{2,3,0,1:T(8,128)(2,1)S(1)} %select_max, ...), kind=kLoop, calls=%fused_computation.146 | loop fusion | bytes 23592960 | tf_op jit(solution)/shard_map/slice | solution.py:58
  97.3 0.7 fusion.81
  98.0 0.7 fusion.79
  98.9 0.7 fusion.77
  99.5 0.7 fusion.75
  100.2 0.7 fusion.73
  100.9 0.7 fusion.71
  101.6 0.7 fusion.69
  103.0 0.7 fusion.65
  103.7 1.4 broadcast_multiply_fusion
  105.0 1.1 copy.21
  106.1 157.9 %all-reduce.4.cloned.1.call-done = f32[3456,128]{1,0:T(8,128)} async-done(((f32[3456,128]{1,0:T(8,128)}), f32[3456,128]{1,0:T(8,128)}) %all-reduce.4.cloned.1.call-update) | async-done | bytes 1769488 | tf_op jit(solution)/shard_map/psum | solution.py:71
  264.0 1.3 constant_dynamic-slice_fusion
  (32 shorter events, 7.1 us)
Async XLA Ops:
  7.2 256.9 %all-reduce.4.cloned.1.call-start = ((), (), s32[]{:S(2)}) async-start(), calls=%async_computation | async-start | bytes 3538944 | tf_op jit(solution)/shard_map/psum | solution.py:71
  8.2 3.5 %collective-permute-start = (bf16[2,1,640,128]{3,2,1,0:T(8,128)(2,1)S(1)}, bf16[2,1,640,128]{3,2,1,0:T(8,128)(2,1)S(1)}, u32[]{:S(2)}, u32[]{:S(2)}) collective-permute-start(bf16[2,1,640,128]{3,2,1,0:T(8,128)(2,1)S(1)} %slice.227), channel_id=1, source_target_pairs={{1,0},{3,2},{5,4},{7,6},{9,8},{11,10},{13,12},{15,14},{17,16},{19,... | collective-permute-start | bytes 983048 | tf_op jit(solution)/shard_map/ppermute | solution.py:10
  11.8 24.8 %collective-permute-start.1 = (bf16[6,1,640,128]{3,2,1,0:T(8,128)(2,1)S(1)}, bf16[6,1,640,128]{3,2,1,0:T(8,128)(2,1)S(1)}, u32[]{:S(2)}, u32[]{:S(2)}) collective-permute-start(bf16[6,1,640,128]{3,2,1,0:T(8,128)(2,1)S(1)} %constant_dynamic-update-slice_fusion), channel_id=1, source_target_pairs={{0,2},{2,4},{4,6},{6,8},{8,10},{10,12},{12,14},{14,16},{16,18},{18... | collective-permute-start | bytes 2949128 | tf_op jit(solution)/shard_map/ppermute | solution.py:20
  15.4 25.4 %collective-permute-start.2 = (bf16[6,1,640,128]{3,2,1,0:T(8,128)(2,1)S(1)}, bf16[6,1,640,128]{3,2,1,0:T(8,128)(2,1)S(1)}, u32[]{:S(2)}, u32[]{:S(2)}) collective-permute-start(bf16[6,1,640,128]{3,2,1,0:T(8,128)(2,1)S(1)} %constant_dynamic-update-slice_fusion), channel_id=1, source_target_pairs={{2,0},{4,2},{6,4},{8,6},{10,8},{12,10},{14,12},{16,14},{18,16},{20... | collective-permute-start | bytes 2949128 | tf_op jit(solution)/shard_map/ppermute | solution.py:21
  46.0 0.9 copy-start.4
  48.0 0.9 copy-start.3
  48.9 0.9 copy-start.2
  50.5 0.9 copy-start.1
  52.0 1.1 copy-start
  58.4 2.5 collective-permute-start.3
  61.1 24.9 %collective-permute-start.4 = (bf16[6,1,640,128]{2,3,0,1:T(8,128)(2,1)S(1)}, bf16[6,1,640,128]{2,3,0,1:T(8,128)(2,1)S(1)}, u32[]{:S(2)}, u32[]{:S(2)}) collective-permute-start(bf16[6,1,640,128]{2,3,0,1:T(8,128)(2,1)S(1)} %pad_maximum_fusion.9), channel_id=1, source_target_pairs={{0,2},{2,4},{4,6},{6,8},{8,10},{10,12},{12,14},{14,16},{16,18},{18... | collective-permute-start | bytes 2949128 | tf_op jit(solution)/shard_map/ppermute | solution.py:20
  64.5 25.6 %collective-permute-start.5 = (bf16[6,1,640,128]{2,3,0,1:T(8,128)(2,1)S(1)}, bf16[6,1,640,128]{2,3,0,1:T(8,128)(2,1)S(1)}, u32[]{:S(2)}, u32[]{:S(2)}) collective-permute-start(bf16[6,1,640,128]{2,3,0,1:T(8,128)(2,1)S(1)} %pad_maximum_fusion.9), channel_id=1, source_target_pairs={{2,0},{4,2},{6,4},{8,6},{10,8},{12,10},{14,12},{16,14},{18,16},{20... | collective-permute-start | bytes 2949128 | tf_op jit(solution)/shard_map/ppermute | solution.py:21
Sparse Core Ops, SparseCore 0:
  105.2 158.8 all-reduce.3

commit v4 on v2

--- a/solution.py
+++ b/solution.py
@@ -101,7 +101,9 @@
     rows = term.shape[2]
     part = term[0]
     for axis in order:
-        part = lax.psum_scatter(part, axis, scatter_dimension=0, tiled=True)
+        count = lax.axis_size(axis)
+        shaped = part.reshape((count, part.shape[0] // count) + part.shape[1:])
+        part = lax.all_to_all(shaped, axis, 0, 0, tiled=True).sum(0)
     return part[0]
 
 

time: 212 us -> 160 us (0.75)
  waiting for transfers between devices: 128 us -> 39.1 us
  blocking collectives: 0 us -> 42.5 us
  between operations: 14.2 us -> 1.06 us
  starting transfers between devices: 12.5 us -> 16.8 us
    reduce_scatter x4 -> x0, waiting for transfers between devices: 92.7 us -> none  [reduce_blocks(): part = lax.psum_scatter(part, axis, scatter_dimension=0, tiled=True)]
    all_to_all x0 -> x3, blocking collectives: none -> 42.5 us  [reduce_blocks(): part = lax.all_to_all(shaped, axis, 0, 0, tiled=True).sum(0)]
    all_to_all x0 -> x1, waiting for transfers between devices: none -> 4.54 us  [reduce_blocks(): part = lax.all_to_all(shaped, axis, 0, 0, tiled=True).sum(0)]
    all_to_all x0 -> x1, starting transfers between devices: none -> 4.47 us  [reduce_blocks(): part = lax.all_to_all(shaped, axis, 0, 0, tiled=True).sum(0)]
    unnamed x27 -> x31, local copies, waits for them, and re-layouts: 16.9 us -> 17.8 us
  transfers between devices with their start and end apart: 10 -> 7, of which waited for: 10 -> 7; matrix products, arithmetic and copies ran while one was open for 8% -> 11% of each run, Pallas kernels for 0% -> 0%
where the time goes in v4:
time: 160 us; the launch traced here: 158 us
  blocking collectives  42.5 us (27%)
  waiting for transfers between devices  39.1 us (24%)
  local copies, waits for them, and re-layouts  33.7 us (21%)
  starting transfers between devices  16.8 us (10%)
  matrix products  13.4 us (8%)
  other arithmetic  11.8 us (7%)
    all_to_all x3, blocking collectives, reduce_blocks(): part = lax.all_to_all(shaped, axis, 0, 0, tiled=True).sum(0)  42.5 us
    ppermute x2, waiting for transfers between devices, with_halo(): before = lax.ppermute(last, axis, up)  24 us
    unnamed x31, local copies, waits for them, and re-layouts  17.8 us
    ppermute x2, waiting for transfers between devices, with_halo(): after = lax.ppermute(leading, axis, down)  8.35 us
    dot_general x9, matrix products, body(): jnp.dot(cot_slab, stacked, preferred_element_type=jnp.float32)  7.34 us
    ppermute x2, starting transfers between devices, with_halo(): before = lax.ppermute(last, axis, up)  6.97 us
    dot_general x9, matrix products, body(): lax.dot_general(act_slab, cot_flat, (((0,), (0,)), ((), ())), preferred_e...  6.09 us
    all_to_all x1, waiting for transfers between devices, reduce_blocks(): part = lax.all_to_all(shaped, axis, 0, 0, tiled=True).sum(0)  4.54 us
  transfers between devices with their start and end apart: 7, of which 7 were waited for; matrix products, arithmetic and copies ran while one was open for 11% of the time, Pallas kernels for 0%

profile of v4, /device:TPU:0, one launch (start us, length us, event | category | flops | bytes accessed | tf_op | source)
XLA Modules:
  0.0 158.4 jit_solution(2643973364243168341)
XLA Ops:
  0.6 1.0 slice.233
  1.6 1.3 collective-permute-start
  2.9 1.1 constant_dynamic-update-slice_fusion.1
  4.1 1.1 collective-permute-done
  5.2 3.6 %collective-permute-start.1 = (bf16[6,1,640,128]{3,2,1,0:T(8,128)(2,1)S(1)}, bf16[6,1,640,128]{3,2,1,0:T(8,128)(2,1)S(1)}, u32[]{:S(2)}, u32[]{:S(2)}) collective-permute-start(bf16[6,1,640,128]{3,2,1,0:T(8,128)(2,1)S(1)} %constant_dynamic-update-slice_fusion), channel_id=1, source_target_pairs={{0,2},{2,4},{4,6},{6,8},{8,10},{10,12},{12,14},{14,16},{16,18},{18... | collective-permute-start | bytes 2949128 | tf_op jit(solution)/shard_map/ppermute | solution.py:24
  8.8 1.3 collective-permute-start.2
  10.1 2.2 %copy.39 = bf16[4,1,640,128]{2,3,0,1:T(8,128)(2,1)} copy(bf16[4,1,640,128]{3,2,1,0:T(8,128)(2,1)} %param.5) | data formatting | bytes 1310720 | tf_op args[1]
  12.2 2.0 %fusion.109 = (bf16[1,1,3,128,128]{4,3,2,1,0:T(8,128)(2,1)S(1)}, bf16[1,1,3,128,128]{4,3,2,1,0:T(8,128)(2,1)S(1)}, bf16[1,1,3,128,128]{4,3,2,1,0:T(8,128)(2,1)S(...) fusion(bf16[3,3,3,128,128]{4,3,2,1,0:T(8,128)(2,1)} %param.6), kind=kLoop, calls=%fused_computation.153 | loop fusion | bytes 1769472 | tf_op jit(solution)/shard_map/slice | solution.py:58
  14.3 1.0 copy.54
  15.3 1.6 %copy.55 = bf16[1,1,3,128,128]{3,4,2,1,0:T(8,128)(2,1)} copy(bf16[1,1,3,128,128]{4,3,2,1,0:T(8,128)(2,1)} %get-tuple-element.70) | data formatting | bytes 196608
  16.9 1.6 %copy.56 = bf16[1,1,3,128,128]{3,4,2,1,0:T(8,128)(2,1)} copy(bf16[1,1,3,128,128]{4,3,2,1,0:T(8,128)(2,1)} %get-tuple-element.69) | data formatting | bytes 196608
  18.5 1.6 %copy.57 = bf16[1,1,3,128,128]{3,4,2,1,0:T(8,128)(2,1)} copy(bf16[1,1,3,128,128]{4,3,2,1,0:T(8,128)(2,1)} %get-tuple-element.68) | data formatting | bytes 196608
  20.2 1.6 %copy.58 = bf16[1,1,3,128,128]{3,4,2,1,0:T(8,128)(2,1)} copy(bf16[1,1,3,128,128]{4,3,2,1,0:T(8,128)(2,1)} %get-tuple-element.67) | data formatting | bytes 196608
  21.8 0.7 copy.59
  22.5 0.7 copy.60
  23.6 2.2 %copy.40 = bf16[4,1,640,128]{2,3,0,1:T(8,128)(2,1)} copy(bf16[4,1,640,128]{3,2,1,0:T(8,128)(2,1)} %param.4) | data formatting | bytes 1310720 | tf_op args[0]
  25.9 4.1 %collective-permute-done.1 = bf16[6,1,640,128]{3,2,1,0:T(8,128)(2,1)S(1)} collective-permute-done((bf16[6,1,640,128]{3,2,1,0:T(8,128)(2,1)S(1)}, bf16[6,1,640,128]{3,2,1,0:T(8,128)(2,1)S(1)}, u32[]{:S(2)}, u32[]{:S(2)}) %collective-permute-start.1) | collective-permute-done | bytes 983072 | tf_op jit(solution)/shard_map/ppermute | solution.py:24
  30.0 4.2 %collective-permute-done.2 = bf16[6,1,640,128]{3,2,1,0:T(8,128)(2,1)S(1)} collective-permute-done((bf16[6,1,640,128]{3,2,1,0:T(8,128)(2,1)S(1)}, bf16[6,1,640,128]{3,2,1,0:T(8,128)(2,1)S(1)}, u32[]{:S(2)}, u32[]{:S(2)}) %collective-permute-start.2) | collective-permute-done | bytes 983072 | tf_op jit(solution)/shard_map/ppermute | solution.py:25
  34.2 1.1 fusion.9
  35.3 3.3 %fusion.103 = (bf16[4,1,640,128]{3,2,1,0:T(8,128)(2,1)S(1)}, bf16[4,1,640,128]{3,2,1,0:T(8,128)(2,1)S(1)}, bf16[4,1,640,128]{3,2,1,0:T(8,128)(2,1)S(1)}, bf16[4,...) fusion(bf16[6,3,642,128]{3,2,1,0:T(8,128)(2,1)S(1)} %fusion.9), kind=kLoop, calls=%fused_computation.147 | loop fusion | bytes 23592960 | tf_op jit(solution)/shard_map/slice | solution.py:49
  40.4 0.7 convolution_add_fusion.7
  42.3 0.7 convolution_add_fusion.6
  43.2 0.7 convolution_add_fusion.5
  44.8 0.7 convolution_add_fusion.4
  45.7 0.7 convolution_add_fusion.3
  47.7 0.7 convolution_add_fusion.2
  48.4 0.7 convolution_add_fusion.1
  49.4 1.8 %convolution_add_fusion = f32[2560,128]{1,0:T(8,128)} fusion(f32[2560,128]{1,0:T(8,128)S(1)} %convolution_add_fusion.1, bf16[2560,384]{1,0:T(8,128)(2,1)S(1)} %bitcast.205, bf16[384,128]{1,0:T(8,128)(2,1)S(1)} %bitcast.218), kind=kOutput, calls=%fused_computation.6 | convolution fusion | flops 251985920 | bytes 4685824 | tf_op jit(solution)/shard_map/dot_general | solution.py:59
  51.2 1.8 %copy.50 = f32[4,1,640,128]{2,3,0,1:T(8,128)S(1)} copy(f32[4,1,640,128]{3,2,0,1:T(8,128)} %bitcast.214) | data formatting | bytes 2621440 | tf_op jit(solution)/shard_map/reshape | solution.py:82
  53.0 2.5 %fusion.63 = (bf16[4,1,640,128]{2,3,0,1:T(8,128)(2,1)S(1)}, bf16[4,1,640,128]{2,3,0,1:T(8,128)(2,1)}) fusion(bf16[4,1,640,128]{2,3,0,1:T(8,128)(2,1)} %copy.40, f32[4,1,640,128]{2,3,0,1:T(8,128)S(1)} %copy.50, bf16[4,1,640,128]{2,3,0,1:T(8,128)(2,1)S(1)} %copy-done.1), kind=kLoop, calls=%fused_computation.101 | loop fusion | flops 4587520 | bytes 3932160 | tf_op jit(solution)/shard_map/convert_element_type | solution.py:33
  55.6 1.3 collective-permute-start.3
  56.9 1.2 collective-permute-done.3
  58.2 3.4 %collective-permute-start.4 = (bf16[6,1,640,128]{2,3,0,1:T(8,128)(2,1)S(1)}, bf16[6,1,640,128]{2,3,0,1:T(8,128)(2,1)S(1)}, u32[]{:S(2)}, u32[]{:S(2)}) collective-permute-start(bf16[6,1,640,128]{2,3,0,1:T(8,128)(2,1)S(1)} %pad_maximum_fusion.9), channel_id=1, source_target_pairs={{0,2},{2,4},{4,6},{6,8},{8,10},{10,12},{12,14},{14,16},{16,18},{18... | collective-permute-start | bytes 2949128 | tf_op jit(solution)/shard_map/ppermute | solution.py:24
  61.6 1.5 collective-permute-start.5
  63.2 19.8 %collective-permute-done.4 = bf16[6,1,640,128]{2,3,0,1:T(8,128)(2,1)S(1)} collective-permute-done((bf16[6,1,640,128]{2,3,0,1:T(8,128)(2,1)S(1)}, bf16[6,1,640,128]{2,3,0,1:T(8,128)(2,1)S(1)}, u32[]{:S(2)}, u32[]{:S(2)}) %collective-permute-start.4) | collective-permute-done | bytes 983072 | tf_op jit(solution)/shard_map/ppermute | solution.py:24
  83.1 4.2 %collective-permute-done.5 = bf16[6,1,640,128]{2,3,0,1:T(8,128)(2,1)S(1)} collective-permute-done((bf16[6,1,640,128]{2,3,0,1:T(8,128)(2,1)S(1)}, bf16[6,1,640,128]{2,3,0,1:T(8,128)(2,1)S(1)}, u32[]{:S(2)}, u32[]{:S(2)}) %collective-permute-start.5) | collective-permute-done | bytes 983072 | tf_op jit(solution)/shard_map/ppermute | solution.py:25
  87.3 3.0 %select_maximum_fusion = bf16[6,3,642,128]{2,3,0,1:T(8,128)(2,1)S(1)} fusion(bf16[6,1,640,128]{2,3,0,1:T(8,128)(2,1)S(1)} %collective-permute-done.5, bf16[6,1,640,128]{2,3,0,1:T(8,128)(2,1)S(1)} %collective-permute-done.4, bf16[4,1,640,128]{2,3,0,1:T(8,128)(2,1)S(1)} %get-tuple-element.72, bf16[2,1,640,128]{2,3,0,1:T(8,128)(2,1)S(1)} %collective-permute-done.3), kind=kLoop, calls=%fused_computation.14 | loop fusion | flops 22187520 | bytes 5907456 | tf_op jit(solution)/shard_map/concatenate | solution.py:26
  90.2 4.0 %fusion.102 = (bf16[4,1,640,128]{2,3,0,1:T(8,128)(2,1)S(1)}, bf16[4,1,640,128]{2,3,0,1:T(8,128)(2,1)S(1)}, bf16[4,1,640,128]{2,3,0,1:T(8,128)(2,1)S(1)}, bf16[4,...) fusion(bf16[6,3,642,128]{2,3,0,1:T(8,128)(2,1)S(1)} %select_max, ...), kind=kLoop, calls=%fused_computation.146 | loop fusion | bytes 23592960 | tf_op jit(solution)/shard_map/slice | solution.py:62
  98.0 0.7 fusion.71
  98.7 0.7 fusion.69
  100.8 1.4 broadcast_multiply_fusion
  102.2 1.5 mul.29
  104.1 5.4 %all_to_all.20 = f32[2,64,32,128]{3,2,1,0:T(8,128)S(1)} all-to-all(f32[2,64,32,128]{3,2,1,0:T(8,128)S(1)} %bitcast.204), channel_id=1, replica_groups=mesh['y'=4,'z'=4,'x'=4,'core'=2] {'core'}, dimensions={0} | all-to-all | bytes 4194304 | tf_op jit(solution)/shard_map/all_to_all | solution.py:106
  109.8 22.7 %all_to_all.21 = f32[4,16,32,128]{3,2,1,0:T(8,128)S(1)} all-to-all(f32[4,16,32,128]{3,2,1,0:T(8,128)S(1)} %bitcast.215), channel_id=1, replica_groups=mesh['y'=4,'z'=4,'x'=4,'core'=2] {'x'}, dimensions={0} | all-to-all | bytes 2097152 | tf_op jit(solution)/shard_map/all_to_all | solution.py:106
  132.6 14.5 %all_to_all.22 = f32[4,4,32,128]{3,2,1,0:T(8,128)S(1)} all-to-all(f32[4,4,32,128]{3,2,1,0:T(8,128)S(1)} %bitcast.216), channel_id=1, replica_groups=mesh['y'=4,'z'=4,'x'=4,'core'=2] {'z'}, dimensions={0} | all-to-all | bytes 524288 | tf_op jit(solution)/shard_map/all_to_all | solution.py:106
  147.7 4.5 %all-to-all-start.3 = ((f32[4,1,32,128]{3,2,1,0:T(8,128)}), f32[4,1,32,128]{3,2,1,0:T(8,128)S(1)}, u32[]{:S(2)}, u32[]{:S(2)}) async-start(f32[4,1,32,128]{3,2,1,0:T(8,128)} %bitcast.62), calls=%async_computation.3 | async-start | bytes 131072 | tf_op jit(solution)/shard_map/all_to_all | solution.py:106
  152.2 1.1 copy.53
  153.3 4.5 %all-to-all-done.3 = f32[4,1,32,128]{3,2,1,0:T(8,128)S(1)} async-done(((f32[4,1,32,128]{3,2,1,0:T(8,128)}), f32[4,1,32,128]{3,2,1,0:T(8,128)S(1)}, u32[]{:S(2)}, u32[]{:S(2)}) %all-to-all-start.3) | async-done | bytes 65568 | tf_op jit(solution)/shard_map/all_to_all | solution.py:106
  (49 shorter events, 13.7 us)
Async XLA Ops:
  1.6 3.5 %collective-permute-start = (bf16[2,1,640,128]{3,2,1,0:T(8,128)(2,1)S(1)}, bf16[2,1,640,128]{3,2,1,0:T(8,128)(2,1)S(1)}, u32[]{:S(2)}, u32[]{:S(2)}) collective-permute-start(bf16[2,1,640,128]{3,2,1,0:T(8,128)(2,1)S(1)} %slice.233), channel_id=1, source_target_pairs={{1,0},{3,2},{5,4},{7,6},{9,8},{11,10},{13,12},{15,14},{17,16},{19,... | collective-permute-start | bytes 983048 | tf_op jit(solution)/shard_map/ppermute | solution.py:14
  5.2 24.8 %collective-permute-start.1 = (bf16[6,1,640,128]{3,2,1,0:T(8,128)(2,1)S(1)}, bf16[6,1,640,128]{3,2,1,0:T(8,128)(2,1)S(1)}, u32[]{:S(2)}, u32[]{:S(2)}) collective-permute-start(bf16[6,1,640,128]{3,2,1,0:T(8,128)(2,1)S(1)} %constant_dynamic-update-slice_fusion), channel_id=1, source_target_pairs={{0,2},{2,4},{4,6},{6,8},{8,10},{10,12},{12,14},{14,16},{16,18},{18... | collective-permute-start | bytes 2949128 | tf_op jit(solution)/shard_map/ppermute | solution.py:24
  8.8 25.4 %collective-permute-start.2 = (bf16[6,1,640,128]{3,2,1,0:T(8,128)(2,1)S(1)}, bf16[6,1,640,128]{3,2,1,0:T(8,128)(2,1)S(1)}, u32[]{:S(2)}, u32[]{:S(2)}) collective-permute-start(bf16[6,1,640,128]{3,2,1,0:T(8,128)(2,1)S(1)} %constant_dynamic-update-slice_fusion), channel_id=1, source_target_pairs={{2,0},{4,2},{6,4},{8,6},{10,8},{12,10},{14,12},{16,14},{18,16},{20... | collective-permute-start | bytes 2949128 | tf_op jit(solution)/shard_map/ppermute | solution.py:25
  39.5 0.9 copy-start.8
  41.5 0.9 copy-start.7
  42.3 0.9 copy-start.6
  43.9 0.9 copy-start.5
  44.8 0.9 copy-start.4
  45.7 1.1 copy-start
  46.8 0.9 copy-start.3
  51.2 1.8 %copy-start.1 = (bf16[4,1,640,128]{2,3,0,1:T(8,128)(2,1)S(1)}, bf16[4,1,640,128]{2,3,0,1:T(8,128)(2,1)}, u32[]{:S(2)}) copy-start(bf16[4,1,640,128]{2,3,0,1:T(8,128)(2,1)} %copy.39) | copy-start | bytes 1966084
  55.6 2.5 %collective-permute-start.3 = (bf16[2,1,640,128]{2,3,0,1:T(8,128)(2,1)S(1)}, bf16[2,1,640,128]{2,3,0,1:T(8,128)(2,1)S(1)}, u32[]{:S(2)}, u32[]{:S(2)}) collective-permute-start(bf16[2,1,640,128]{2,3,0,1:T(8,128)(2,1)S(1)} %slice.324), channel_id=1, source_target_pairs={{0,1},{2,3},{4,5},{6,7},{8,9},{10,11},{12,13},{14,15},{16,17},{18,... | collective-permute-start | bytes 983048 | tf_op jit(solution)/shard_map/ppermute | solution.py:14
  58.2 24.9 %collective-permute-start.4 = (bf16[6,1,640,128]{2,3,0,1:T(8,128)(2,1)S(1)}, bf16[6,1,640,128]{2,3,0,1:T(8,128)(2,1)S(1)}, u32[]{:S(2)}, u32[]{:S(2)}) collective-permute-start(bf16[6,1,640,128]{2,3,0,1:T(8,128)(2,1)S(1)} %pad_maximum_fusion.9), channel_id=1, source_target_pairs={{0,2},{2,4},{4,6},{6,8},{8,10},{10,12},{12,14},{14,16},{16,18},{18... | collective-permute-start | bytes 2949128 | tf_op jit(solution)/shard_map/ppermute | solution.py:24
  61.6 25.6 %collective-permute-start.5 = (bf16[6,1,640,128]{2,3,0,1:T(8,128)(2,1)S(1)}, bf16[6,1,640,128]{2,3,0,1:T(8,128)(2,1)S(1)}, u32[]{:S(2)}, u32[]{:S(2)}) collective-permute-start(bf16[6,1,640,128]{2,3,0,1:T(8,128)(2,1)S(1)} %pad_maximum_fusion.9), channel_id=1, source_target_pairs={{2,0},{4,2},{6,4},{8,6},{10,8},{12,10},{14,12},{16,14},{18,16},{20... | collective-permute-start | bytes 2949128 | tf_op jit(solution)/shard_map/ppermute | solution.py:25
  109.8 42.4 %copy-start.2 = (bf16[4,1,640,128]{2,3,0,1:T(8,128)(2,1)S(1)}, bf16[4,1,640,128]{2,3,0,1:T(8,128)(2,1)}, u32[]{:S(2)}) copy-start(bf16[4,1,640,128]{2,3,0,1:T(8,128)(2,1)} %get-tuple-element.73) | copy-start | bytes 1966084
  147.7 10.1 %all-to-all-start.3 = ((f32[4,1,32,128]{3,2,1,0:T(8,128)}), f32[4,1,32,128]{3,2,1,0:T(8,128)S(1)}, u32[]{:S(2)}, u32[]{:S(2)}) async-start(f32[4,1,32,128]{3,2,1,0:T(8,128)} %bitcast.62), calls=%async_computation.3 | async-start | bytes 131072 | tf_op jit(solution)/shard_map/all_to_all | solution.py:106

commit v5 on v4

--- a/solution.py
+++ b/solution.py
@@ -35,11 +35,7 @@
     cot_ext = jnp.concatenate([cotangent, future], axis=0)
     cot_rows = with_halo(cot_ext, (("ha", 1),), 1)
     cot_pad = jnp.pad(cot_rows, ((0, 0), (0, 0), (1, 1), (0, 0)))
-    cot_flat = cotangent.reshape(-1, channels)
-    past = passed_along(active[-2:], "ta", 1)
-    act_ext = jnp.concatenate([past, active], axis=0)
-    act_rows = with_halo(act_ext, (("ha", 1),), 1)
-    act_pad = jnp.pad(act_rows, ((0, 0), (0, 0), (1, 1), (0, 0)))
+    act_flat = active.reshape(-1, channels)
     grad_input = jnp.zeros((frames * height * breadth, channels), jnp.float32)
     blocks = []
     for t_tap in range(3):
@@ -57,17 +53,11 @@
             ).reshape(-1, 3 * channels)
             stacked = jnp.transpose(kernel[t_tap, h_tap], (0, 2, 1)).reshape(3 * channels, channels)
             grad_input = grad_input + jnp.dot(cot_slab, stacked, preferred_element_type=jnp.float32)
-            act_slab = jnp.concatenate(
-                [
-                    act_pad[t_tap : t_tap + frames, h_tap : h_tap + height, w_tap : w_tap + breadth]
-                    for w_tap in range(3)
-                ],
-                axis=-1,
-            ).reshape(-1, 3 * channels)
+            paired = lax.dot_general(
+                act_flat, cot_slab, (((0,), (0,)), ((), ())), preferred_element_type=jnp.float32
+            )
             blocks.append(
-                lax.dot_general(
-                    act_slab, cot_flat, (((0,), (0,)), ((), ())), preferred_element_type=jnp.float32
-                )
+                paired.reshape(channels, 3, channels).transpose(1, 0, 2).reshape(3 * channels, channels)
             )
     total_cells = frames * height * breadth * lax.axis_size("ha") * lax.axis_size("ta")
     factor = float(total_cells) ** (-0.5)

time: 160 us -> 169 us (1.056)
  local copies, waits for them, and re-layouts: 33.7 us -> 63.7 us
  waiting for transfers between devices: 39.1 us -> 15 us
  starting transfers between devices: 16.8 us -> 6.15 us
  blocking collectives: 42.5 us -> 49.3 us
  other arithmetic: 11.8 us -> 16.9 us
  matrix products: 13.4 us -> 15.6 us
    reshape x1 -> x9, local copies, waits for them, and re-layouts: 1.78 us -> 33 us  [body(): cot_slab = jnp.concatenate([cot_pad[2 - t_tap:2 - t_tap + frames, 2 - h_t...]
    ppermute x2 -> x1, waiting for transfers between devices: 24 us -> 9.75 us  [with_halo(): before = lax.ppermute(last, axis, up)]
    concatenate x5, other arithmetic: 2.51 us -> 12.5 us  [body(): jnp.concatenate([cot_pad[2 - t_tap:2 - t_tap + frames, 2 - h_tap:2 - h_ta...]
    all_to_all x3 -> x4, blocking collectives: 42.5 us -> 49.3 us  [reduce_blocks(): part = lax.all_to_all(shaped, axis, 0, 0, tiled=True).sum(0)]
    all_to_all x1 -> x0, waiting for transfers between devices: 4.54 us -> none  [reduce_blocks(): part = lax.all_to_all(shaped, axis, 0, 0, tiled=True).sum(0)]
    all_to_all x1 -> x0, starting transfers between devices: 4.47 us -> none  [reduce_blocks(): part = lax.all_to_all(shaped, axis, 0, 0, tiled=True).sum(0)]
    slice x4 -> x0, local copies, waits for them, and re-layouts: 4.4 us -> none  [the longest x3 4.37 us: body(): act_pad[t_tap:t_tap + frames, h_tap:h_tap + height, w_tap:w_tap + breadth]]
    ppermute x2 -> x1, waiting for transfers between devices: 8.35 us -> 4.17 us  [with_halo(): after = lax.ppermute(leading, axis, down)]
  transfers between devices with their start and end apart: 7 -> 3, of which waited for: 7 -> 3; matrix products, arithmetic and copies ran while one was open for 11% -> 7% of each run, Pallas kernels for 0% -> 0%
where the time goes in v5:
time: 169 us; the launch traced here: 168 us
  local copies, waits for them, and re-layouts  63.7 us (38%)
  blocking collectives  49.3 us (29%)
  other arithmetic  16.9 us (10%)
  matrix products  15.6 us (9%)
  waiting for transfers between devices  15 us (9%)
  starting transfers between devices  6.15 us (4%)
    all_to_all x4, blocking collectives, reduce_blocks(): part = lax.all_to_all(shaped, axis, 0, 0, tiled=True).sum(0)  49.3 us
    reshape x9, local copies, waits for them, and re-layouts, body(): cot_slab = jnp.concatenate([cot_pad[2 - t_tap:2 - t_tap + frames, 2 - h_t...  33 us
    unnamed x76, local copies, waits for them, and re-layouts  18.6 us
    concatenate x5, other arithmetic, body(): jnp.concatenate([cot_pad[2 - t_tap:2 - t_tap + frames, 2 - h_tap:2 - h_ta...  12.5 us
    ppermute x1, waiting for transfers between devices, with_halo(): before = lax.ppermute(last, axis, up)  9.75 us
    dot_general x9, matrix products, body(): jnp.dot(cot_slab, stacked, preferred_element_type=jnp.float32)  9.21 us
    slice x4, local copies, waits for them, and re-layouts, body(): cot_pad[2 - t_tap:2 - t_tap + frames, 2 - h_tap:2 - h_tap + height, 2 - w...  7.76 us
    dot_general x9, matrix products, body(): lax.dot_general(act_flat, cot_slab, (((0,), (0,)), ((), ())), preferred_e...  6.35 us
  transfers between devices with their start and end apart: 3, of which 3 were waited for; matrix products, arithmetic and copies ran while one was open for 7% of the time, Pallas kernels for 0%

profile of v5, /device:TPU:0, one launch (start us, length us, event | category | flops | bytes accessed | tf_op | source)
XLA Modules:
  0.0 167.7 jit_solution(5722307703793977515)
XLA Ops:
  0.6 1.1 slice.133
  1.7 1.3 collective-permute-start
  3.0 1.1 constant_dynamic-update-slice_fusion.1
  4.2 1.1 collective-permute-done
  5.3 3.6 %collective-permute-start.1 = (bf16[6,1,640,128]{3,2,1,0:T(8,128)(2,1)S(1)}, bf16[6,1,640,128]{3,2,1,0:T(8,128)(2,1)S(1)}, u32[]{:S(2)}, u32[]{:S(2)}) collective-permute-start(bf16[6,1,640,128]{3,2,1,0:T(8,128)(2,1)S(1)} %constant_dynamic-update-slice_fusion), channel_id=1, source_target_pairs={{0,2},{2,4},{4,6},{6,8},{8,10},{10,12},{12,14},{14,16},{16,18},{18... | collective-permute-start | bytes 2949128 | tf_op jit(solution)/shard_map/ppermute | solution.py:24
  8.9 1.3 collective-permute-start.2
  10.2 0.8 fusion.19
  10.9 1.0 copy.132
  12.0 1.6 copy.133
  13.6 1.6 copy.134
  15.2 1.6 copy.135
  16.9 0.7 copy.136
  17.6 0.7 copy.137
  19.4 1.0 fusion.18
  20.3 9.8 %collective-permute-done.1 = bf16[6,1,640,128]{3,2,1,0:T(8,128)(2,1)S(1)} collective-permute-done((bf16[6,1,640,128]{3,2,1,0:T(8,128)(2,1)S(1)}, bf16[6,1,640,128]{3,2,1,0:T(8,128)(2,1)S(1)}, u32[]{:S(2)}, u32[]{:S(2)}) %collective-permute-start.1) | collective-permute-done | bytes 983072 | tf_op jit(solution)/shard_map/ppermute | solution.py:24
  30.1 4.2 %collective-permute-done.2 = bf16[6,1,640,128]{3,2,1,0:T(8,128)(2,1)S(1)} collective-permute-done((bf16[6,1,640,128]{3,2,1,0:T(8,128)(2,1)S(1)}, bf16[6,1,640,128]{3,2,1,0:T(8,128)(2,1)S(1)}, u32[]{:S(2)}, u32[]{:S(2)}) %collective-permute-start.2) | collective-permute-done | bytes 983072 | tf_op jit(solution)/shard_map/ppermute | solution.py:25
  34.3 1.1 fusion.5
  35.4 4.2 %fusion.15 = (bf16[4,1,640,128]{3,2,1,0:T(8,128)(2,1)}, bf16[4,1,640,128]{3,2,1,0:T(8,128)(2,1)}, bf16[4,1,640,128]{3,2,1,0:T(8,128)(2,1)}, bf16[4,1,640,128]{3,...) fusion(bf16[6,3,642,128]{3,2,1,0:T(8,128)(2,1)S(1)} %fusion.5), kind=kLoop, calls=%fused_computation.50 | loop fusion | bytes 23592960 | tf_op jit(solution)/shard_map/slice | solution.py:45
  39.5 1.3 fusion.17
  40.8 1.6 pad_maximum_fusion
  42.4 2.4 %copy.94 = bf16[2560,384]{0,1:T(8,128)(2,1)} copy(bf16[2560,384]{1,0:T(8,128)(2,1)S(1)} %bitcast.195) | data formatting | bytes 3932160 | tf_op jit(solution)/shard_map/reshape | solution.py:53
  44.9 1.8 %fusion.20 = f32[2560,128]{1,0:T(8,128)} fusion(bf16[2560,384]{1,0:T(8,128)(2,1)S(1)} %bitcast.196, bf16[384,128]{1,0:T(8,128)(2,1)S(1)} %bitcast.220), kind=kOutput, calls=%fused_computation.55 | convolution fusion | flops 251658240 | bytes 3375104 | tf_op jit(solution)/shard_map/dot_general | solution.py:55
  46.6 1.3 fusion.16
  48.5 2.4 %copy.110 = bf16[2560,384]{0,1:T(8,128)(2,1)} copy(bf16[2560,384]{1,0:T(8,128)(2,1)S(1)} %bitcast.179) | data formatting | bytes 3932160 | tf_op jit(solution)/shard_map/reshape | solution.py:53
  51.0 3.4 %pad_maximum_fusion.6 = (bf16[4,1,640,384]{3,2,1,0:T(8,128)(2,1)}, bf16[4,1,640,384]{3,2,1,0:T(8,128)(2,1)}) fusion(bf16[4,1,640,128]{3,2,1,0:T(8,128)(2,1)} %get-tuple-element.6, bf16[4,1,640,128]{3,2,1,0:T(8,128)(2,1)} %get-tuple-element.24, bf16[4,1,640,128]{3,2,1,0:T(8,128)(2,1)} %get-tuple-element.7, bf16[4,1,640,128]{3,2,1,0:T(8,128)(2,1)S(1)} %copy-done.18, ...), kind=kLoop, calls=%fused_computation.22 | loop fusion | flops 11796480 | bytes 7864320 | tf_op jit(solution)/shard_map/concatenate | solution.py:43
  54.4 4.0 %copy.108 = bf16[2560,384]{0,1:T(8,128)(2,1)} copy(bf16[2560,384]{1,0:T(8,128)(2,1)} %bitcast.181) | data formatting | bytes 3932160 | tf_op jit(solution)/shard_map/reshape | solution.py:53
  58.4 4.0 %copy.106 = bf16[2560,384]{0,1:T(8,128)(2,1)} copy(bf16[2560,384]{1,0:T(8,128)(2,1)} %bitcast.185) | data formatting | bytes 3932160 | tf_op jit(solution)/shard_map/reshape | solution.py:53
  62.4 3.6 %pad_maximum_fusion.4 = (bf16[4,1,640,384]{3,2,1,0:T(8,128)(2,1)}, bf16[4,1,640,384]{3,2,1,0:T(8,128)(2,1)}) fusion(bf16[4,1,640,128]{3,2,1,0:T(8,128)(2,1)} %get-tuple-element.10, bf16[4,1,640,128]{3,2,1,0:T(8,128)(2,1)} %get-tuple-element.27, bf16[4,1,640,128]{3,2,1,0:T(8,128)(2,1)} %get-tuple-element.11, bf16[4,1,640,128]{3,2,1,0:T(8,128)(2,1)S(1)} %copy-done.17, ...), kind=kLoop, calls=%fused_computation.20 | loop fusion | flops 11796480 | bytes 7864320 | tf_op jit(solution)/shard_map/concatenate | solution.py:43
  66.0 4.0 %copy.104 = bf16[2560,384]{0,1:T(8,128)(2,1)} copy(bf16[2560,384]{1,0:T(8,128)(2,1)} %bitcast.187) | data formatting | bytes 3932160 | tf_op jit(solution)/shard_map/reshape | solution.py:53
  70.0 4.1 %copy.102 = bf16[2560,384]{0,1:T(8,128)(2,1)} copy(bf16[2560,384]{1,0:T(8,128)(2,1)} %bitcast.189) | data formatting | bytes 3932160 | tf_op jit(solution)/shard_map/reshape | solution.py:53
  74.1 3.6 %pad_maximum_fusion.2 = (bf16[4,1,640,384]{3,2,1,0:T(8,128)(2,1)}, bf16[4,1,640,384]{3,2,1,0:T(8,128)(2,1)}) fusion(bf16[4,1,640,128]{3,2,1,0:T(8,128)(2,1)} %get-tuple-element.14, bf16[4,1,640,128]{3,2,1,0:T(8,128)(2,1)} %get-tuple-element.23, bf16[4,1,640,128]{3,2,1,0:T(8,128)(2,1)} %get-tuple-element.15, bf16[4,1,640,128]{3,2,1,0:T(8,128)(2,1)S(1)} %copy-done.16, ...), kind=kLoop, calls=%fused_computation.18 | loop fusion | flops 11796480 | bytes 7864320 | tf_op jit(solution)/shard_map/concatenate | solution.py:43
  77.7 4.0 %copy.100 = bf16[2560,384]{0,1:T(8,128)(2,1)} copy(bf16[2560,384]{1,0:T(8,128)(2,1)} %bitcast.191) | data formatting | bytes 3932160 | tf_op jit(solution)/shard_map/reshape | solution.py:53
  81.6 4.0 %copy.98 = bf16[2560,384]{0,1:T(8,128)(2,1)} copy(bf16[2560,384]{1,0:T(8,128)(2,1)} %bitcast.193) | data formatting | bytes 3932160 | tf_op jit(solution)/shard_map/reshape | solution.py:53
  85.7 4.0 %copy.96 = bf16[2560,384]{0,1:T(8,128)(2,1)} copy(bf16[2560,384]{1,0:T(8,128)(2,1)} %bitcast.183) | data formatting | bytes 3932160 | tf_op jit(solution)/shard_map/reshape | solution.py:53
  89.7 2.7 %convolution_add_fusion.7 = f32[2560,128]{1,0:T(8,128)S(1)} fusion(f32[2560,128]{1,0:T(8,128)} %fusion.20, bf16[2560,384]{1,0:T(8,128)(2,1)} %bitcast.184, bf16[384,128]{1,0:T(8,128)(2,1)S(1)} %bitcast.228), kind=kOutput, calls=%fused_computation.10 | convolution fusion | flops 251985920 | bytes 4685824 | tf_op jit(solution)/shard_map/dot_general | solution.py:55
  93.2 0.8 copy-done.4
  94.7 0.9 copy-done.3
  96.2 0.9 copy-done.2
  97.8 0.9 copy-done.1
  99.3 0.9 copy-done
  102.0 1.5 fusion.14
  104.2 0.8 copy-done.9
  114.1 1.4 broadcast_multiply_fusion
  115.5 1.5 mul.29
  117.4 5.4 %all_to_all.20 = f32[2,64,32,128]{3,2,1,0:T(8,128)S(1)} all-to-all(f32[2,64,32,128]{3,2,1,0:T(8,128)S(1)} %bitcast.198), channel_id=1, replica_groups=mesh['y'=4,'z'=4,'x'=4,'core'=2] {'core'}, dimensions={0} | all-to-all | bytes 4194304 | tf_op jit(solution)/shard_map/all_to_all | solution.py:96
  123.1 21.6 %all_to_all.21 = f32[4,16,32,128]{3,2,1,0:T(8,128)S(1)} all-to-all(f32[4,16,32,128]{3,2,1,0:T(8,128)S(1)} %bitcast.209), channel_id=1, replica_groups=mesh['y'=4,'z'=4,'x'=4,'core'=2] {'x'}, dimensions={0} | all-to-all | bytes 2097152 | tf_op jit(solution)/shard_map/all_to_all | solution.py:96
  144.8 12.3 %all_to_all.22 = f32[4,4,32,128]{3,2,1,0:T(8,128)S(1)} all-to-all(f32[4,4,32,128]{3,2,1,0:T(8,128)S(1)} %bitcast.210), channel_id=1, replica_groups=mesh['y'=4,'z'=4,'x'=4,'core'=2] {'z'}, dimensions={0} | all-to-all | bytes 524288 | tf_op jit(solution)/shard_map/all_to_all | solution.py:96
  157.2 9.9 %all_to_all.23 = f32[4,1,32,128]{3,2,1,0:T(8,128)S(1)} all-to-all(f32[4,1,32,128]{3,2,1,0:T(8,128)S(1)} %bitcast.229), channel_id=1, replica_groups=mesh['y'=4,'z'=4,'x'=4,'core'=2] {'y'}, dimensions={0} | all-to-all | bytes 131072 | tf_op jit(solution)/shard_map/all_to_all | solution.py:96
  (89 shorter events, 17.7 us)
Async XLA Ops:
  0.6 9.5 %copy-start.21 = (bf16[3,3,3,128,128]{4,3,2,1,0:T(8,128)(2,1)S(1)}, bf16[3,3,3,128,128]{4,3,2,1,0:T(8,128)(2,1)}, u32[]{:S(2)}) copy-start(bf16[3,3,3,128,128]{4,3,2,1,0:T(8,128)(2,1)} %param.6) | copy-start | bytes 2654212
  1.7 3.5 %collective-permute-start = (bf16[2,1,640,128]{3,2,1,0:T(8,128)(2,1)S(1)}, bf16[2,1,640,128]{3,2,1,0:T(8,128)(2,1)S(1)}, u32[]{:S(2)}, u32[]{:S(2)}) collective-permute-start(bf16[2,1,640,128]{3,2,1,0:T(8,128)(2,1)S(1)} %slice.133), channel_id=1, source_target_pairs={{1,0},{3,2},{5,4},{7,6},{9,8},{11,10},{13,12},{15,14},{17,16},{19,... | collective-permute-start | bytes 983048 | tf_op jit(solution)/shard_map/ppermute | solution.py:14
  5.3 24.8 %collective-permute-start.1 = (bf16[6,1,640,128]{3,2,1,0:T(8,128)(2,1)S(1)}, bf16[6,1,640,128]{3,2,1,0:T(8,128)(2,1)S(1)}, u32[]{:S(2)}, u32[]{:S(2)}) collective-permute-start(bf16[6,1,640,128]{3,2,1,0:T(8,128)(2,1)S(1)} %constant_dynamic-update-slice_fusion), channel_id=1, source_target_pairs={{0,2},{2,4},{4,6},{6,8},{8,10},{10,12},{12,14},{14,16},{16,18},{18... | collective-permute-start | bytes 2949128 | tf_op jit(solution)/shard_map/ppermute | solution.py:24
  8.9 25.4 %collective-permute-start.2 = (bf16[6,1,640,128]{3,2,1,0:T(8,128)(2,1)S(1)}, bf16[6,1,640,128]{3,2,1,0:T(8,128)(2,1)S(1)}, u32[]{:S(2)}, u32[]{:S(2)}) collective-permute-start(bf16[6,1,640,128]{3,2,1,0:T(8,128)(2,1)S(1)} %constant_dynamic-update-slice_fusion), channel_id=1, source_target_pairs={{2,0},{4,2},{6,4},{8,6},{10,8},{12,10},{14,12},{16,14},{18,16},{20... | collective-permute-start | bytes 2949128 | tf_op jit(solution)/shard_map/ppermute | solution.py:25
  46.6 1.3 copy-start.19
  46.6 1.6 copy-start.20
  48.5 2.5 %copy-start.6 = (bf16[4,1,640,128]{3,2,1,0:T(8,128)(2,1)S(1)}, bf16[4,1,640,128]{3,2,1,0:T(8,128)(2,1)}, u32[]{:S(2)}) copy-start(bf16[4,1,640,128]{3,2,1,0:T(8,128)(2,1)} %param.5) | copy-start | bytes 1966084
  48.5 2.4 %copy-start.18 = (bf16[4,1,640,128]{3,2,1,0:T(8,128)(2,1)S(1)}, bf16[4,1,640,128]{3,2,1,0:T(8,128)(2,1)}, u32[]{:S(2)}) copy-start(bf16[4,1,640,128]{3,2,1,0:T(8,128)(2,1)} %get-tuple-element.4) | copy-start | bytes 1966084
  58.4 4.0 %copy-start.17 = (bf16[4,1,640,128]{3,2,1,0:T(8,128)(2,1)S(1)}, bf16[4,1,640,128]{3,2,1,0:T(8,128)(2,1)}, u32[]{:S(2)}) copy-start(bf16[4,1,640,128]{3,2,1,0:T(8,128)(2,1)} %get-tuple-element.8) | copy-start | bytes 1966084
  70.0 4.1 %copy-start.16 = (bf16[4,1,640,128]{3,2,1,0:T(8,128)(2,1)S(1)}, bf16[4,1,640,128]{3,2,1,0:T(8,128)(2,1)}, u32[]{:S(2)}) copy-start(bf16[4,1,640,128]{3,2,1,0:T(8,128)(2,1)} %get-tuple-element.12) | copy-start | bytes 1966084
  85.7 4.0 %copy-start.28 = (bf16[1,1,3,128,128]{3,4,2,1,0:T(8,128)(2,1)S(1)}, bf16[1,1,3,128,128]{3,4,2,1,0:T(8,128)(2,1)}, u32[]{:S(2)}) copy-start(bf16[1,1,3,128,128]{3,4,2,1,0:T(8,128)(2,1)} %copy.133) | copy-start | bytes 294916
  89.7 2.7 %copy-start.5 = (bf16[4,1,640,384]{3,2,1,0:T(8,128)(2,1)S(1)}, bf16[4,1,640,384]{3,2,1,0:T(8,128)(2,1)}, u32[]{:S(2)}) copy-start(bf16[4,1,640,384]{3,2,1,0:T(8,128)(2,1)} %get-tuple-element.42) | copy-start | bytes 5898244
  89.7 2.8 %copy-start.27 = (bf16[1,1,3,128,128]{3,4,2,1,0:T(8,128)(2,1)S(1)}, bf16[1,1,3,128,128]{3,4,2,1,0:T(8,128)(2,1)}, u32[]{:S(2)}) copy-start(bf16[1,1,3,128,128]{3,4,2,1,0:T(8,128)(2,1)} %copy.134) | copy-start | bytes 294916
  92.5 1.5 copy-start.4
  92.5 1.5 copy-start.26
  94.0 1.5 copy-start.3
  94.0 1.5 copy-start.25
  95.6 1.5 copy-start.2
  95.6 1.5 copy-start.24
  97.1 1.5 copy-start.1
  97.1 1.5 copy-start.23
  98.7 1.5 copy-start
  100.9 1.1 copy-start.22
  102.0 1.5 copy-start.8
  103.5 1.5 copy-start.9
  104.2 1.7 %copy-start.10 = (bf16[2560,384]{0,1:T(8,128)(2,1)S(1)}, bf16[2560,384]{0,1:T(8,128)(2,1)}, u32[]{:S(2)}) copy-start(bf16[2560,384]{0,1:T(8,128)(2,1)} %copy.106) | copy-start | bytes 5898244
  105.8 1.6 copy-start.11
  106.6 1.7 %copy-start.12 = (bf16[2560,384]{0,1:T(8,128)(2,1)S(1)}, bf16[2560,384]{0,1:T(8,128)(2,1)}, u32[]{:S(2)}) copy-start(bf16[2560,384]{0,1:T(8,128)(2,1)} %copy.102) | copy-start | bytes 5898244
  108.1 1.6 copy-start.13
  109.1 1.7 %copy-start.14 = (bf16[2560,384]{0,1:T(8,128)(2,1)S(1)}, bf16[2560,384]{0,1:T(8,128)(2,1)}, u32[]{:S(2)}) copy-start(bf16[2560,384]{0,1:T(8,128)(2,1)} %copy.98) | copy-start | bytes 5898244
  110.4 1.6 copy-start.15
  111.5 1.7 %copy-start.7 = (bf16[2560,384]{0,1:T(8,128)(2,1)S(1)}, bf16[2560,384]{0,1:T(8,128)(2,1)}, u32[]{:S(2)}) copy-start(bf16[2560,384]{0,1:T(8,128)(2,1)} %copy.94) | copy-start | bytes 5898244

commit v6 on v5

--- a/solution.py
+++ b/solution.py
@@ -34,43 +34,35 @@
     future = passed_along(cotangent[:2], "ta", -1)
     cot_ext = jnp.concatenate([cotangent, future], axis=0)
     cot_rows = with_halo(cot_ext, (("ha", 1),), 1)
-    cot_pad = jnp.pad(cot_rows, ((0, 0), (0, 0), (1, 1), (0, 0)))
-    act_flat = active.reshape(-1, channels)
-    grad_input = jnp.zeros((frames * height * breadth, channels), jnp.float32)
-    blocks = []
-    for t_tap in range(3):
-        for h_tap in range(3):
-            cot_slab = jnp.concatenate(
-                [
-                    cot_pad[
-                        2 - t_tap : 2 - t_tap + frames,
-                        2 - h_tap : 2 - h_tap + height,
-                        2 - w_tap : 2 - w_tap + breadth,
-                    ]
-                    for w_tap in range(3)
-                ],
-                axis=-1,
-            ).reshape(-1, 3 * channels)
-            stacked = jnp.transpose(kernel[t_tap, h_tap], (0, 2, 1)).reshape(3 * channels, channels)
-            grad_input = grad_input + jnp.dot(cot_slab, stacked, preferred_element_type=jnp.float32)
-            paired = lax.dot_general(
-                act_flat, cot_slab, (((0,), (0,)), ((), ())), preferred_element_type=jnp.float32
-            )
-            blocks.append(
-                paired.reshape(channels, 3, channels).transpose(1, 0, 2).reshape(3 * channels, channels)
-            )
+    taps = kernel.shape[:3]
+    edges = ((0, 0), (0, 0), (1, 1))
+    flipped = jnp.flip(kernel, (0, 1, 2))
+    grad_input = lax.conv_general_dilated(
+        cot_rows[None],
+        flipped,
+        (1, 1, 1),
+        edges,
+        dimension_numbers=("NDHWC", "DHWOI", "NDHWC"),
+        preferred_element_type=jnp.float32,
+    )[0]
+    paired = lax.conv_general_dilated(
+        cot_rows[..., None],
+        active[:, :, :, None, :],
+        (1, 1, 1),
+        edges,
+        dimension_numbers=("DHWNC", "DHWIO", "DHWCN"),
+        preferred_element_type=jnp.float32,
+    )
     total_cells = frames * height * breadth * lax.axis_size("ha") * lax.axis_size("ta")
     factor = float(total_cells) ** (-0.5)
-    term = jnp.concatenate(blocks, axis=0) * factor
+    term = jnp.flip(paired, (0, 1, 2)).reshape(-1, channels) * factor
     owners = lax.axis_size("ha") * lax.axis_size("ta")
     rows = term.shape[0] // owners
     padded = -(-rows // 8) * 8
     term = jnp.pad(term.reshape(owners, rows, channels), ((0, 0), (0, padded - rows), (0, 0)))
     sigmoid_part = jax.nn.sigmoid(values)
     derivative = sigmoid_part * (1.0 + values * (1.0 - sigmoid_part))
-    grad_features = (
-        cotangent.astype(jnp.float32) + derivative * grad_input.reshape(features.shape)
-    ).astype(jnp.bfloat16)
+    grad_features = (cotangent.astype(jnp.float32) + derivative * grad_input).astype(jnp.bfloat16)
     return (grad_features, term[None])
 
 

time: 169 us -> 152 us (0.90)
  local copies, waits for them, and re-layouts: 63.7 us -> 19 us
  matrix products: 15.6 us -> 41.8 us
  waiting for transfers between devices: 15 us -> 26.7 us
  other arithmetic: 16.9 us -> 6.25 us
  starting transfers between devices: 6.15 us -> 14.7 us
  blocking collectives: 49.3 us -> 41.8 us
    conv_general_dilated x0 -> x2, matrix products: none -> 41.8 us  [the longest x1 36.7 us: body(): lax.conv_general_dilated(cot_rows[..., None], active[:, :, :, None, :], (...]
    reshape x9 -> x0, local copies, waits for them, and re-layouts: 33 us -> none  [body(): cot_slab = jnp.concatenate([cot_pad[2 - t_tap:2 - t_tap + frames, 2 - h_t...]
    ppermute x1, waiting for transfers between devices: 4.17 us -> 19.8 us  [with_halo(): after = lax.ppermute(leading, axis, down)]
    unnamed x76 -> x14, local copies, waits for them, and re-layouts: 18.6 us -> 3 us
    dot_general x18 -> x0, matrix products: 15.6 us -> none  [the longest x9 9.21 us: body(): jnp.dot(cot_slab, stacked, preferred_element_type=jnp.float32)]
    concatenate x6 -> x0, other arithmetic: 13.6 us -> none  [the longest x5 12.5 us: body(): jnp.concatenate([cot_pad[2 - t_tap:2 - t_tap + frames, 2 - h_tap:2 - h_ta...]
    ppermute x1, waiting for transfers between devices: 9.75 us -> 1.18 us  [with_halo(): before = lax.ppermute(last, axis, up)]
    slice x5 -> x0, local copies, waits for them, and re-layouts: 8.53 us -> none  [the longest x4 7.76 us: body(): cot_pad[2 - t_tap:2 - t_tap + frames, 2 - h_tap:2 - h_tap + height, 2 - w...]
  transfers between devices with their start and end apart: 3 -> 4, of which waited for: 3 -> 4; matrix products, arithmetic and copies ran while one was open for 7% -> 1% of each run, Pallas kernels for 0% -> 0%
where the time goes in v6:
time: 152 us; the launch traced here: 151 us
  matrix products  41.8 us (28%)
  blocking collectives  41.8 us (28%)
  waiting for transfers between devices  26.7 us (18%)
  local copies, waits for them, and re-layouts  19 us (12%)
  starting transfers between devices  14.7 us (10%)
  other arithmetic  6.25 us (4%)
    all_to_all x3, blocking collectives, reduce_blocks(): part = lax.all_to_all(shaped, axis, 0, 0, tiled=True).sum(0)  41.8 us
    conv_general_dilated x1, matrix products, body(): lax.conv_general_dilated(cot_rows[..., None], active[:, :, :, None, :], (...  36.7 us
    ppermute x1, waiting for transfers between devices, with_halo(): after = lax.ppermute(leading, axis, down)  19.8 us
    conv_general_dilated x4, local copies, waits for them, and re-layouts, body(): lax.conv_general_dilated(cot_rows[None], flipped, (1, 1, 1), edges, dimen...  7.92 us
    all_to_all x1, starting transfers between devices, reduce_blocks(): part = lax.all_to_all(shaped, axis, 0, 0, tiled=True).sum(0)  7.49 us
    conv_general_dilated x1, matrix products, body(): lax.conv_general_dilated(cot_rows[None], flipped, (1, 1, 1), edges, dimen...  5.08 us
    all_to_all x1, waiting for transfers between devices, reduce_blocks(): part = lax.all_to_all(shaped, axis, 0, 0, tiled=True).sum(0)  4.7 us
    ppermute x1, starting transfers between devices, with_halo(): before = lax.ppermute(last, axis, up)  4.61 us
  transfers between devices with their start and end apart: 4, of which 4 were waited for; matrix products, arithmetic and copies ran while one was open for 1% of the time, Pallas kernels for 0%

profile of v6, /device:TPU:0, one launch (start us, length us, event | category | flops | bytes accessed | tf_op | source)
XLA Modules:
  0.0 151.1 jit_solution(7385949535220676404)
XLA Ops:
  0.6 0.0 copy-start
  0.6 1.1 slice.9
  1.7 1.3 collective-permute-start
  3.0 1.1 constant_dynamic-update-slice_fusion.1
  4.2 1.1 collective-permute-done
  5.3 1.3 collective-permute-start.2
  6.6 4.6 %collective-permute-start.1 = (bf16[6,1,640,128]{3,2,1,0:T(8,128)(2,1)S(1)}, bf16[6,1,640,128]{3,2,1,0:T(8,128)(2,1)S(1)}, u32[]{:S(2)}, u32[]{:S(2)}) collective-permute-start(bf16[6,1,640,128]{3,2,1,0:T(8,128)(2,1)S(1)} %constant_dynamic-update-slice_fusion), channel_id=1, source_target_pairs={{0,2},{2,4},{4,6},{6,8},{8,10},{10,12},{12,14},{14,16},{16,18},{18... | collective-permute-start | bytes 2949128 | tf_op jit(solution)/shard_map/ppermute | solution.py:24
  11.2 19.8 %collective-permute-done.2 = bf16[6,1,640,128]{3,2,1,0:T(8,128)(2,1)S(1)} collective-permute-done((bf16[6,1,640,128]{3,2,1,0:T(8,128)(2,1)S(1)}, bf16[6,1,640,128]{3,2,1,0:T(8,128)(2,1)S(1)}, u32[]{:S(2)}, u32[]{:S(2)}) %collective-permute-start.2) | collective-permute-done | bytes 983072 | tf_op jit(solution)/shard_map/ppermute | solution.py:25
  31.0 1.2 collective-permute-done.1
  32.2 1.8 %fusion.24 = (bf16[6,3,640,128,1]{3,2,1,0,4:T(8,128)(2,1)}, bf16[6,3,1,640,128]{4,3,1,0,2:T(8,128)(2,1)S(1)}) fusion(bf16[6,1,640,128]{3,2,1,0:T(8,128)(2,1)S(1)} %collective-permute-done.2, bf16[6,1,640,128]{3,2,1,0:T(8,128)(2,1)S(1)} %constant_dynamic-update-slice_fusion, bf16[6,1,640,128]{3,2,1,0:T(8,128)(2,1)S(1)} %collective-permute-done.1), kind=kLoop, calls=%fused_computation.28 | loop fusion | flops 2949120 | bytes 8847360 | tf_op jit(solution)/shard_map/broadcast_in_dim | solution.py:49
  34.0 2.4 %pad.5 = bf16[6,3,1,648,128]{4,3,1,0,2:T(8,128)(2,1)} pad(bf16[6,3,1,640,128]{4,3,1,0,2:T(8,128)(2,1)S(1)} %get-tuple-element.10, bf16[]{:T(256)} %constant.16), padding=0_0x0_0x0_0x1_7x0_0 | pad | bytes 5935106 | tf_op jit(solution)/shard_map/broadcast_in_dim | solution.py:41
  36.4 5.2 %reshape.35 = bf16[6,3,1,8,81,128]{5,4,3,1,0,2:T(8,128)(2,1)} reshape(bf16[6,3,1,648,128]{4,3,1,0,2:T(8,128)(2,1)} %pad.5) | data formatting | bytes 5971968 | tf_op jit(solution)/shard_map/conv_general_dilated | solution.py:40
  41.6 0.0 copy-start.5
  41.6 2.3 %copy.31 = bf16[6,3,1,8,81,128]{5,3,4,1,0,2:T(8,128)(2,1)S(1)} copy(bf16[6,3,1,8,81,128]{5,4,3,1,0,2:T(8,128)(2,1)} %reshape.35) | data formatting | bytes 5971968 | tf_op jit(solution)/shard_map/conv_general_dilated | solution.py:40
  44.0 0.0 copy-done
  44.0 0.0 copy-done.5
  44.0 5.1 %fusion.21 = f32[4,1,8,81,128]{4,2,3,1,0:T(8,128)S(1)} fusion(bf16[3,3,3,128,128]{4,3,2,1,0:T(8,128)(2,1)S(1)} %copy-done, bf16[6,3,1,7,2,128]{5,3,4,1,0,2:T(8,128)(2,1)S(1)} %slice.14, bf16[6,3,1,8,81,128]{5,3,4,1,0,2:T(8,128)(2,1)S(1)} %copy.31, pred[8,81]{0,1:T(8,128)(4,1)S(1)} %copy-done.5), kind=kOutput, calls=%fused_computation.27 | convolution fusion | flops 2302746624 | bytes 5262984 | tf_op jit(solution)/shard_map/conv_general_dilated | solution.py:40
  49.1 0.0 copy-start.1
  49.1 0.0 copy-start.4
  49.1 0.3 copy.32
  49.5 0.7 copy-done.1
  50.2 0.2 copy-done.4
  50.4 0.0 copy-start.2
  50.4 2.3 %fusion.26 = (bf16[4,1,640,1,128]{4,0,2,3,1:T(4,128)(2,1)S(1)}, bf16[4,1,640,128]{3,0,2,1:T(4,128)(2,1)}) fusion(bf16[4,1,640,128]{3,2,1,0:T(8,128)(2,1)S(1)} %copy-done.4, f32[4,1,1,648,128]{4,0,3,2,1:T(4,128)S(1)} %bitcast.37, bf16[4,1,640,128]{3,2,1,0:T(8,128)(2,1)S(1)} %copy-done.1), kind=kLoop, calls=%fused_computation.30 | loop fusion | flops 4587520 | bytes 3932160 | tf_op jit(solution)/shard_map/broadcast_in_dim | solution.py:50
  52.7 0.0 copy-done.2
  52.7 36.7 %fusion.1 = f32[3,3,3,128,128]{3,4,2,1,0:T(8,128)S(1)} fusion(bf16[6,3,640,128,1]{3,2,1,0,4:T(8,128)(2,1)S(1)} %copy-done.2, bf16[4,1,640,1,128]{4,0,2,3,1:T(4,128)(2,1)S(1)} %get-tuple-element.11), kind=kOutput, calls=%fused_computation.2 | convolution fusion | flops 2262564864 | bytes 5373952 | tf_op jit(solution)/shard_map/conv_general_dilated | solution.py:48
  89.5 0.2 reverse_multiply_fusion
  89.6 2.0 %copy.35 = f32[3,3,3,128,128]{4,3,2,1,0:T(8,128)} copy(f32[3,3,3,128,128]{3,4,2,1,0:T(8,128)S(1)} %reverse_multiply_fusion) | data formatting | bytes 3538944 | tf_op jit(solution)/shard_map/mul | solution.py:58
  91.7 1.5 mul.29
  93.2 0.2 pad.4
  93.4 0.2 copy.36
  93.6 5.4 %all_to_all.20 = f32[2,64,32,128]{3,2,1,0:T(8,128)S(1)} all-to-all(f32[2,64,32,128]{3,2,1,0:T(8,128)S(1)} %bitcast.36), channel_id=1, replica_groups=mesh['y'=4,'z'=4,'x'=4,'core'=2] {'core'}, dimensions={0} | all-to-all | bytes 4194304 | tf_op jit(solution)/shard_map/all_to_all | solution.py:88
  99.0 1.2 reduce_sum.38
  100.3 0.0 copy-start.3
  100.3 21.8 %all_to_all.21 = f32[4,16,32,128]{3,2,1,0:T(8,128)S(1)} all-to-all(f32[4,16,32,128]{3,2,1,0:T(8,128)} %bitcast.38), channel_id=1, replica_groups=mesh['y'=4,'z'=4,'x'=4,'core'=2] {'x'}, dimensions={0} | all-to-all | bytes 2097152 | tf_op jit(solution)/shard_map/all_to_all | solution.py:88
  122.0 0.1 reduce_sum.39
  122.1 14.6 %all_to_all.22 = f32[4,4,32,128]{3,2,1,0:T(8,128)S(1)} all-to-all(f32[4,4,32,128]{3,2,1,0:T(8,128)S(1)} %bitcast.39), channel_id=1, replica_groups=mesh['y'=4,'z'=4,'x'=4,'core'=2] {'z'}, dimensions={0} | all-to-all | bytes 524288 | tf_op jit(solution)/shard_map/all_to_all | solution.py:88
  136.7 0.6 reduce_sum.40
  137.3 7.5 %all-to-all-start.3 = ((f32[4,1,32,128]{3,2,1,0:T(8,128)}), f32[4,1,32,128]{3,2,1,0:T(8,128)S(1)}, u32[]{:S(2)}, u32[]{:S(2)}) async-start(f32[4,1,32,128]{3,2,1,0:T(8,128)} %bitcast.12), calls=%async_computation.3 | async-start | bytes 131072 | tf_op jit(solution)/shard_map/all_to_all | solution.py:88
  144.8 0.0 copy-done.3
  144.8 0.9 copy.38
  145.7 4.7 %all-to-all-done.3 = f32[4,1,32,128]{3,2,1,0:T(8,128)S(1)} async-done(((f32[4,1,32,128]{3,2,1,0:T(8,128)}), f32[4,1,32,128]{3,2,1,0:T(8,128)S(1)}, u32[]{:S(2)}, u32[]{:S(2)}) %all-to-all-start.3) | async-done | bytes 65568 | tf_op jit(solution)/shard_map/all_to_all | solution.py:88
  150.5 0.6 slice_bitcast_fusion.1
  (3 shorter events, 0.1 us)
Async XLA Ops:
  0.6 43.4 %copy-start = (bf16[3,3,3,128,128]{4,3,2,1,0:T(8,128)(2,1)S(1)}, bf16[3,3,3,128,128]{4,3,2,1,0:T(8,128)(2,1)}, u32[]{:S(2)}) copy-start(bf16[3,3,3,128,128]{4,3,2,1,0:T(8,128)(2,1)} %param.6) | copy-start | bytes 2654212
  1.7 3.5 %collective-permute-start = (bf16[2,1,640,128]{3,2,1,0:T(8,128)(2,1)S(1)}, bf16[2,1,640,128]{3,2,1,0:T(8,128)(2,1)S(1)}, u32[]{:S(2)}, u32[]{:S(2)}) collective-permute-start(bf16[2,1,640,128]{3,2,1,0:T(8,128)(2,1)S(1)} %slice.9), channel_id=1, source_target_pairs={{1,0},{3,2},{5,4},{7,6},{9,8},{11,10},{13,12},{15,14},{17,16},{19,... | collective-permute-start | bytes 983048 | tf_op jit(solution)/shard_map/ppermute | solution.py:14
  5.3 25.7 %collective-permute-start.2 = (bf16[6,1,640,128]{3,2,1,0:T(8,128)(2,1)S(1)}, bf16[6,1,640,128]{3,2,1,0:T(8,128)(2,1)S(1)}, u32[]{:S(2)}, u32[]{:S(2)}) collective-permute-start(bf16[6,1,640,128]{3,2,1,0:T(8,128)(2,1)S(1)} %constant_dynamic-update-slice_fusion), channel_id=1, source_target_pairs={{2,0},{4,2},{6,4},{8,6},{10,8},{12,10},{14,12},{16,14},{18,16},{20... | collective-permute-start | bytes 2949128 | tf_op jit(solution)/shard_map/ppermute | solution.py:25
  6.6 25.6 %collective-permute-start.1 = (bf16[6,1,640,128]{3,2,1,0:T(8,128)(2,1)S(1)}, bf16[6,1,640,128]{3,2,1,0:T(8,128)(2,1)S(1)}, u32[]{:S(2)}, u32[]{:S(2)}) collective-permute-start(bf16[6,1,640,128]{3,2,1,0:T(8,128)(2,1)S(1)} %constant_dynamic-update-slice_fusion), channel_id=1, source_target_pairs={{0,2},{2,4},{4,6},{6,8},{8,10},{10,12},{12,14},{14,16},{16,18},{18... | collective-permute-start | bytes 2949128 | tf_op jit(solution)/shard_map/ppermute | solution.py:24
  41.6 2.4 %copy-start.5 = (pred[8,81]{0,1:T(8,128)(4,1)S(1)}, pred[8,81]{0,1:T(8,128)(4,1)}, u32[]{:S(2)}) copy-start(pred[8,81]{0,1:T(8,128)(4,1)} %constant.20) | copy-start | bytes 1948
  49.1 1.1 copy-start.1
  49.1 1.3 copy-start.4
  50.4 2.3 %copy-start.2 = (bf16[6,3,640,128,1]{3,2,1,0,4:T(8,128)(2,1)S(1)}, bf16[6,3,640,128,1]{3,2,1,0,4:T(8,128)(2,1)}, u32[]{:S(2)}) copy-start(bf16[6,3,640,128,1]{3,2,1,0,4:T(8,128)(2,1)} %get-tuple-element.9) | copy-start | bytes 8847364
  100.3 44.6 %copy-start.3 = (bf16[4,1,640,128]{3,0,2,1:T(4,128)(2,1)S(1)}, bf16[4,1,640,128]{3,0,2,1:T(4,128)(2,1)}, u32[]{:S(2)}) copy-start(bf16[4,1,640,128]{3,0,2,1:T(4,128)(2,1)} %get-tuple-element.12) | copy-start | bytes 1966084
  137.3 13.1 %all-to-all-start.3 = ((f32[4,1,32,128]{3,2,1,0:T(8,128)}), f32[4,1,32,128]{3,2,1,0:T(8,128)S(1)}, u32[]{:S(2)}, u32[]{:S(2)}) async-start(f32[4,1,32,128]{3,2,1,0:T(8,128)} %bitcast.12), calls=%async_computation.3 | async-start | bytes 131072 | tf_op jit(solution)/shard_map/all_to_all | solution.py:88

commit v7 on v6

--- a/solution.py
+++ b/solution.py
@@ -4,6 +4,8 @@
 from jax import lax
 from jax.sharding import Mesh, NamedSharding
 from jax.sharding import PartitionSpec as P
+from jax.experimental import pallas as pl
+from jax.experimental.pallas import tpu as pltpu
 
 PHYSICAL = ("y", "z", "x")
 
@@ -27,43 +29,79 @@
     return x
 
 
+def local_kernel(factor, cot_ref, kt_ref, a_ref, feat_ref, gf_ref, term_ref, z_ref):
+    frames, breadth, channels = feat_ref.shape
+    term_ref[...] = jnp.zeros_like(term_ref)
+    rows = lax.broadcasted_iota(jnp.int32, (breadth, channels), 0)
+    for t in range(frames):
+        for i in range(3):
+            for j in range(3):
+                slab = cot_ref[t + 2 - i, 2 - j]
+                part = jnp.dot(slab, kt_ref[i, j], preferred_element_type=jnp.float32)
+                if i == 0 and j == 0:
+                    z_ref[...] = part
+                else:
+                    z_ref[...] += part
+                term_ref[i * 3 + j] += jnp.dot(a_ref[t], slab, preferred_element_type=jnp.float32)
+        ahead = pltpu.roll(z_ref[:, 0:channels], breadth - 1, 0)
+        behind = pltpu.roll(z_ref[:, 2 * channels : 3 * channels], 1, 0)
+        grad_input = (
+            jnp.where(rows == breadth - 1, 0.0, ahead)
+            + z_ref[:, channels : 2 * channels]
+            + jnp.where(rows == 0, 0.0, behind)
+        )
+        values = feat_ref[t].astype(jnp.float32)
+        sigmoid_part = jax.nn.sigmoid(values)
+        derivative = sigmoid_part * (1.0 + values * (1.0 - sigmoid_part))
+        own = cot_ref[t, 1].astype(jnp.float32)
+        gf_ref[t] = (own + derivative * grad_input).astype(gf_ref.dtype)
+    term_ref[...] = term_ref[...] * factor
+
+
+def local_grads(cot_rows, kt, a, feat, factor):
+    frames, breadth, channels = feat.shape
+    vmem = pl.BlockSpec(memory_space=pltpu.VMEM)
+    flops = 2 * 2 * frames * 9 * breadth * channels * 3 * channels
+    moved = 2 * (cot_rows.size + kt.size + a.size + 2 * feat.size) + 4 * 9 * 3 * channels * channels
+    return pl.pallas_call(
+        lambda *refs: local_kernel(factor, *refs),
+        out_shape=(
+            jax.ShapeDtypeStruct((frames, breadth, channels), jnp.bfloat16),
+            jax.ShapeDtypeStruct((9, 3 * channels, channels), jnp.float32),
+        ),
+        in_specs=[vmem] * 4,
+        out_specs=(vmem, vmem),
+        scratch_shapes=[pltpu.VMEM((breadth, 3 * channels), jnp.float32)],
+        compiler_params=pltpu.CompilerParams(vmem_limit_bytes=48 * 1024 * 1024),
+        cost_estimate=pl.CostEstimate(flops=flops, bytes_accessed=moved, transcendentals=feat.size),
+    )(cot_rows, kt, a, feat)
+
+
+def local_inputs(features, cotangent, kernel, cot_rows):
+    frames, height, breadth, channels = features.shape
+    active = jax.nn.silu(features.astype(jnp.float32)).astype(jnp.bfloat16)
+    wide = jnp.pad(active[:, 0], ((0, 0), (1, 1), (0, 0)))
+    shifted = jnp.stack([wide[:, k : k + breadth] for k in range(3)], axis=1)
+    a = shifted.transpose(0, 1, 3, 2).reshape(frames, 3 * channels, breadth)
+    kt = kernel.transpose(0, 1, 4, 2, 3).reshape(3, 3, channels, 3 * channels)
+    return cot_rows[:, :, 0], kt, a, features[:, 0]
+
+
 def body(features, cotangent, kernel):
     frames, height, breadth, channels = features.shape
-    values = features.astype(jnp.float32)
-    active = jax.nn.silu(values).astype(jnp.bfloat16)
     future = passed_along(cotangent[:2], "ta", -1)
     cot_ext = jnp.concatenate([cotangent, future], axis=0)
     cot_rows = with_halo(cot_ext, (("ha", 1),), 1)
-    taps = kernel.shape[:3]
-    edges = ((0, 0), (0, 0), (1, 1))
-    flipped = jnp.flip(kernel, (0, 1, 2))
-    grad_input = lax.conv_general_dilated(
-        cot_rows[None],
-        flipped,
-        (1, 1, 1),
-        edges,
-        dimension_numbers=("NDHWC", "DHWOI", "NDHWC"),
-        preferred_element_type=jnp.float32,
-    )[0]
-    paired = lax.conv_general_dilated(
-        cot_rows[..., None],
-        active[:, :, :, None, :],
-        (1, 1, 1),
-        edges,
-        dimension_numbers=("DHWNC", "DHWIO", "DHWCN"),
-        preferred_element_type=jnp.float32,
-    )
     total_cells = frames * height * breadth * lax.axis_size("ha") * lax.axis_size("ta")
     factor = float(total_cells) ** (-0.5)
-    term = jnp.flip(paired, (0, 1, 2)).reshape(-1, channels) * factor
+    cot_in, kt, a, feat = local_inputs(features, cotangent, kernel, cot_rows[:, :, None])
+    grad_features, term = local_grads(cot_in, kt, a, feat, factor)
+    term = term.reshape(-1, channels)
     owners = lax.axis_size("ha") * lax.axis_size("ta")
     rows = term.shape[0] // owners
     padded = -(-rows // 8) * 8
     term = jnp.pad(term.reshape(owners, rows, channels), ((0, 0), (0, padded - rows), (0, 0)))
-    sigmoid_part = jax.nn.sigmoid(values)
-    derivative = sigmoid_part * (1.0 + values * (1.0 - sigmoid_part))
-    grad_features = (cotangent.astype(jnp.float32) + derivative * grad_input).astype(jnp.bfloat16)
-    return (grad_features, term[None])
+    return (grad_features[:, None], term[None])
 
 
 def physical_mesh(mesh):

time: 152 us -> 106 us (0.70)
  matrix products: 41.8 us -> 0 us
  Pallas kernels: 0 us -> 12 us
  waiting for transfers between devices: 26.7 us -> 17.6 us
  starting transfers between devices: 14.7 us -> 7.04 us
  blocking collectives: 41.8 us -> 48.4 us
  local copies, waits for them, and re-layouts: 19 us -> 13.1 us
    conv_general_dilated x2 -> x0, matrix products: 41.8 us -> none  [the longest x1 36.7 us: body(): lax.conv_general_dilated(cot_rows[..., None], active[:, :, :, None, :], (...]
    ppermute x1, waiting for transfers between devices: 19.8 us -> 5.06 us  [with_halo(): after = lax.ppermute(leading, axis, down)]
    pallas_call x0 -> x1, Pallas kernels: none -> 12 us  [local_grads(): pl.pallas_call(lambda *refs: local_kernel(factor, *refs), out_shape=(jax....]
    ppermute x1, waiting for transfers between devices: 1.18 us -> 12.3 us  [with_halo(): before = lax.ppermute(last, axis, up)]
    conv_general_dilated x4 -> x0, local copies, waits for them, and re-layouts: 7.92 us -> none  [body(): lax.conv_general_dilated(cot_rows[None], flipped, (1, 1, 1), edges, dimen...]
    all_to_all x1 -> x0, starting transfers between devices: 7.49 us -> none  [reduce_blocks(): part = lax.all_to_all(shaped, axis, 0, 0, tiled=True).sum(0)]
    all_to_all x3 -> x4, blocking collectives: 41.8 us -> 48.4 us  [reduce_blocks(): part = lax.all_to_all(shaped, axis, 0, 0, tiled=True).sum(0)]
    all_to_all x1 -> x0, waiting for transfers between devices: 4.7 us -> none  [reduce_blocks(): part = lax.all_to_all(shaped, axis, 0, 0, tiled=True).sum(0)]
  transfers between devices with their start and end apart: 4 -> 3, of which waited for: 4 -> 3; matrix products, arithmetic and copies ran while one was open for 1% -> 9% of each run, Pallas kernels for 0% -> 0%
where the time goes in v7:
time: 106 us; the launch traced here: 105 us
  blocking collectives  48.4 us (46%)
  waiting for transfers between devices  17.6 us (17%)
  local copies, waits for them, and re-layouts  13.1 us (12%)
  Pallas kernels  12 us (11%)
  starting transfers between devices  7.04 us (7%)
  other arithmetic  6.27 us (6%)
    all_to_all x4, blocking collectives, reduce_blocks(): part = lax.all_to_all(shaped, axis, 0, 0, tiled=True).sum(0)  48.4 us
    ppermute x1, waiting for transfers between devices, with_halo(): before = lax.ppermute(last, axis, up)  12.3 us
    pallas_call x1, Pallas kernels, local_grads(): pl.pallas_call(lambda *refs: local_kernel(factor, *refs), out_shape=(jax....  12 us
    ppermute x1, waiting for transfers between devices, with_halo(): after = lax.ppermute(leading, axis, down)  5.06 us
    ppermute x1, starting transfers between devices, with_halo(): before = lax.ppermute(last, axis, up)  4.47 us
    concatenate x1, other arithmetic, with_halo(): x = jnp.concatenate([before, x, after], axis=dim)  3.7 us
    unnamed x5, local copies, waits for them, and re-layouts  3.19 us
    transpose x1, local copies, waits for them, and re-layouts, local_inputs(): a = shifted.transpose(0, 1, 3, 2).reshape(frames, 3 * channels, breadth)  2.79 us
  transfers between devices with their start and end apart: 3, of which 3 were waited for; matrix products, arithmetic and copies ran while one was open for 9% of the time, Pallas kernels for 0%

profile of v7, /device:TPU:0, one launch (start us, length us, event | category | flops | bytes accessed | tf_op | source)
XLA Modules:
  0.0 105.2 jit_solution(1821255846106881591)
XLA Ops:
  0.6 0.0 copy-start
  0.6 1.1 %slice.16 = bf16[2,1,640,128]{3,2,1,0:T(8,128)(2,1)S(1)} slice(bf16[4,1,640,128]{3,2,1,0:T(8,128)(2,1)} %param.5), slice={[0:2], [0:1], [0:640], [0:128]} | slice | bytes 655360 | tf_op jit(solution)/shard_map/slice | solution.py:92
  1.7 1.3 %collective-permute-start = (bf16[2,1,640,128]{3,2,1,0:T(8,128)(2,1)S(1)}, bf16[2,1,640,128]{3,2,1,0:T(8,128)(2,1)S(1)}, u32[]{:S(2)}, u32[]{:S(2)}) collective-permute-start(bf16[2,1,640,128]{3,2,1,0:T(8,128)(2,1)S(1)} %slice.16), channel_id=1, source_target_pairs={{1,0},{3,2},{5,4},{7,6},{9,8},{11,10},{13,12},{15,14},{17,16},{19,... | collective-permute-start | bytes 983048 | tf_op jit(solution)/shard_map/ppermute | solution.py:16
  3.0 2.0 %constant_dynamic-update-slice_fusion.1 = bf16[6,1,640,128]{3,2,1,0:T(8,128)(2,1)} fusion(bf16[4,1,640,128]{3,2,1,0:T(8,128)(2,1)} %param.5), kind=kLoop, calls=%fused_computation.12 | loop fusion | bytes 1310720
  5.0 0.3 collective-permute-done
  5.2 0.7 constant_dynamic-update-slice_fusion
  6.0 4.5 %collective-permute-start.1 = (bf16[6,1,640,128]{3,2,1,0:T(8,128)(2,1)}, bf16[6,1,640,128]{3,2,1,0:T(8,128)(2,1)}, u32[]{:S(2)}, u32[]{:S(2)}) collective-permute-start(bf16[6,1,640,128]{3,2,1,0:T(8,128)(2,1)} %constant_dynamic-update-slice_fusion), channel_id=1, source_target_pairs={{0,2},{2,4},{4,6},{6,8},{8,10},{10,12},{12,14},{14,16},{16,18},{18... | collective-permute-start | bytes 2949128 | tf_op jit(solution)/shard_map/ppermute | solution.py:26
  10.4 1.3 %collective-permute-start.2 = (bf16[6,1,640,128]{3,2,1,0:T(8,128)(2,1)}, bf16[6,1,640,128]{3,2,1,0:T(8,128)(2,1)}, u32[]{:S(2)}, u32[]{:S(2)}) collective-permute-start(bf16[6,1,640,128]{3,2,1,0:T(8,128)(2,1)} %constant_dynamic-update-slice_fusion), channel_id=1, source_target_pairs={{2,0},{4,2},{6,4},{8,6},{10,8},{12,10},{14,12},{16,14},{18,16},{20... | collective-permute-start | bytes 2949128 | tf_op jit(solution)/shard_map/ppermute | solution.py:27
  11.7 0.0 copy-done
  11.7 0.4 fusion.4
  12.1 0.3 slice_bitcast_fusion.1
  12.4 0.4 fusion.3
  12.8 1.5 %maximum_bitcast_fusion = bf16[4,3,128,640]{2,3,1,0:T(8,128)(2,1)} fusion(bf16[4,1,640,128]{3,2,1,0:T(8,128)(2,1)S(1)} %get-tuple-element.16, bf16[4,1,640,128]{3,2,1,0:T(8,128)(2,1)S(1)} %fusion.3, bf16[4,1,640,128]{3,2,1,0:T(8,128)(2,1)S(1)} %get-tuple-element.15), kind=kLoop, calls=%fused_computation.1 | loop fusion | flops 1966080 | bytes 3932160 | tf_op jit(solution)/shard_map/transpose | solution.py:85
  14.3 2.8 %copy.22 = bf16[4,3,128,640]{3,2,1,0:T(8,128)(2,1)S(1)} copy(bf16[4,3,128,640]{2,3,1,0:T(8,128)(2,1)} %maximum_bitcast_fusion) | data formatting | bytes 3932160 | tf_op jit(solution)/shard_map/transpose | solution.py:85
  17.1 2.5 %copy.23.refs_1_ = bf16[3,3,128,384]{3,2,1,0:T(8,128)(2,1)S(1)} copy(bf16[3,3,128,384]{2,3,1,0:T(8,128)(2,1)} %bitcast.36) | data formatting | bytes 1769472 | tf_op jit(solution)/shard_map/reshape | solution.py:86
  19.5 12.3 %collective-permute-done.1 = bf16[6,1,640,128]{3,2,1,0:T(8,128)(2,1)} collective-permute-done((bf16[6,1,640,128]{3,2,1,0:T(8,128)(2,1)}, bf16[6,1,640,128]{3,2,1,0:T(8,128)(2,1)}, u32[]{:S(2)}, u32[]{:S(2)}) %collective-permute-start.1) | collective-permute-done | bytes 983072 | tf_op jit(solution)/shard_map/ppermute | solution.py:26
  31.9 5.1 %collective-permute-done.2 = bf16[6,1,640,128]{3,2,1,0:T(8,128)(2,1)} collective-permute-done((bf16[6,1,640,128]{3,2,1,0:T(8,128)(2,1)}, bf16[6,1,640,128]{3,2,1,0:T(8,128)(2,1)}, u32[]{:S(2)}, u32[]{:S(2)}) %collective-permute-start.2) | collective-permute-done | bytes 983072 | tf_op jit(solution)/shard_map/ppermute | solution.py:27
  36.9 3.7 %pad_maximum_fusion.refs_0_ = bf16[6,3,640,128]{3,2,1,0:T(8,128)(2,1)} fusion(bf16[6,1,640,128]{3,2,1,0:T(8,128)(2,1)} %collective-permute-done.2, bf16[6,1,640,128]{3,2,1,0:T(8,128)(2,1)} %constant_dynamic-update-slice_fusion, bf16[6,1,640,128]{3,2,1,0:T(8,128)(2,1)} %collective-permute-done.1), kind=kLoop, calls=%fused_computation | loop fusion | flops 2949120 | bytes 5898240 | tf_op jit(solution)/shard_map/concatenate | solution.py:28
  40.6 12.0 %shard_map.67 = (bf16[4,640,128]{2,1,0:T(8,128)(2,1)}, f32[9,384,128]{2,1,0:T(8,128)S(1)}) custom-call(bf16[6,3,640,128]{3,2,1,0:T(8,128)(2,1)} %pad_maximum_fusion.refs_0_, bf16[3,3,128,384]{3,2,1,0:T(8,128)(2,1)S(1)} %copy.23.refs_1_, bf16[4,384,640]{2,1,0:T(8,128)(2,1)S(1)} %bitcast.31, bf16[4,640,128]{2,1,0:T(8,128)(2,1)S(1)} %bitcast.30), custom_call_target="tpu_custom_call" | custom-call | flops 4529848320 | bytes 8880128 | tf_op jit(solution)/shard_map/pallas_call | solution.py:66
  52.6 0.0 copy-start.1
  52.6 1.2 %copy-done.1 = f32[9,384,128]{2,1,0:T(8,128)} copy-done((f32[9,384,128]{2,1,0:T(8,128)}, f32[9,384,128]{2,1,0:T(8,128)S(1)}, u32[]{:S(2)}) %copy-start.1) | copy-done | bytes 1769496
  53.8 1.5 %reshape_reshape.3 = f32[128,27,128]{2,1,0:T(8,128)S(1)} reshape(f32[9,384,128]{2,1,0:T(8,128)} %copy-done.1) | data formatting | bytes 3538944 | tf_op jit(solution)/shard_map/reshape;reshape | solution.py:103
  55.3 0.2 pad.9
  55.5 0.2 copy.24
  55.8 5.4 %all_to_all.20 = f32[2,64,32,128]{3,2,1,0:T(8,128)S(1)} all-to-all(f32[2,64,32,128]{3,2,1,0:T(8,128)S(1)} %bitcast.33), channel_id=1, replica_groups=mesh['y'=4,'z'=4,'x'=4,'core'=2] {'core'}, dimensions={0} | all-to-all | bytes 4194304 | tf_op jit(solution)/shard_map/all_to_all | solution.py:126
  61.2 0.3 reduce_sum.38
  61.5 20.7 %all_to_all.21 = f32[4,16,32,128]{3,2,1,0:T(8,128)S(1)} all-to-all(f32[4,16,32,128]{3,2,1,0:T(8,128)S(1)} %bitcast.34), channel_id=1, replica_groups=mesh['y'=4,'z'=4,'x'=4,'core'=2] {'x'}, dimensions={0} | all-to-all | bytes 2097152 | tf_op jit(solution)/shard_map/all_to_all | solution.py:126
  82.2 0.1 reduce_sum.39
  82.3 12.4 %all_to_all.22 = f32[4,4,32,128]{3,2,1,0:T(8,128)S(1)} all-to-all(f32[4,4,32,128]{3,2,1,0:T(8,128)S(1)} %bitcast.35), channel_id=1, replica_groups=mesh['y'=4,'z'=4,'x'=4,'core'=2] {'z'}, dimensions={0} | all-to-all | bytes 524288 | tf_op jit(solution)/shard_map/all_to_all | solution.py:126
  94.7 9.9 %all_to_all.23 = f32[4,1,32,128]{3,2,1,0:T(8,128)S(1)} all-to-all(f32[4,1,32,128]{3,2,1,0:T(8,128)S(1)} %bitcast.37), channel_id=1, replica_groups=mesh['y'=4,'z'=4,'x'=4,'core'=2] {'y'}, dimensions={0} | all-to-all | bytes 131072 | tf_op jit(solution)/shard_map/all_to_all | solution.py:126
  104.6 0.6 slice_bitcast_fusion.2
  (2 shorter events, 0.0 us)
Async XLA Ops:
  0.6 11.1 %copy-start = (bf16[4,1,640,128]{3,2,1,0:T(8,128)(2,1)S(1)}, bf16[4,1,640,128]{3,2,1,0:T(8,128)(2,1)}, u32[]{:S(2)}) copy-start(bf16[4,1,640,128]{3,2,1,0:T(8,128)(2,1)} %param.4) | copy-start | bytes 1966084
  1.7 3.5 %collective-permute-start = (bf16[2,1,640,128]{3,2,1,0:T(8,128)(2,1)S(1)}, bf16[2,1,640,128]{3,2,1,0:T(8,128)(2,1)S(1)}, u32[]{:S(2)}, u32[]{:S(2)}) collective-permute-start(bf16[2,1,640,128]{3,2,1,0:T(8,128)(2,1)S(1)} %slice.16), channel_id=1, source_target_pairs={{1,0},{3,2},{5,4},{7,6},{9,8},{11,10},{13,12},{15,14},{17,16},{19,... | collective-permute-start | bytes 983048 | tf_op jit(solution)/shard_map/ppermute | solution.py:16
  6.0 25.9 %collective-permute-start.1 = (bf16[6,1,640,128]{3,2,1,0:T(8,128)(2,1)}, bf16[6,1,640,128]{3,2,1,0:T(8,128)(2,1)}, u32[]{:S(2)}, u32[]{:S(2)}) collective-permute-start(bf16[6,1,640,128]{3,2,1,0:T(8,128)(2,1)} %constant_dynamic-update-slice_fusion), channel_id=1, source_target_pairs={{0,2},{2,4},{4,6},{6,8},{8,10},{10,12},{12,14},{14,16},{16,18},{18... | collective-permute-start | bytes 2949128 | tf_op jit(solution)/shard_map/ppermute | solution.py:26
  10.4 26.5 %collective-permute-start.2 = (bf16[6,1,640,128]{3,2,1,0:T(8,128)(2,1)}, bf16[6,1,640,128]{3,2,1,0:T(8,128)(2,1)}, u32[]{:S(2)}, u32[]{:S(2)}) collective-permute-start(bf16[6,1,640,128]{3,2,1,0:T(8,128)(2,1)} %constant_dynamic-update-slice_fusion), channel_id=1, source_target_pairs={{2,0},{4,2},{6,4},{8,6},{10,8},{12,10},{14,12},{16,14},{18,16},{20... | collective-permute-start | bytes 2949128 | tf_op jit(solution)/shard_map/ppermute | solution.py:27
  52.6 1.2 %copy-start.1 = (f32[9,384,128]{2,1,0:T(8,128)}, f32[9,384,128]{2,1,0:T(8,128)S(1)}, u32[]{:S(2)}) copy-start(f32[9,384,128]{2,1,0:T(8,128)S(1)} %get-tuple-element.6) | copy-start | bytes 5308420

commit v8 on v7

--- a/solution.py
+++ b/solution.py
@@ -137,7 +137,8 @@
         check_vma=False,
     )
     grid = physical_mesh(mesh)
-    order = ("core", "x", "z", "y")
+    order = ("core", "y", "z", "x")
+    stages = ("core", PHYSICAL)
     names = PHYSICAL + ("core",)
     sizes = [grid.shape[a] for a in names]
 
@@ -162,7 +163,7 @@
         term = reorder(term)
         spec = P(names)
         part = jax.shard_map(
-            lambda t: reduce_blocks(t, order)[:rows],
+            lambda t: reduce_blocks(t, stages)[:rows],
             mesh=grid,
             in_specs=spec,
             out_specs=P(names),

time: 106 us -> 96.2 us (0.908)
  blocking collectives: 48.4 us -> 37.9 us
    all_to_all x4 -> x2, blocking collectives: 48.4 us -> 37.9 us  [reduce_blocks(): part = lax.all_to_all(shaped, axis, 0, 0, tiled=True).sum(0)]
  transfers between devices with their start and end apart: 3 -> 3, of which waited for: 3 -> 3; matrix products, arithmetic and copies ran while one was open for 9% -> 10% of each run, Pallas kernels for 0% -> 0%
where the time goes in v8:
time: 96.2 us; the launch traced here: 95.6 us
  blocking collectives  37.9 us (39%)
  waiting for transfers between devices  17.6 us (18%)
  local copies, waits for them, and re-layouts  13.1 us (14%)
  Pallas kernels  12 us (12%)
  other arithmetic  7.24 us (8%)
  starting transfers between devices  7.03 us (7%)
    all_to_all x2, blocking collectives, reduce_blocks(): part = lax.all_to_all(shaped, axis, 0, 0, tiled=True).sum(0)  37.9 us
    ppermute x1, waiting for transfers between devices, with_halo(): before = lax.ppermute(last, axis, up)  12.3 us
    pallas_call x1, Pallas kernels, local_grads(): pl.pallas_call(lambda *refs: local_kernel(factor, *refs), out_shape=(jax....  12 us
    ppermute x1, waiting for transfers between devices, with_halo(): after = lax.ppermute(leading, axis, down)  5.05 us
    ppermute x1, starting transfers between devices, with_halo(): before = lax.ppermute(last, axis, up)  4.45 us
    concatenate x1, other arithmetic, with_halo(): x = jnp.concatenate([before, x, after], axis=dim)  3.7 us
    unnamed x5, local copies, waits for them, and re-layouts  3.2 us
    transpose x1, local copies, waits for them, and re-layouts, local_inputs(): a = shifted.transpose(0, 1, 3, 2).reshape(frames, 3 * channels, breadth)  2.79 us
  transfers between devices with their start and end apart: 3, of which 3 were waited for; matrix products, arithmetic and copies ran while one was open for 10% of the time, Pallas kernels for 0%

profile of v8, /device:TPU:0, one launch (start us, length us, event | category | flops | bytes accessed | tf_op | source)
XLA Modules:
  0.0 95.6 jit_solution(17463599238945409265)
XLA Ops:
  0.6 0.0 copy-start
  0.6 1.1 %slice.16 = bf16[2,1,640,128]{3,2,1,0:T(8,128)(2,1)S(1)} slice(bf16[4,1,640,128]{3,2,1,0:T(8,128)(2,1)} %param.5), slice={[0:2], [0:1], [0:640], [0:128]} | slice | bytes 655360 | tf_op jit(solution)/shard_map/slice | solution.py:92
  1.7 1.3 %collective-permute-start = (bf16[2,1,640,128]{3,2,1,0:T(8,128)(2,1)S(1)}, bf16[2,1,640,128]{3,2,1,0:T(8,128)(2,1)S(1)}, u32[]{:S(2)}, u32[]{:S(2)}) collective-permute-start(bf16[2,1,640,128]{3,2,1,0:T(8,128)(2,1)S(1)} %slice.16), channel_id=1, source_target_pairs={{1,0},{3,2},{5,4},{7,6},{9,8},{11,10},{13,12},{15,14},{17,16},{19,... | collective-permute-start | bytes 983048 | tf_op jit(solution)/shard_map/ppermute | solution.py:16
  3.0 2.0 %constant_dynamic-update-slice_fusion.1 = bf16[6,1,640,128]{3,2,1,0:T(8,128)(2,1)} fusion(bf16[4,1,640,128]{3,2,1,0:T(8,128)(2,1)} %param.5), kind=kLoop, calls=%fused_computation.12 | loop fusion | bytes 1310720
  5.0 0.3 collective-permute-done
  5.2 0.7 constant_dynamic-update-slice_fusion
  6.0 4.5 %collective-permute-start.1 = (bf16[6,1,640,128]{3,2,1,0:T(8,128)(2,1)}, bf16[6,1,640,128]{3,2,1,0:T(8,128)(2,1)}, u32[]{:S(2)}, u32[]{:S(2)}) collective-permute-start(bf16[6,1,640,128]{3,2,1,0:T(8,128)(2,1)} %constant_dynamic-update-slice_fusion), channel_id=1, source_target_pairs={{0,2},{2,4},{4,6},{6,8},{8,10},{10,12},{12,14},{14,16},{16,18},{18... | collective-permute-start | bytes 2949128 | tf_op jit(solution)/shard_map/ppermute | solution.py:26
  10.4 1.3 %collective-permute-start.2 = (bf16[6,1,640,128]{3,2,1,0:T(8,128)(2,1)}, bf16[6,1,640,128]{3,2,1,0:T(8,128)(2,1)}, u32[]{:S(2)}, u32[]{:S(2)}) collective-permute-start(bf16[6,1,640,128]{3,2,1,0:T(8,128)(2,1)} %constant_dynamic-update-slice_fusion), channel_id=1, source_target_pairs={{2,0},{4,2},{6,4},{8,6},{10,8},{12,10},{14,12},{16,14},{18,16},{20... | collective-permute-start | bytes 2949128 | tf_op jit(solution)/shard_map/ppermute | solution.py:27
  11.7 0.0 copy-done
  11.7 0.4 fusion.4
  12.1 0.3 slice_bitcast_fusion.1
  12.4 0.4 fusion.3
  12.7 1.5 %maximum_bitcast_fusion = bf16[4,3,128,640]{2,3,1,0:T(8,128)(2,1)} fusion(bf16[4,1,640,128]{3,2,1,0:T(8,128)(2,1)S(1)} %get-tuple-element.14, bf16[4,1,640,128]{3,2,1,0:T(8,128)(2,1)S(1)} %fusion.3, bf16[4,1,640,128]{3,2,1,0:T(8,128)(2,1)S(1)} %get-tuple-element.13), kind=kLoop, calls=%fused_computation.1 | loop fusion | flops 1966080 | bytes 3932160 | tf_op jit(solution)/shard_map/transpose | solution.py:85
  14.2 2.8 %copy.16 = bf16[4,3,128,640]{3,2,1,0:T(8,128)(2,1)S(1)} copy(bf16[4,3,128,640]{2,3,1,0:T(8,128)(2,1)} %maximum_bitcast_fusion) | data formatting | bytes 3932160 | tf_op jit(solution)/shard_map/transpose | solution.py:85
  17.0 2.5 %copy.17.refs_1_ = bf16[3,3,128,384]{3,2,1,0:T(8,128)(2,1)S(1)} copy(bf16[3,3,128,384]{2,3,1,0:T(8,128)(2,1)} %bitcast.31) | data formatting | bytes 1769472 | tf_op jit(solution)/shard_map/reshape | solution.py:86
  19.5 12.3 %collective-permute-done.1 = bf16[6,1,640,128]{3,2,1,0:T(8,128)(2,1)} collective-permute-done((bf16[6,1,640,128]{3,2,1,0:T(8,128)(2,1)}, bf16[6,1,640,128]{3,2,1,0:T(8,128)(2,1)}, u32[]{:S(2)}, u32[]{:S(2)}) %collective-permute-start.1) | collective-permute-done | bytes 983072 | tf_op jit(solution)/shard_map/ppermute | solution.py:26
  31.8 5.1 %collective-permute-done.2 = bf16[6,1,640,128]{3,2,1,0:T(8,128)(2,1)} collective-permute-done((bf16[6,1,640,128]{3,2,1,0:T(8,128)(2,1)}, bf16[6,1,640,128]{3,2,1,0:T(8,128)(2,1)}, u32[]{:S(2)}, u32[]{:S(2)}) %collective-permute-start.2) | collective-permute-done | bytes 983072 | tf_op jit(solution)/shard_map/ppermute | solution.py:27
  36.9 3.7 %pad_maximum_fusion.refs_0_ = bf16[6,3,640,128]{3,2,1,0:T(8,128)(2,1)} fusion(bf16[6,1,640,128]{3,2,1,0:T(8,128)(2,1)} %collective-permute-done.2, bf16[6,1,640,128]{3,2,1,0:T(8,128)(2,1)} %constant_dynamic-update-slice_fusion, bf16[6,1,640,128]{3,2,1,0:T(8,128)(2,1)} %collective-permute-done.1), kind=kLoop, calls=%fused_computation | loop fusion | flops 2949120 | bytes 5898240 | tf_op jit(solution)/shard_map/concatenate | solution.py:28
  40.6 12.0 %shard_map.67 = (bf16[4,640,128]{2,1,0:T(8,128)(2,1)}, f32[9,384,128]{2,1,0:T(8,128)S(1)}) custom-call(bf16[6,3,640,128]{3,2,1,0:T(8,128)(2,1)} %pad_maximum_fusion.refs_0_, bf16[3,3,128,384]{3,2,1,0:T(8,128)(2,1)S(1)} %copy.17.refs_1_, bf16[4,384,640]{2,1,0:T(8,128)(2,1)S(1)} %bitcast.27, bf16[4,640,128]{2,1,0:T(8,128)(2,1)S(1)} %bitcast.26), custom_call_target="tpu_custom_call" | custom-call | flops 4529848320 | bytes 8880128 | tf_op jit(solution)/shard_map/pallas_call | solution.py:66
  52.6 0.0 copy-start.1
  52.6 1.2 %copy-done.1 = f32[9,384,128]{2,1,0:T(8,128)} copy-done((f32[9,384,128]{2,1,0:T(8,128)}, f32[9,384,128]{2,1,0:T(8,128)S(1)}, u32[]{:S(2)}) %copy-start.1) | copy-done | bytes 1769496
  53.8 1.5 %reshape_reshape.3 = f32[128,27,128]{2,1,0:T(8,128)S(1)} reshape(f32[9,384,128]{2,1,0:T(8,128)} %copy-done.1) | data formatting | bytes 3538944 | tf_op jit(solution)/shard_map/reshape;reshape | solution.py:103
  55.3 0.2 pad.9
  55.5 0.2 copy.18
  55.8 5.4 %all_to_all.10 = f32[2,64,32,128]{3,2,1,0:T(8,128)S(1)} all-to-all(f32[2,64,32,128]{3,2,1,0:T(8,128)S(1)} %bitcast.29), channel_id=1, replica_groups=mesh['y'=4,'z'=4,'x'=4,'core'=2] {'core'}, dimensions={0} | all-to-all | bytes 4194304 | tf_op jit(solution)/shard_map/all_to_all | solution.py:126
  61.2 1.2 %reduce_sum.20 = f32[64,32,128]{2,1,0:T(8,128)} reduce(f32[2,64,32,128]{3,2,1,0:T(8,128)S(1)} %all_to_all.10, f32[]{:T(128)} %constant.8.clone.1), dimensions={0}, to_apply=%region_0.2 | reduce | flops 262144 | bytes 3145732 | tf_op jit(solution)/shard_map/reduce_sum | solution.py:126
  62.4 32.5 %all_to_all.11 = f32[64,1,32,128]{3,2,1,0:T(8,128)S(1)} all-to-all(f32[64,1,32,128]{3,2,1,0:T(8,128)} %bitcast.30), channel_id=1, replica_groups=mesh['y'=4,'z'=4,'x'=4,'core'=2] {'y','z','x'}, dimensions={0} | all-to-all | bytes 2097152 | tf_op jit(solution)/shard_map/all_to_all | solution.py:126
  94.9 0.1 reduce_sum.21
  95.0 0.6 slice_bitcast_fusion.2
Async XLA Ops:
  0.6 11.1 %copy-start = (bf16[4,1,640,128]{3,2,1,0:T(8,128)(2,1)S(1)}, bf16[4,1,640,128]{3,2,1,0:T(8,128)(2,1)}, u32[]{:S(2)}) copy-start(bf16[4,1,640,128]{3,2,1,0:T(8,128)(2,1)} %param.4) | copy-start | bytes 1966084
  1.7 3.5 %collective-permute-start = (bf16[2,1,640,128]{3,2,1,0:T(8,128)(2,1)S(1)}, bf16[2,1,640,128]{3,2,1,0:T(8,128)(2,1)S(1)}, u32[]{:S(2)}, u32[]{:S(2)}) collective-permute-start(bf16[2,1,640,128]{3,2,1,0:T(8,128)(2,1)S(1)} %slice.16), channel_id=1, source_target_pairs={{1,0},{3,2},{5,4},{7,6},{9,8},{11,10},{13,12},{15,14},{17,16},{19,... | collective-permute-start | bytes 983048 | tf_op jit(solution)/shard_map/ppermute | solution.py:16
  6.0 25.9 %collective-permute-start.1 = (bf16[6,1,640,128]{3,2,1,0:T(8,128)(2,1)}, bf16[6,1,640,128]{3,2,1,0:T(8,128)(2,1)}, u32[]{:S(2)}, u32[]{:S(2)}) collective-permute-start(bf16[6,1,640,128]{3,2,1,0:T(8,128)(2,1)} %constant_dynamic-update-slice_fusion), channel_id=1, source_target_pairs={{0,2},{2,4},{4,6},{6,8},{8,10},{10,12},{12,14},{14,16},{16,18},{18... | collective-permute-start | bytes 2949128 | tf_op jit(solution)/shard_map/ppermute | solution.py:26
  10.4 26.5 %collective-permute-start.2 = (bf16[6,1,640,128]{3,2,1,0:T(8,128)(2,1)}, bf16[6,1,640,128]{3,2,1,0:T(8,128)(2,1)}, u32[]{:S(2)}, u32[]{:S(2)}) collective-permute-start(bf16[6,1,640,128]{3,2,1,0:T(8,128)(2,1)} %constant_dynamic-update-slice_fusion), channel_id=1, source_target_pairs={{2,0},{4,2},{6,4},{8,6},{10,8},{12,10},{14,12},{16,14},{18,16},{20... | collective-permute-start | bytes 2949128 | tf_op jit(solution)/shard_map/ppermute | solution.py:27
  52.6 1.2 %copy-start.1 = (f32[9,384,128]{2,1,0:T(8,128)}, f32[9,384,128]{2,1,0:T(8,128)S(1)}, u32[]{:S(2)}) copy-start(f32[9,384,128]{2,1,0:T(8,128)S(1)} %get-tuple-element.6) | copy-start | bytes 5308420

commit v9 on v8

--- a/solution.py
+++ b/solution.py
@@ -29,20 +29,28 @@
     return x
 
 
-def local_kernel(factor, cot_ref, kt_ref, a_ref, feat_ref, gf_ref, term_ref, z_ref):
+def local_kernel(factor, own_ref, fut_ref, up_ref, down_ref, fwd_ref, kt_ref, a_ref, feat_ref, gf_ref, term_ref, z_ref):
     frames, breadth, channels = feat_ref.shape
+
+    def slab(frame, row):
+        if frame < frames:
+            return (up_ref, own_ref, down_ref)[row][frame]
+        if row == 1:
+            return fut_ref[frame - frames]
+        return fwd_ref[row // 2, frame - frames]
+
     term_ref[...] = jnp.zeros_like(term_ref)
     rows = lax.broadcasted_iota(jnp.int32, (breadth, channels), 0)
     for t in range(frames):
         for i in range(3):
             for j in range(3):
-                slab = cot_ref[t + 2 - i, 2 - j]
-                part = jnp.dot(slab, kt_ref[i, j], preferred_element_type=jnp.float32)
+                piece = slab(t + 2 - i, 2 - j)
+                part = jnp.dot(piece, kt_ref[i, j], preferred_element_type=jnp.float32)
                 if i == 0 and j == 0:
                     z_ref[...] = part
                 else:
                     z_ref[...] += part
-                term_ref[i * 3 + j] += jnp.dot(a_ref[t], slab, preferred_element_type=jnp.float32)
+                term_ref[i * 3 + j] += jnp.dot(a_ref[t], piece, preferred_element_type=jnp.float32)
         ahead = pltpu.roll(z_ref[:, 0:channels], breadth - 1, 0)
         behind = pltpu.roll(z_ref[:, 2 * channels : 3 * channels], 1, 0)
         grad_input = (
@@ -53,49 +61,57 @@
         values = feat_ref[t].astype(jnp.float32)
         sigmoid_part = jax.nn.sigmoid(values)
         derivative = sigmoid_part * (1.0 + values * (1.0 - sigmoid_part))
-        own = cot_ref[t, 1].astype(jnp.float32)
-        gf_ref[t] = (own + derivative * grad_input).astype(gf_ref.dtype)
+        gf_ref[t] = (own_ref[t].astype(jnp.float32) + derivative * grad_input).astype(gf_ref.dtype)
     term_ref[...] = term_ref[...] * factor
 
 
-def local_grads(cot_rows, kt, a, feat, factor):
+def local_grads(pieces, kt, a, feat, factor):
     frames, breadth, channels = feat.shape
     vmem = pl.BlockSpec(memory_space=pltpu.VMEM)
+    operands = tuple(pieces) + (kt, a, feat)
     flops = 2 * 2 * frames * 9 * breadth * channels * 3 * channels
-    moved = 2 * (cot_rows.size + kt.size + a.size + 2 * feat.size) + 4 * 9 * 3 * channels * channels
+    moved = sum(2 * x.size for x in operands) + 2 * feat.size + 4 * 9 * 3 * channels * channels
     return pl.pallas_call(
         lambda *refs: local_kernel(factor, *refs),
         out_shape=(
             jax.ShapeDtypeStruct((frames, breadth, channels), jnp.bfloat16),
             jax.ShapeDtypeStruct((9, 3 * channels, channels), jnp.float32),
         ),
-        in_specs=[vmem] * 4,
+        in_specs=[vmem] * len(operands),
         out_specs=(vmem, vmem),
         scratch_shapes=[pltpu.VMEM((breadth, 3 * channels), jnp.float32)],
         compiler_params=pltpu.CompilerParams(vmem_limit_bytes=48 * 1024 * 1024),
         cost_estimate=pl.CostEstimate(flops=flops, bytes_accessed=moved, transcendentals=feat.size),
-    )(cot_rows, kt, a, feat)
+    )(*operands)
 
 
-def local_inputs(features, cotangent, kernel, cot_rows):
+def local_inputs(features, kernel):
     frames, height, breadth, channels = features.shape
     active = jax.nn.silu(features.astype(jnp.float32)).astype(jnp.bfloat16)
     wide = jnp.pad(active[:, 0], ((0, 0), (1, 1), (0, 0)))
     shifted = jnp.stack([wide[:, k : k + breadth] for k in range(3)], axis=1)
     a = shifted.transpose(0, 1, 3, 2).reshape(frames, 3 * channels, breadth)
     kt = kernel.transpose(0, 1, 4, 2, 3).reshape(3, 3, channels, 3 * channels)
-    return cot_rows[:, :, 0], kt, a, features[:, 0]
+    return kt, a, features[:, 0]
+
+
+def row_neighbours(x, axis):
+    count = lax.axis_size(axis)
+    up = [(i, i + 1) for i in range(count - 1)]
+    down = [(j, i) for i, j in up]
+    return lax.ppermute(x, axis, up), lax.ppermute(x, axis, down)
 
 
 def body(features, cotangent, kernel):
     frames, height, breadth, channels = features.shape
-    future = passed_along(cotangent[:2], "ta", -1)
-    cot_ext = jnp.concatenate([cotangent, future], axis=0)
-    cot_rows = with_halo(cot_ext, (("ha", 1),), 1)
+    own = cotangent[:, 0]
+    future = passed_along(own[:2], "ta", -1)
+    above, below = row_neighbours(own, "ha")
+    forwarded = passed_along(jnp.stack([above[:2], below[:2]]), "ta", -1)
     total_cells = frames * height * breadth * lax.axis_size("ha") * lax.axis_size("ta")
     factor = float(total_cells) ** (-0.5)
-    cot_in, kt, a, feat = local_inputs(features, cotangent, kernel, cot_rows[:, :, None])
-    grad_features, term = local_grads(cot_in, kt, a, feat, factor)
+    kt, a, feat = local_inputs(features, kernel)
+    grad_features, term = local_grads((own, future, above, below, forwarded), kt, a, feat, factor)
     term = term.reshape(-1, channels)
     owners = lax.axis_size("ha") * lax.axis_size("ta")
     rows = term.shape[0] // owners

time: 96.2 us -> 90.1 us (0.937)
  waiting for transfers between devices: 17.6 us -> 10.6 us
  blocking collectives: 37.9 us -> 42.4 us
  other arithmetic: 7.24 us -> 3.43 us
  local copies, waits for them, and re-layouts: 13.1 us -> 11.2 us
  starting transfers between devices: 7.03 us -> 8.58 us
    ppermute x2, waiting for transfers between devices: 17.4 us -> 10.6 us  [row_neighbours(): return (lax.ppermute(x, axis, up), lax.ppermute(x, axis, down))]
    all_to_all x2, blocking collectives: 37.9 us -> 42.4 us  [reduce_blocks(): part = lax.all_to_all(shaped, axis, 0, 0, tiled=True).sum(0)]
    concatenate x1 -> x0, other arithmetic: 3.7 us -> none  [with_halo(): x = jnp.concatenate([before, x, after], axis=dim)]
    unnamed x5 -> x4, local copies, waits for them, and re-layouts: 3.2 us -> 0.01 us
    ppermute x1 -> x2, starting transfers between devices: 1.29 us -> 2.69 us  [passed_along(): return lax.ppermute(block, axis, route)]
    transpose x1, local copies, waits for them, and re-layouts: 2.79 us -> 4.02 us  [local_inputs(): a = shifted.transpose(0, 1, 3, 2).reshape(frames, 3 * channels, breadth)]
    reduce_sum x2, other arithmetic: 1.34 us -> 0.36 us  [reduce_blocks(): part = lax.all_to_all(shaped, axis, 0, 0, tiled=True).sum(0)]
  transfers between devices with their start and end apart: 3 -> 4, of which waited for: 3 -> 2; matrix products, arithmetic and copies ran while one was open for 10% -> 13% of each run, Pallas kernels for 0% -> 0%
where the time goes in v9:
time: 90.1 us; the launch traced here: 89.7 us
  blocking collectives  42.4 us (47%)
  Pallas kernels  12.6 us (14%)
  local copies, waits for them, and re-layouts  11.2 us (12%)
  waiting for transfers between devices  10.6 us (12%)
  starting transfers between devices  8.58 us (10%)
  other arithmetic  3.43 us (4%)
    all_to_all x2, blocking collectives, reduce_blocks(): part = lax.all_to_all(shaped, axis, 0, 0, tiled=True).sum(0)  42.4 us
    pallas_call x1, Pallas kernels, local_grads(): pl.pallas_call(lambda *refs: local_kernel(factor, *refs), out_shape=(jax....  12.6 us
    ppermute x2, waiting for transfers between devices, row_neighbours(): return (lax.ppermute(x, axis, up), lax.ppermute(x, axis, down))  10.6 us
    ppermute x2, starting transfers between devices, row_neighbours(): return (lax.ppermute(x, axis, up), lax.ppermute(x, axis, down))  5.88 us
    transpose x1, local copies, waits for them, and re-layouts, local_inputs(): a = shifted.transpose(0, 1, 3, 2).reshape(frames, 3 * channels, breadth)  4.02 us
    ppermute x2, starting transfers between devices, passed_along(): return lax.ppermute(block, axis, route)  2.69 us
    reshape x1, local copies, waits for them, and re-layouts, local_inputs(): kt = kernel.transpose(0, 1, 4, 2, 3).reshape(3, 3, channels, 3 * channels)  2.54 us
  transfers between devices with their start and end apart: 4, of which 2 were waited for; matrix products, arithmetic and copies ran while one was open for 13% of the time, Pallas kernels for 0%

profile of v9, /device:TPU:0, one launch (start us, length us, event | category | flops | bytes accessed | tf_op | source)
XLA Modules:
  0.0 89.7 jit_solution(15045013384088657382)
XLA Ops:
  0.6 1.3 %collective-permute-start.2 = (bf16[4,640,128]{2,1,0:T(8,128)(2,1)}, bf16[4,640,128]{2,1,0:T(8,128)(2,1)S(1)}, u32[]{:S(2)}, u32[]{:S(2)}) collective-permute-start(bf16[4,640,128]{2,1,0:T(8,128)(2,1)} %bitcast.35), channel_id=1, source_target_pairs={{2,0},{4,2},{6,4},{8,6},{10,8},{12,10},{14,12},{16,14},{18,16},{20... | collective-permute-start | bytes 1966088 | tf_op jit(solution)/shard_map/ppermute | solution.py:102
  1.9 4.6 %collective-permute-start.1 = (bf16[4,640,128]{2,1,0:T(8,128)(2,1)}, bf16[4,640,128]{2,1,0:T(8,128)(2,1)S(1)}, u32[]{:S(2)}, u32[]{:S(2)}) collective-permute-start(bf16[4,640,128]{2,1,0:T(8,128)(2,1)} %bitcast.36), channel_id=1, source_target_pairs={{0,2},{2,4},{4,6},{6,8},{8,10},{10,12},{12,14},{14,16},{16,18},{18... | collective-permute-start | bytes 1966088 | tf_op jit(solution)/shard_map/ppermute | solution.py:102
  6.5 1.7 %slice_bitcast_fusion.4 = bf16[2,640,128]{2,1,0:T(8,128)(2,1)} fusion(bf16[4,1,640,128]{3,2,0,1:T(8,128)(2,1)} %bitcast.37), kind=kLoop, calls=%fused_computation.12 | loop fusion | bytes 655360 | tf_op jit(solution)/shard_map/slice | solution.py:108
  8.3 0.0 copy-start
  8.3 1.4 %collective-permute-start = (bf16[2,640,128]{2,1,0:T(8,128)(2,1)}, bf16[2,640,128]{2,1,0:T(8,128)(2,1)}, u32[]{:S(2)}, u32[]{:S(2)}) collective-permute-start(bf16[2,640,128]{2,1,0:T(8,128)(2,1)} %slice_bitcast_fusion.4), channel_id=1, source_target_pairs={{1,0},{3,2},{5,4},{7,6},{9,8},{11,10},{13,12},{15,14},{17,16},{19,... | collective-permute-start | bytes 983048 | tf_op jit(solution)/shard_map/ppermute | solution.py:16
  9.7 9.4 %collective-permute-done.2.refs_3_ = bf16[4,640,128]{2,1,0:T(8,128)(2,1)S(1)} collective-permute-done((bf16[4,640,128]{2,1,0:T(8,128)(2,1)}, bf16[4,640,128]{2,1,0:T(8,128)(2,1)S(1)}, u32[]{:S(2)}, u32[]{:S(2)}) %collective-permute-start.2) | collective-permute-done | bytes 655392 | tf_op jit(solution)/shard_map/ppermute | solution.py:102
  19.1 1.3 %collective-permute-done.1.refs_2_ = bf16[4,640,128]{2,1,0:T(8,128)(2,1)S(1)} collective-permute-done((bf16[4,640,128]{2,1,0:T(8,128)(2,1)}, bf16[4,640,128]{2,1,0:T(8,128)(2,1)S(1)}, u32[]{:S(2)}, u32[]{:S(2)}) %collective-permute-start.1) | collective-permute-done | bytes 655392 | tf_op jit(solution)/shard_map/ppermute | solution.py:102
  20.4 0.9 pad_maximum_fusion
  21.3 1.3 %collective-permute-start.3 = (bf16[2,2,640,128]{3,2,1,0:T(8,128)(2,1)}, bf16[2,2,640,128]{3,2,1,0:T(8,128)(2,1)}, u32[]{:S(2)}, u32[]{:S(2)}) collective-permute-start(bf16[2,2,640,128]{3,2,1,0:T(8,128)(2,1)} %pad_maximum_fusion), channel_id=1, source_target_pairs={{1,0},{3,2},{5,4},{7,6},{9,8},{11,10},{13,12},{15,14},{17,16},{19,... | collective-permute-start | bytes 1966088 | tf_op jit(solution)/shard_map/ppermute | solution.py:16
  22.6 0.0 copy-done
  22.6 0.4 fusion.4
  22.9 0.4 fusion.3
  23.3 0.3 slice_bitcast_fusion.1
  23.6 1.5 %maximum_bitcast_fusion = bf16[4,3,128,640]{2,3,1,0:T(8,128)(2,1)} fusion(bf16[4,1,640,128]{3,2,1,0:T(8,128)(2,1)S(1)} %get-tuple-element.14, bf16[4,1,640,128]{3,2,1,0:T(8,128)(2,1)S(1)} %fusion.3, bf16[4,1,640,128]{3,2,1,0:T(8,128)(2,1)S(1)} %get-tuple-element.13), kind=kLoop, calls=%fused_computation | loop fusion | flops 1966080 | bytes 3932160 | tf_op jit(solution)/shard_map/transpose | solution.py:93
  25.1 4.0 %copy.19 = bf16[4,3,128,640]{3,2,1,0:T(8,128)(2,1)} copy(bf16[4,3,128,640]{2,3,1,0:T(8,128)(2,1)} %maximum_bitcast_fusion) | data formatting | bytes 3932160 | tf_op jit(solution)/shard_map/transpose | solution.py:93
  29.1 0.0 copy-start.1
  29.1 2.5 %copy.20.refs_5_ = bf16[3,3,128,384]{3,2,1,0:T(8,128)(2,1)S(1)} copy(bf16[3,3,128,384]{2,3,1,0:T(8,128)(2,1)} %bitcast.43) | data formatting | bytes 1769472 | tf_op jit(solution)/shard_map/reshape | solution.py:94
  31.7 0.0 collective-permute-done.refs_1_
  31.7 0.0 collective-permute-done.3.refs_4_
  31.7 0.0 copy-done.1
  31.7 12.6 %shard_map.67 = (bf16[4,640,128]{2,1,0:T(8,128)(2,1)}, f32[9,384,128]{2,1,0:T(8,128)}) custom-call(bf16[4,640,128]{2,1,0:T(8,128)(2,1)S(1)} %bitcast.38, bf16[2,640,128]{2,1,0:T(8,128)(2,1)} %collective-permute-done.refs_1_, bf16[4,640,128]{2,1,0:T(8,128)(2,1)S(1)} %collective-permute-done.1.refs_2_, ...), custom_call_target="tpu_custom_call" | custom-call | flops 4529848320 | bytes 8880128 | tf_op jit(solution)/shard_map/pallas_call | solution.py:74
  44.3 1.5 %reshape_reshape.3 = f32[128,27,128]{2,1,0:T(8,128)S(1)} reshape(f32[9,384,128]{2,1,0:T(8,128)} %get-tuple-element.6) | data formatting | bytes 3538944 | tf_op jit(solution)/shard_map/reshape;reshape | solution.py:119
  45.8 0.2 pad.9
  46.0 0.2 copy.21
  46.3 6.8 %all_to_all.10 = f32[2,64,32,128]{3,2,1,0:T(8,128)S(1)} all-to-all(f32[2,64,32,128]{3,2,1,0:T(8,128)S(1)} %bitcast.40), channel_id=1, replica_groups=mesh['y'=4,'z'=4,'x'=4,'core'=2] {'core'}, dimensions={0} | all-to-all | bytes 4194304 | tf_op jit(solution)/shard_map/all_to_all | solution.py:142
  53.1 0.3 reduce_sum.20
  53.4 35.6 %all_to_all.11 = f32[64,1,32,128]{3,2,1,0:T(8,128)S(1)} all-to-all(f32[64,1,32,128]{3,2,1,0:T(8,128)S(1)} %bitcast.41), channel_id=1, replica_groups=mesh['y'=4,'z'=4,'x'=4,'core'=2] {'y','z','x'}, dimensions={0} | all-to-all | bytes 2097152 | tf_op jit(solution)/shard_map/all_to_all | solution.py:142
  88.9 0.1 reduce_sum.21
  89.0 0.6 slice_bitcast_fusion.5
  (2 shorter events, 0.0 us)
Async XLA Ops:
  0.6 18.4 %collective-permute-start.2 = (bf16[4,640,128]{2,1,0:T(8,128)(2,1)}, bf16[4,640,128]{2,1,0:T(8,128)(2,1)S(1)}, u32[]{:S(2)}, u32[]{:S(2)}) collective-permute-start(bf16[4,640,128]{2,1,0:T(8,128)(2,1)} %bitcast.35), channel_id=1, source_target_pairs={{2,0},{4,2},{6,4},{8,6},{10,8},{12,10},{14,12},{16,14},{18,16},{20... | collective-permute-start | bytes 1966088 | tf_op jit(solution)/shard_map/ppermute | solution.py:102
  1.9 18.4 %collective-permute-start.1 = (bf16[4,640,128]{2,1,0:T(8,128)(2,1)}, bf16[4,640,128]{2,1,0:T(8,128)(2,1)S(1)}, u32[]{:S(2)}, u32[]{:S(2)}) collective-permute-start(bf16[4,640,128]{2,1,0:T(8,128)(2,1)} %bitcast.36), channel_id=1, source_target_pairs={{0,2},{2,4},{4,6},{6,8},{8,10},{10,12},{12,14},{14,16},{16,18},{18... | collective-permute-start | bytes 1966088 | tf_op jit(solution)/shard_map/ppermute | solution.py:102
  8.3 14.3 %copy-start = (bf16[4,1,640,128]{3,2,1,0:T(8,128)(2,1)S(1)}, bf16[4,1,640,128]{3,2,1,0:T(8,128)(2,1)}, u32[]{:S(2)}) copy-start(bf16[4,1,640,128]{3,2,1,0:T(8,128)(2,1)} %param.4) | copy-start | bytes 1966084
  8.3 23.4 %collective-permute-start = (bf16[2,640,128]{2,1,0:T(8,128)(2,1)}, bf16[2,640,128]{2,1,0:T(8,128)(2,1)}, u32[]{:S(2)}, u32[]{:S(2)}) collective-permute-start(bf16[2,640,128]{2,1,0:T(8,128)(2,1)} %slice_bitcast_fusion.4), channel_id=1, source_target_pairs={{1,0},{3,2},{5,4},{7,6},{9,8},{11,10},{13,12},{15,14},{17,16},{19,... | collective-permute-start | bytes 983048 | tf_op jit(solution)/shard_map/ppermute | solution.py:16
  21.3 10.4 %collective-permute-start.3 = (bf16[2,2,640,128]{3,2,1,0:T(8,128)(2,1)}, bf16[2,2,640,128]{3,2,1,0:T(8,128)(2,1)}, u32[]{:S(2)}, u32[]{:S(2)}) collective-permute-start(bf16[2,2,640,128]{3,2,1,0:T(8,128)(2,1)} %pad_maximum_fusion), channel_id=1, source_target_pairs={{1,0},{3,2},{5,4},{7,6},{9,8},{11,10},{13,12},{15,14},{17,16},{19,... | collective-permute-start | bytes 1966088 | tf_op jit(solution)/shard_map/ppermute | solution.py:16
  29.1 2.6 %copy-start.1 = (bf16[4,1,640,128]{3,2,1,0:T(8,128)(2,1)S(1)}, bf16[4,1,640,128]{3,2,1,0:T(8,128)(2,1)}, u32[]{:S(2)}) copy-start(bf16[4,1,640,128]{3,2,1,0:T(8,128)(2,1)} %param.5) | copy-start | bytes 1966084

commit v10 on v9

--- a/solution.py
+++ b/solution.py
@@ -29,7 +29,7 @@
     return x
 
 
-def local_kernel(factor, own_ref, fut_ref, up_ref, down_ref, fwd_ref, kt_ref, a_ref, feat_ref, gf_ref, term_ref, z_ref):
+def local_kernel(factor, own_ref, fut_ref, up_ref, down_ref, fwd_ref, k_ref, feat_ref, gf_ref, term_ref, z_ref, a_ref):
     frames, breadth, channels = feat_ref.shape
 
     def slab(frame, row):
@@ -39,17 +39,34 @@
             return fut_ref[frame - frames]
         return fwd_ref[row // 2, frame - frames]
 
+    lanes = lax.broadcasted_iota(jnp.int32, (channels, breadth), 1)
+    for t in range(frames):
+        values = feat_ref[t].astype(jnp.float32)
+        active = (values * jax.nn.sigmoid(values)).astype(jnp.bfloat16).astype(jnp.float32)
+        turned = active.T
+        a_ref[t, 0:channels] = jnp.where(lanes == 0, 0.0, pltpu.roll(turned, 1, 1)).astype(a_ref.dtype)
+        a_ref[t, channels : 2 * channels] = turned.astype(a_ref.dtype)
+        a_ref[t, 2 * channels : 3 * channels] = jnp.where(
+            lanes == breadth - 1, 0.0, pltpu.roll(turned, breadth - 1, 1)
+        ).astype(a_ref.dtype)
     term_ref[...] = jnp.zeros_like(term_ref)
     rows = lax.broadcasted_iota(jnp.int32, (breadth, channels), 0)
     for t in range(frames):
         for i in range(3):
             for j in range(3):
                 piece = slab(t + 2 - i, 2 - j)
-                part = jnp.dot(piece, kt_ref[i, j], preferred_element_type=jnp.float32)
-                if i == 0 and j == 0:
-                    z_ref[...] = part
-                else:
-                    z_ref[...] += part
+                for k in range(3):
+                    part = lax.dot_general(
+                        piece,
+                        k_ref[(i * 3 + j) * 3 + k],
+                        (((1,), (1,)), ((), ())),
+                        preferred_element_type=jnp.float32,
+                    )
+                    window = slice(k * channels, (k + 1) * channels)
+                    if i == 0 and j == 0:
+                        z_ref[:, window] = part
+                    else:
+                        z_ref[:, window] += part
                 term_ref[i * 3 + j] += jnp.dot(a_ref[t], piece, preferred_element_type=jnp.float32)
         ahead = pltpu.roll(z_ref[:, 0:channels], breadth - 1, 0)
         behind = pltpu.roll(z_ref[:, 2 * channels : 3 * channels], 1, 0)
@@ -65,10 +82,10 @@
     term_ref[...] = term_ref[...] * factor
 
 
-def local_grads(pieces, kt, a, feat, factor):
+def local_grads(pieces, weights, feat, factor):
     frames, breadth, channels = feat.shape
     vmem = pl.BlockSpec(memory_space=pltpu.VMEM)
-    operands = tuple(pieces) + (kt, a, feat)
+    operands = tuple(pieces) + (weights, feat)
     flops = 2 * 2 * frames * 9 * breadth * channels * 3 * channels
     moved = sum(2 * x.size for x in operands) + 2 * feat.size + 4 * 9 * 3 * channels * channels
     return pl.pallas_call(
@@ -79,20 +96,13 @@
         ),
         in_specs=[vmem] * len(operands),
         out_specs=(vmem, vmem),
-        scratch_shapes=[pltpu.VMEM((breadth, 3 * channels), jnp.float32)],
+        scratch_shapes=[
+            pltpu.VMEM((breadth, 3 * channels), jnp.float32),
+            pltpu.VMEM((frames, 3 * channels, breadth), jnp.bfloat16),
+        ],
         compiler_params=pltpu.CompilerParams(vmem_limit_bytes=48 * 1024 * 1024),
-        cost_estimate=pl.CostEstimate(flops=flops, bytes_accessed=moved, transcendentals=feat.size),
+        cost_estimate=pl.CostEstimate(flops=flops, bytes_accessed=moved, transcendentals=2 * feat.size),
     )(*operands)
-
-
-def local_inputs(features, kernel):
-    frames, height, breadth, channels = features.shape
-    active = jax.nn.silu(features.astype(jnp.float32)).astype(jnp.bfloat16)
-    wide = jnp.pad(active[:, 0], ((0, 0), (1, 1), (0, 0)))
-    shifted = jnp.stack([wide[:, k : k + breadth] for k in range(3)], axis=1)
-    a = shifted.transpose(0, 1, 3, 2).reshape(frames, 3 * channels, breadth)
-    kt = kernel.transpose(0, 1, 4, 2, 3).reshape(3, 3, channels, 3 * channels)
-    return kt, a, features[:, 0]
 
 
 def row_neighbours(x, axis):
@@ -110,8 +120,8 @@
     forwarded = passed_along(jnp.stack([above[:2], below[:2]]), "ta", -1)
     total_cells = frames * height * breadth * lax.axis_size("ha") * lax.axis_size("ta")
     factor = float(total_cells) ** (-0.5)
-    kt, a, feat = local_inputs(features, kernel)
-    grad_features, term = local_grads((own, future, above, below, forwarded), kt, a, feat, factor)
+    weights = kernel.reshape(-1, channels, channels)
+    grad_features, term = local_grads((own, future, above, below, forwarded), weights, features[:, 0], factor)
     term = term.reshape(-1, channels)
     owners = lax.axis_size("ha") * lax.axis_size("ta")
     rows = term.shape[0] // owners

time: 90.1 us -> 80.7 us (0.90)
  local copies, waits for them, and re-layouts: 11.2 us -> 2.61 us
  waiting for transfers between devices: 10.6 us -> 16.1 us
  other arithmetic: 3.43 us -> 0.42 us
  Pallas kernels: 12.6 us -> 11 us
  blocking collectives: 42.4 us -> 41 us
    transpose x1 -> x0, local copies, waits for them, and re-layouts: 4.02 us -> none  [local_inputs(): a = shifted.transpose(0, 1, 3, 2).reshape(frames, 3 * channels, breadth)]
    ppermute x2, waiting for transfers between devices: 10.6 us -> 13.8 us  [row_neighbours(): return (lax.ppermute(x, axis, up), lax.ppermute(x, axis, down))]
    reshape x1 -> x0, local copies, waits for them, and re-layouts: 2.54 us -> none  [local_inputs(): kt = kernel.transpose(0, 1, 4, 2, 3).reshape(3, 3, channels, 3 * channels)]
    ppermute x2, waiting for transfers between devices: 0.01 us -> 2.26 us  [passed_along(): return lax.ppermute(block, axis, route)]
    slice x1, local copies, waits for them, and re-layouts: 1.75 us -> 0.02 us  [body(): future = passed_along(own[:2], 'ta', -1)]
    pallas_call x1, Pallas kernels: 12.6 us -> 11 us  [local_grads(): pl.pallas_call(lambda *refs: local_kernel(factor, *refs), out_shape=(jax....]
    transpose x1 -> x0, other arithmetic: 1.48 us -> none  [local_inputs(): a = shifted.transpose(0, 1, 3, 2).reshape(frames, 3 * channels, breadth)]
    all_to_all x2, blocking collectives: 42.4 us -> 41 us  [reduce_blocks(): part = lax.all_to_all(shaped, axis, 0, 0, tiled=True).sum(0)]
  transfers between devices with their start and end apart: 4 -> 4, of which waited for: 2 -> 3; matrix products, arithmetic and copies ran while one was open for 13% -> 0% of each run, Pallas kernels for 0% -> 0%
where the time goes in v10:
time: 80.7 us; the launch traced here: 80.4 us
  blocking collectives  41 us (51%)
  waiting for transfers between devices  16.1 us (20%)
  Pallas kernels  11 us (14%)
  starting transfers between devices  8.59 us (11%)
  local copies, waits for them, and re-layouts  2.61 us (3%)
    all_to_all x2, blocking collectives, reduce_blocks(): part = lax.all_to_all(shaped, axis, 0, 0, tiled=True).sum(0)  41 us
    ppermute x2, waiting for transfers between devices, row_neighbours(): return (lax.ppermute(x, axis, up), lax.ppermute(x, axis, down))  13.8 us
    pallas_call x1, Pallas kernels, local_grads(): pl.pallas_call(lambda *refs: local_kernel(factor, *refs), out_shape=(jax....  11 us
    ppermute x2, starting transfers between devices, row_neighbours(): return (lax.ppermute(x, axis, up), lax.ppermute(x, axis, down))  6.01 us
    ppermute x2, starting transfers between devices, passed_along(): return lax.ppermute(block, axis, route)  2.58 us
    ppermute x2, waiting for transfers between devices, passed_along(): return lax.ppermute(block, axis, route)  2.26 us
  transfers between devices with their start and end apart: 4, of which 3 were waited for; matrix products, arithmetic and copies ran while one was open for 0% of the time, Pallas kernels for 0%

profile of v10, /device:TPU:0, one launch (start us, length us, event | category | flops | bytes accessed | tf_op | source)
XLA Modules:
  0.0 80.4 jit_solution(2393662057868244666)
XLA Ops:
  0.6 0.0 copy-start
  0.6 0.0 copy-start.1
  0.6 0.0 copy-start.2
  0.7 1.4 %collective-permute-start.2 = (bf16[4,640,128]{2,1,0:T(8,128)(2,1)}, bf16[4,640,128]{2,1,0:T(8,128)(2,1)S(1)}, u32[]{:S(2)}, u32[]{:S(2)}) collective-permute-start(bf16[4,640,128]{2,1,0:T(8,128)(2,1)} %bitcast.21), channel_id=1, source_target_pairs={{2,0},{4,2},{6,4},{8,6},{10,8},{12,10},{14,12},{16,14},{18,16},{20... | collective-permute-start | bytes 1966088 | tf_op jit(solution)/shard_map/ppermute | solution.py:112
  2.1 4.6 %collective-permute-start.1 = (bf16[4,640,128]{2,1,0:T(8,128)(2,1)}, bf16[4,640,128]{2,1,0:T(8,128)(2,1)S(1)}, u32[]{:S(2)}, u32[]{:S(2)}) collective-permute-start(bf16[4,640,128]{2,1,0:T(8,128)(2,1)} %bitcast.22), channel_id=1, source_target_pairs={{0,2},{2,4},{4,6},{6,8},{8,10},{10,12},{12,14},{14,16},{16,18},{18... | collective-permute-start | bytes 1966088 | tf_op jit(solution)/shard_map/ppermute | solution.py:112
  6.7 12.6 %collective-permute-done.2.refs_3_ = bf16[4,640,128]{2,1,0:T(8,128)(2,1)S(1)} collective-permute-done((bf16[4,640,128]{2,1,0:T(8,128)(2,1)}, bf16[4,640,128]{2,1,0:T(8,128)(2,1)S(1)}, u32[]{:S(2)}, u32[]{:S(2)}) %collective-permute-start.2) | collective-permute-done | bytes 655392 | tf_op jit(solution)/shard_map/ppermute | solution.py:112
  19.3 1.3 %collective-permute-done.1.refs_2_ = bf16[4,640,128]{2,1,0:T(8,128)(2,1)S(1)} collective-permute-done((bf16[4,640,128]{2,1,0:T(8,128)(2,1)}, bf16[4,640,128]{2,1,0:T(8,128)(2,1)S(1)}, u32[]{:S(2)}, u32[]{:S(2)}) %collective-permute-start.1) | collective-permute-done | bytes 655392 | tf_op jit(solution)/shard_map/ppermute | solution.py:112
  20.5 0.1 pad_maximum_fusion
  20.6 1.3 %collective-permute-start.3 = (bf16[2,2,640,128]{3,2,1,0:T(8,128)(2,1)S(1)}, bf16[2,2,640,128]{3,2,1,0:T(8,128)(2,1)S(1)}, u32[]{:S(2)}, u32[]{:S(2)}) collective-permute-start(bf16[2,2,640,128]{3,2,1,0:T(8,128)(2,1)S(1)} %pad_maximum_fusion), channel_id=1, source_target_pairs={{1,0},{3,2},{5,4},{7,6},{9,8},{11,10},{13,12},{15,14},{17,16},{19,... | collective-permute-start | bytes 1966088 | tf_op jit(solution)/shard_map/ppermute | solution.py:16
  21.9 0.0 copy-done
  22.0 1.3 %collective-permute-start = (bf16[2,640,128]{2,1,0:T(8,128)(2,1)S(1)}, bf16[2,640,128]{2,1,0:T(8,128)(2,1)S(1)}, u32[]{:S(2)}, u32[]{:S(2)}) collective-permute-start(bf16[2,640,128]{2,1,0:T(8,128)(2,1)S(1)} %slice_bitcast_fusion.2), channel_id=1, source_target_pairs={{1,0},{3,2},{5,4},{7,6},{9,8},{11,10},{13,12},{15,14},{17,16},{19,... | collective-permute-start | bytes 983048 | tf_op jit(solution)/shard_map/ppermute | solution.py:16
  23.3 2.3 %collective-permute-done.refs_1_ = bf16[2,640,128]{2,1,0:T(8,128)(2,1)S(1)} collective-permute-done((bf16[2,640,128]{2,1,0:T(8,128)(2,1)S(1)}, bf16[2,640,128]{2,1,0:T(8,128)(2,1)S(1)}, u32[]{:S(2)}, u32[]{:S(2)}) %collective-permute-start) | collective-permute-done | bytes 327712 | tf_op jit(solution)/shard_map/ppermute | solution.py:16
  25.5 0.0 collective-permute-done.3.refs_4_
  25.5 0.0 copy-done.1
  25.5 0.0 copy-done.2
  25.5 11.0 %shard_map.67 = (bf16[4,640,128]{2,1,0:T(8,128)(2,1)}, f32[9,384,128]{2,1,0:T(8,128)}) custom-call(bf16[4,640,128]{2,1,0:T(8,128)(2,1)S(1)} %bitcast.24, bf16[2,640,128]{2,1,0:T(8,128)(2,1)S(1)} %collective-permute-done.refs_1_, bf16[4,640,128]{2,1,0:T(8,128)(2,1)S(1)} %collective-permute-done.1.refs_2_, ...), custom_call_target="tpu_custom_call" | custom-call | flops 4529848320 | bytes 6914048 | tf_op jit(solution)/shard_map/pallas_call | solution.py:91
  36.5 1.5 %reshape_reshape.3 = f32[128,27,128]{2,1,0:T(8,128)S(1)} reshape(f32[9,384,128]{2,1,0:T(8,128)} %get-tuple-element.6) | data formatting | bytes 3538944 | tf_op jit(solution)/shard_map/reshape;reshape | solution.py:129
  38.1 0.2 pad.4
  38.2 0.2 copy.12
  38.5 5.4 %all_to_all.10 = f32[2,64,32,128]{3,2,1,0:T(8,128)S(1)} all-to-all(f32[2,64,32,128]{3,2,1,0:T(8,128)S(1)} %bitcast.28), channel_id=1, replica_groups=mesh['y'=4,'z'=4,'x'=4,'core'=2] {'core'}, dimensions={0} | all-to-all | bytes 4194304 | tf_op jit(solution)/shard_map/all_to_all | solution.py:152
  43.9 0.3 reduce_sum.20
  44.2 35.6 %all_to_all.11 = f32[64,1,32,128]{3,2,1,0:T(8,128)S(1)} all-to-all(f32[64,1,32,128]{3,2,1,0:T(8,128)S(1)} %bitcast.29), channel_id=1, replica_groups=mesh['y'=4,'z'=4,'x'=4,'core'=2] {'y','z','x'}, dimensions={0} | all-to-all | bytes 2097152 | tf_op jit(solution)/shard_map/all_to_all | solution.py:152
  79.7 0.1 reduce_sum.21
  79.8 0.6 slice_bitcast_fusion.3
  (3 shorter events, 0.1 us)
Async XLA Ops:
  0.6 21.3 %copy-start = (bf16[4,1,640,128]{3,2,1,0:T(8,128)(2,1)S(1)}, bf16[4,1,640,128]{3,2,1,0:T(8,128)(2,1)}, u32[]{:S(2)}) copy-start(bf16[4,1,640,128]{3,2,1,0:T(8,128)(2,1)} %param.5) | copy-start | bytes 1966084
  0.6 24.9 %copy-start.1 = (bf16[3,3,3,128,128]{4,3,2,1,0:T(8,128)(2,1)S(1)}, bf16[3,3,3,128,128]{4,3,2,1,0:T(8,128)(2,1)}, u32[]{:S(2)}) copy-start(bf16[3,3,3,128,128]{4,3,2,1,0:T(8,128)(2,1)} %param.6) | copy-start | bytes 2654212
  0.6 24.9 %copy-start.2 = (bf16[4,1,640,128]{3,2,1,0:T(8,128)(2,1)S(1)}, bf16[4,1,640,128]{3,2,1,0:T(8,128)(2,1)}, u32[]{:S(2)}) copy-start(bf16[4,1,640,128]{3,2,1,0:T(8,128)(2,1)} %param.4) | copy-start | bytes 1966084
  0.7 18.6 %collective-permute-start.2 = (bf16[4,640,128]{2,1,0:T(8,128)(2,1)}, bf16[4,640,128]{2,1,0:T(8,128)(2,1)S(1)}, u32[]{:S(2)}, u32[]{:S(2)}) collective-permute-start(bf16[4,640,128]{2,1,0:T(8,128)(2,1)} %bitcast.21), channel_id=1, source_target_pairs={{2,0},{4,2},{6,4},{8,6},{10,8},{12,10},{14,12},{16,14},{18,16},{20... | collective-permute-start | bytes 1966088 | tf_op jit(solution)/shard_map/ppermute | solution.py:112
  2.1 18.4 %collective-permute-start.1 = (bf16[4,640,128]{2,1,0:T(8,128)(2,1)}, bf16[4,640,128]{2,1,0:T(8,128)(2,1)S(1)}, u32[]{:S(2)}, u32[]{:S(2)}) collective-permute-start(bf16[4,640,128]{2,1,0:T(8,128)(2,1)} %bitcast.22), channel_id=1, source_target_pairs={{0,2},{2,4},{4,6},{6,8},{8,10},{10,12},{12,14},{14,16},{16,18},{18... | collective-permute-start | bytes 1966088 | tf_op jit(solution)/shard_map/ppermute | solution.py:112
  20.6 4.9 %collective-permute-start.3 = (bf16[2,2,640,128]{3,2,1,0:T(8,128)(2,1)S(1)}, bf16[2,2,640,128]{3,2,1,0:T(8,128)(2,1)S(1)}, u32[]{:S(2)}, u32[]{:S(2)}) collective-permute-start(bf16[2,2,640,128]{3,2,1,0:T(8,128)(2,1)S(1)} %pad_maximum_fusion), channel_id=1, source_target_pairs={{1,0},{3,2},{5,4},{7,6},{9,8},{11,10},{13,12},{15,14},{17,16},{19,... | collective-permute-start | bytes 1966088 | tf_op jit(solution)/shard_map/ppermute | solution.py:16
  22.0 3.6 %collective-permute-start = (bf16[2,640,128]{2,1,0:T(8,128)(2,1)S(1)}, bf16[2,640,128]{2,1,0:T(8,128)(2,1)S(1)}, u32[]{:S(2)}, u32[]{:S(2)}) collective-permute-start(bf16[2,640,128]{2,1,0:T(8,128)(2,1)S(1)} %slice_bitcast_fusion.2), channel_id=1, source_target_pairs={{1,0},{3,2},{5,4},{7,6},{9,8},{11,10},{13,12},{15,14},{17,16},{19,... | collective-permute-start | bytes 983048 | tf_op jit(solution)/shard_map/ppermute | solution.py:16

commit v11 on v10

--- a/solution.py
+++ b/solution.py
@@ -29,15 +29,13 @@
     return x
 
 
-def local_kernel(factor, own_ref, fut_ref, up_ref, down_ref, fwd_ref, k_ref, feat_ref, gf_ref, term_ref, z_ref, a_ref):
+def local_kernel(factor, own_ref, up_ref, down_ref, bnd_ref, k_ref, feat_ref, gf_ref, term_ref, z_ref, a_ref):
     frames, breadth, channels = feat_ref.shape
 
     def slab(frame, row):
         if frame < frames:
             return (up_ref, own_ref, down_ref)[row][frame]
-        if row == 1:
-            return fut_ref[frame - frames]
-        return fwd_ref[row // 2, frame - frames]
+        return bnd_ref[row, frame - frames]
 
     lanes = lax.broadcasted_iota(jnp.int32, (channels, breadth), 1)
     for t in range(frames):
@@ -115,13 +113,12 @@
 def body(features, cotangent, kernel):
     frames, height, breadth, channels = features.shape
     own = cotangent[:, 0]
-    future = passed_along(own[:2], "ta", -1)
     above, below = row_neighbours(own, "ha")
-    forwarded = passed_along(jnp.stack([above[:2], below[:2]]), "ta", -1)
+    boundary = passed_along(jnp.stack([above[:2], own[:2], below[:2]]), "ta", -1)
     total_cells = frames * height * breadth * lax.axis_size("ha") * lax.axis_size("ta")
     factor = float(total_cells) ** (-0.5)
     weights = kernel.reshape(-1, channels, channels)
-    grad_features, term = local_grads((own, future, above, below, forwarded), weights, features[:, 0], factor)
+    grad_features, term = local_grads((own, above, below, boundary), weights, features[:, 0], factor)
     term = term.reshape(-1, channels)
     owners = lax.axis_size("ha") * lax.axis_size("ta")
     rows = term.shape[0] // owners

time: 80.7 us -> 80.4 us (level)
  starting transfers between devices: 8.59 us -> 7.3 us
  local copies, waits for them, and re-layouts: 2.61 us -> 3.6 us
    ppermute x2 -> x1, starting transfers between devices: 2.58 us -> 1.29 us  [passed_along(): return lax.ppermute(block, axis, route)]
    ppermute x2, waiting for transfers between devices: 13.8 us -> 12.8 us  [row_neighbours(): return (lax.ppermute(x, axis, up), lax.ppermute(x, axis, down))]
    another operation x2 -> x3, local copies, waits for them, and re-layouts: 0.04 us -> 1.05 us  [body(): jnp.stack([above[:2], own[:2], below[:2]])]
    ppermute x2 -> x1, waiting for transfers between devices: 2.26 us -> 3.16 us  [passed_along(): return lax.ppermute(block, axis, route)]
  transfers between devices with their start and end apart: 4 -> 3, of which waited for: 3 -> 3; matrix products, arithmetic and copies ran while one was open for 0% -> 1% of each run, Pallas kernels for 0% -> 0%
where the time goes in v11:
time: 80.4 us; the launch traced here: 80 us
  blocking collectives  41 us (51%)
  waiting for transfers between devices  16 us (20%)
  Pallas kernels  11 us (14%)
  starting transfers between devices  7.3 us (9%)
  local copies, waits for them, and re-layouts  3.6 us (4%)
    all_to_all x2, blocking collectives, reduce_blocks(): part = lax.all_to_all(shaped, axis, 0, 0, tiled=True).sum(0)  41 us
    ppermute x2, waiting for transfers between devices, row_neighbours(): return (lax.ppermute(x, axis, up), lax.ppermute(x, axis, down))  12.8 us
    pallas_call x1, Pallas kernels, local_grads(): pl.pallas_call(lambda *refs: local_kernel(factor, *refs), out_shape=(jax....  11 us
    ppermute x2, starting transfers between devices, row_neighbours(): return (lax.ppermute(x, axis, up), lax.ppermute(x, axis, down))  6.01 us
    ppermute x1, waiting for transfers between devices, passed_along(): return lax.ppermute(block, axis, route)  3.16 us
  transfers between devices with their start and end apart: 3, of which 3 were waited for; matrix products, arithmetic and copies ran while one was open for 1% of the time, Pallas kernels for 0%

profile of v11, /device:TPU:0, one launch (start us, length us, event | category | flops | bytes accessed | tf_op | source)
XLA Modules:
  0.0 80.0 jit_solution(11535799052575420298)
XLA Ops:
  0.6 0.0 copy-start
  0.6 0.0 copy-start.1
  0.6 0.0 copy-start.2
  0.7 1.4 %collective-permute-start.1 = (bf16[4,640,128]{2,1,0:T(8,128)(2,1)}, bf16[4,640,128]{2,1,0:T(8,128)(2,1)S(1)}, u32[]{:S(2)}, u32[]{:S(2)}) collective-permute-start(bf16[4,640,128]{2,1,0:T(8,128)(2,1)} %bitcast.21), channel_id=1, source_target_pairs={{2,0},{4,2},{6,4},{8,6},{10,8},{12,10},{14,12},{16,14},{18,16},{20... | collective-permute-start | bytes 1966088 | tf_op jit(solution)/shard_map/ppermute | solution.py:110
  2.1 4.6 %collective-permute-start = (bf16[4,640,128]{2,1,0:T(8,128)(2,1)}, bf16[4,640,128]{2,1,0:T(8,128)(2,1)S(1)}, u32[]{:S(2)}, u32[]{:S(2)}) collective-permute-start(bf16[4,640,128]{2,1,0:T(8,128)(2,1)} %bitcast.22), channel_id=1, source_target_pairs={{0,2},{2,4},{4,6},{6,8},{8,10},{10,12},{12,14},{14,16},{16,18},{18... | collective-permute-start | bytes 1966088 | tf_op jit(solution)/shard_map/ppermute | solution.py:110
  6.7 1.0 %slice_bitcast_fusion.1 = bf16[1,2,640,128]{3,2,1,0:T(8,128)(2,1)S(1)} fusion(bf16[4,1,640,128]{3,2,0,1:T(8,128)(2,1)} %bitcast.23), kind=kLoop, calls=%fused_computation.2 | loop fusion | bytes 655360 | tf_op jit(solution)/shard_map/stack | solution.py:117
  7.7 11.5 %collective-permute-done.1.refs_2_ = bf16[4,640,128]{2,1,0:T(8,128)(2,1)S(1)} collective-permute-done((bf16[4,640,128]{2,1,0:T(8,128)(2,1)}, bf16[4,640,128]{2,1,0:T(8,128)(2,1)S(1)}, u32[]{:S(2)}, u32[]{:S(2)}) %collective-permute-start.1) | collective-permute-done | bytes 655392 | tf_op jit(solution)/shard_map/ppermute | solution.py:110
  19.3 1.3 %collective-permute-done.refs_1_ = bf16[4,640,128]{2,1,0:T(8,128)(2,1)S(1)} collective-permute-done((bf16[4,640,128]{2,1,0:T(8,128)(2,1)}, bf16[4,640,128]{2,1,0:T(8,128)(2,1)S(1)}, u32[]{:S(2)}, u32[]{:S(2)}) %collective-permute-start) | collective-permute-done | bytes 655392 | tf_op jit(solution)/shard_map/ppermute | solution.py:110
  20.5 0.1 pad_maximum_fusion
  20.7 1.3 %collective-permute-start.2 = (bf16[3,2,640,128]{3,2,1,0:T(8,128)(2,1)S(1)}, bf16[3,2,640,128]{3,2,1,0:T(8,128)(2,1)S(1)}, u32[]{:S(2)}, u32[]{:S(2)}) collective-permute-start(bf16[3,2,640,128]{3,2,1,0:T(8,128)(2,1)S(1)} %pad_maximum_fusion), channel_id=1, source_target_pairs={{1,0},{3,2},{5,4},{7,6},{9,8},{11,10},{13,12},{15,14},{17,16},{19,... | collective-permute-start | bytes 2949128 | tf_op jit(solution)/shard_map/ppermute | solution.py:16
  22.0 3.2 %collective-permute-done.2.refs_3_ = bf16[3,2,640,128]{3,2,1,0:T(8,128)(2,1)S(1)} collective-permute-done((bf16[3,2,640,128]{3,2,1,0:T(8,128)(2,1)S(1)}, bf16[3,2,640,128]{3,2,1,0:T(8,128)(2,1)S(1)}, u32[]{:S(2)}, u32[]{:S(2)}) %collective-permute-start.2) | collective-permute-done | bytes 983072 | tf_op jit(solution)/shard_map/ppermute | solution.py:16
  25.1 0.0 copy-done
  25.1 0.0 copy-done.1
  25.1 0.0 copy-done.2
  25.1 11.0 %shard_map.67 = (bf16[4,640,128]{2,1,0:T(8,128)(2,1)}, f32[9,384,128]{2,1,0:T(8,128)}) custom-call(bf16[4,640,128]{2,1,0:T(8,128)(2,1)S(1)} %bitcast.24, bf16[4,640,128]{2,1,0:T(8,128)(2,1)S(1)} %collective-permute-done.refs_1_, bf16[4,640,128]{2,1,0:T(8,128)(2,1)S(1)} %collective-permute-done.1.refs_2_, ...), custom_call_target="tpu_custom_call" | custom-call | flops 4529848320 | bytes 6914048 | tf_op jit(solution)/shard_map/pallas_call | solution.py:89
  36.1 1.5 %reshape_reshape.3 = f32[128,27,128]{2,1,0:T(8,128)S(1)} reshape(f32[9,384,128]{2,1,0:T(8,128)} %get-tuple-element.6) | data formatting | bytes 3538944 | tf_op jit(solution)/shard_map/reshape;reshape | solution.py:126
  37.7 0.2 pad.4
  37.8 0.2 copy.12
  38.1 5.4 %all_to_all.10 = f32[2,64,32,128]{3,2,1,0:T(8,128)S(1)} all-to-all(f32[2,64,32,128]{3,2,1,0:T(8,128)S(1)} %bitcast.28), channel_id=1, replica_groups=mesh['y'=4,'z'=4,'x'=4,'core'=2] {'core'}, dimensions={0} | all-to-all | bytes 4194304 | tf_op jit(solution)/shard_map/all_to_all | solution.py:149
  43.5 0.3 reduce_sum.20
  43.8 35.6 %all_to_all.11 = f32[64,1,32,128]{3,2,1,0:T(8,128)S(1)} all-to-all(f32[64,1,32,128]{3,2,1,0:T(8,128)S(1)} %bitcast.29), channel_id=1, replica_groups=mesh['y'=4,'z'=4,'x'=4,'core'=2] {'y','z','x'}, dimensions={0} | all-to-all | bytes 2097152 | tf_op jit(solution)/shard_map/all_to_all | solution.py:149
  79.3 0.1 reduce_sum.21
  79.4 0.6 slice_bitcast_fusion.3
  (2 shorter events, 0.0 us)
Async XLA Ops:
  0.6 24.5 %copy-start = (bf16[4,1,640,128]{3,2,1,0:T(8,128)(2,1)S(1)}, bf16[4,1,640,128]{3,2,1,0:T(8,128)(2,1)}, u32[]{:S(2)}) copy-start(bf16[4,1,640,128]{3,2,1,0:T(8,128)(2,1)} %param.5) | copy-start | bytes 1966084
  0.6 24.5 %copy-start.1 = (bf16[3,3,3,128,128]{4,3,2,1,0:T(8,128)(2,1)S(1)}, bf16[3,3,3,128,128]{4,3,2,1,0:T(8,128)(2,1)}, u32[]{:S(2)}) copy-start(bf16[3,3,3,128,128]{4,3,2,1,0:T(8,128)(2,1)} %param.6) | copy-start | bytes 2654212
  0.6 24.5 %copy-start.2 = (bf16[4,1,640,128]{3,2,1,0:T(8,128)(2,1)S(1)}, bf16[4,1,640,128]{3,2,1,0:T(8,128)(2,1)}, u32[]{:S(2)}) copy-start(bf16[4,1,640,128]{3,2,1,0:T(8,128)(2,1)} %param.4) | copy-start | bytes 1966084
  0.7 18.6 %collective-permute-start.1 = (bf16[4,640,128]{2,1,0:T(8,128)(2,1)}, bf16[4,640,128]{2,1,0:T(8,128)(2,1)S(1)}, u32[]{:S(2)}, u32[]{:S(2)}) collective-permute-start(bf16[4,640,128]{2,1,0:T(8,128)(2,1)} %bitcast.21), channel_id=1, source_target_pairs={{2,0},{4,2},{6,4},{8,6},{10,8},{12,10},{14,12},{16,14},{18,16},{20... | collective-permute-start | bytes 1966088 | tf_op jit(solution)/shard_map/ppermute | solution.py:110
  2.1 18.4 %collective-permute-start = (bf16[4,640,128]{2,1,0:T(8,128)(2,1)}, bf16[4,640,128]{2,1,0:T(8,128)(2,1)S(1)}, u32[]{:S(2)}, u32[]{:S(2)}) collective-permute-start(bf16[4,640,128]{2,1,0:T(8,128)(2,1)} %bitcast.22), channel_id=1, source_target_pairs={{0,2},{2,4},{4,6},{6,8},{8,10},{10,12},{12,14},{14,16},{16,18},{18... | collective-permute-start | bytes 1966088 | tf_op jit(solution)/shard_map/ppermute | solution.py:110
  20.7 4.5 %collective-permute-start.2 = (bf16[3,2,640,128]{3,2,1,0:T(8,128)(2,1)S(1)}, bf16[3,2,640,128]{3,2,1,0:T(8,128)(2,1)S(1)}, u32[]{:S(2)}, u32[]{:S(2)}) collective-permute-start(bf16[3,2,640,128]{3,2,1,0:T(8,128)(2,1)S(1)} %pad_maximum_fusion), channel_id=1, source_target_pairs={{1,0},{3,2},{5,4},{7,6},{9,8},{11,10},{13,12},{15,14},{17,16},{19,... | collective-permute-start | bytes 2949128 | tf_op jit(solution)/shard_map/ppermute | solution.py:16

commit v12 on v11

--- a/solution.py
+++ b/solution.py
@@ -29,7 +29,7 @@
     return x
 
 
-def local_kernel(factor, own_ref, up_ref, down_ref, bnd_ref, k_ref, feat_ref, gf_ref, term_ref, z_ref, a_ref):
+def local_kernel(factor, own_ref, up_ref, down_ref, bnd_ref, k_ref, feat_ref, gf_ref, term_ref, z_ref, a_ref, w_ref, cat_ref, acc_ref):
     frames, breadth, channels = feat_ref.shape
 
     def slab(frame, row):
@@ -37,47 +37,52 @@
             return (up_ref, own_ref, down_ref)[row][frame]
         return bnd_ref[row, frame - frames]
 
+    def block(n):
+        return slice(n * channels, (n + 1) * channels)
+
+    for i in range(3):
+        for j in range(3):
+            for k in range(3):
+                w_ref[j, block(k), block(i)] = k_ref[(i * 3 + j) * 3 + k]
     lanes = lax.broadcasted_iota(jnp.int32, (channels, breadth), 1)
     for t in range(frames):
         values = feat_ref[t].astype(jnp.float32)
         active = (values * jax.nn.sigmoid(values)).astype(jnp.bfloat16).astype(jnp.float32)
         turned = active.T
-        a_ref[t, 0:channels] = jnp.where(lanes == 0, 0.0, pltpu.roll(turned, 1, 1)).astype(a_ref.dtype)
-        a_ref[t, channels : 2 * channels] = turned.astype(a_ref.dtype)
-        a_ref[t, 2 * channels : 3 * channels] = jnp.where(
+        a_ref[t, block(0)] = jnp.where(lanes == 0, 0.0, pltpu.roll(turned, 1, 1)).astype(a_ref.dtype)
+        a_ref[t, block(1)] = turned.astype(a_ref.dtype)
+        a_ref[t, block(2)] = jnp.where(
             lanes == breadth - 1, 0.0, pltpu.roll(turned, breadth - 1, 1)
         ).astype(a_ref.dtype)
-    term_ref[...] = jnp.zeros_like(term_ref)
+    acc_ref[...] = jnp.zeros_like(acc_ref)
     rows = lax.broadcasted_iota(jnp.int32, (breadth, channels), 0)
     for t in range(frames):
-        for i in range(3):
-            for j in range(3):
-                piece = slab(t + 2 - i, 2 - j)
-                for k in range(3):
-                    part = lax.dot_general(
-                        piece,
-                        k_ref[(i * 3 + j) * 3 + k],
-                        (((1,), (1,)), ((), ())),
-                        preferred_element_type=jnp.float32,
-                    )
-                    window = slice(k * channels, (k + 1) * channels)
-                    if i == 0 and j == 0:
-                        z_ref[:, window] = part
-                    else:
-                        z_ref[:, window] += part
-                term_ref[i * 3 + j] += jnp.dot(a_ref[t], piece, preferred_element_type=jnp.float32)
-        ahead = pltpu.roll(z_ref[:, 0:channels], breadth - 1, 0)
-        behind = pltpu.roll(z_ref[:, 2 * channels : 3 * channels], 1, 0)
+        for j in range(3):
+            for i in range(3):
+                cat_ref[:, block(i)] = slab(t + 2 - i, 2 - j)
+            joined = cat_ref[...]
+            part = lax.dot_general(
+                joined, w_ref[j], (((1,), (1,)), ((), ())), preferred_element_type=jnp.float32
+            )
+            if j == 0:
+                z_ref[...] = part
+            else:
+                z_ref[...] += part
+            acc_ref[j] += jnp.dot(a_ref[t], joined, preferred_element_type=jnp.float32)
+        ahead = pltpu.roll(z_ref[:, block(0)], breadth - 1, 0)
+        behind = pltpu.roll(z_ref[:, block(2)], 1, 0)
         grad_input = (
             jnp.where(rows == breadth - 1, 0.0, ahead)
-            + z_ref[:, channels : 2 * channels]
+            + z_ref[:, block(1)]
             + jnp.where(rows == 0, 0.0, behind)
         )
         values = feat_ref[t].astype(jnp.float32)
         sigmoid_part = jax.nn.sigmoid(values)
         derivative = sigmoid_part * (1.0 + values * (1.0 - sigmoid_part))
         gf_ref[t] = (own_ref[t].astype(jnp.float32) + derivative * grad_input).astype(gf_ref.dtype)
-    term_ref[...] = term_ref[...] * factor
+    for i in range(3):
+        for j in range(3):
+            term_ref[i * 3 + j] = acc_ref[j, :, block(i)] * factor
 
 
 def local_grads(pieces, weights, feat, factor):
@@ -97,6 +102,9 @@
         scratch_shapes=[
             pltpu.VMEM((breadth, 3 * channels), jnp.float32),
             pltpu.VMEM((frames, 3 * channels, breadth), jnp.bfloat16),
+            pltpu.VMEM((3, 3 * channels, 3 * channels), jnp.bfloat16),
+            pltpu.VMEM((breadth, 3 * channels), jnp.bfloat16),
+            pltpu.VMEM((3, 3 * channels, 3 * channels), jnp.float32),
         ],
         compiler_params=pltpu.CompilerParams(vmem_limit_bytes=48 * 1024 * 1024),
         cost_estimate=pl.CostEstimate(flops=flops, bytes_accessed=moved, transcendentals=2 * feat.size),

time: 80.4 us -> 78.3 us (0.974)
  Pallas kernels: 11 us -> 8.92 us
    pallas_call x1, Pallas kernels: 11 us -> 8.92 us  [local_grads(): pl.pallas_call(lambda *refs: local_kernel(factor, *refs), out_shape=(jax....]
where the time goes in v12:
time: 78.3 us; the launch traced here: 78 us
  blocking collectives  41 us (52%)
  waiting for transfers between devices  16 us (20%)
  Pallas kernels  8.92 us (11%)
  starting transfers between devices  7.3 us (9%)
  local copies, waits for them, and re-layouts  3.6 us (5%)
    all_to_all x2, blocking collectives, reduce_blocks(): part = lax.all_to_all(shaped, axis, 0, 0, tiled=True).sum(0)  41 us
    ppermute x2, waiting for transfers between devices, row_neighbours(): return (lax.ppermute(x, axis, up), lax.ppermute(x, axis, down))  12.8 us
    pallas_call x1, Pallas kernels, local_grads(): pl.pallas_call(lambda *refs: local_kernel(factor, *refs), out_shape=(jax....  8.92 us
    ppermute x2, starting transfers between devices, row_neighbours(): return (lax.ppermute(x, axis, up), lax.ppermute(x, axis, down))  6.01 us
    ppermute x1, waiting for transfers between devices, passed_along(): return lax.ppermute(block, axis, route)  3.16 us
  transfers between devices with their start and end apart: 3, of which 3 were waited for; matrix products, arithmetic and copies ran while one was open for 1% of the time, Pallas kernels for 0%

profile of v12, /device:TPU:0, one launch (start us, length us, event | category | flops | bytes accessed | tf_op | source)
XLA Modules:
  0.0 78.0 jit_solution(4686352443086309920)
XLA Ops:
  0.6 0.0 copy-start
  0.6 0.0 copy-start.1
  0.6 0.0 copy-start.2
  0.7 1.4 %collective-permute-start.1 = (bf16[4,640,128]{2,1,0:T(8,128)(2,1)}, bf16[4,640,128]{2,1,0:T(8,128)(2,1)S(1)}, u32[]{:S(2)}, u32[]{:S(2)}) collective-permute-start(bf16[4,640,128]{2,1,0:T(8,128)(2,1)} %bitcast.21), channel_id=1, source_target_pairs={{2,0},{4,2},{6,4},{8,6},{10,8},{12,10},{14,12},{16,14},{18,16},{20... | collective-permute-start | bytes 1966088 | tf_op jit(solution)/shard_map/ppermute | solution.py:118
  2.1 4.6 %collective-permute-start = (bf16[4,640,128]{2,1,0:T(8,128)(2,1)}, bf16[4,640,128]{2,1,0:T(8,128)(2,1)S(1)}, u32[]{:S(2)}, u32[]{:S(2)}) collective-permute-start(bf16[4,640,128]{2,1,0:T(8,128)(2,1)} %bitcast.22), channel_id=1, source_target_pairs={{0,2},{2,4},{4,6},{6,8},{8,10},{10,12},{12,14},{14,16},{16,18},{18... | collective-permute-start | bytes 1966088 | tf_op jit(solution)/shard_map/ppermute | solution.py:118
  6.7 1.0 %slice_bitcast_fusion.1 = bf16[1,2,640,128]{3,2,1,0:T(8,128)(2,1)S(1)} fusion(bf16[4,1,640,128]{3,2,0,1:T(8,128)(2,1)} %bitcast.23), kind=kLoop, calls=%fused_computation.2 | loop fusion | bytes 655360 | tf_op jit(solution)/shard_map/stack | solution.py:125
  7.7 11.5 %collective-permute-done.1.refs_2_ = bf16[4,640,128]{2,1,0:T(8,128)(2,1)S(1)} collective-permute-done((bf16[4,640,128]{2,1,0:T(8,128)(2,1)}, bf16[4,640,128]{2,1,0:T(8,128)(2,1)S(1)}, u32[]{:S(2)}, u32[]{:S(2)}) %collective-permute-start.1) | collective-permute-done | bytes 655392 | tf_op jit(solution)/shard_map/ppermute | solution.py:118
  19.3 1.3 %collective-permute-done.refs_1_ = bf16[4,640,128]{2,1,0:T(8,128)(2,1)S(1)} collective-permute-done((bf16[4,640,128]{2,1,0:T(8,128)(2,1)}, bf16[4,640,128]{2,1,0:T(8,128)(2,1)S(1)}, u32[]{:S(2)}, u32[]{:S(2)}) %collective-permute-start) | collective-permute-done | bytes 655392 | tf_op jit(solution)/shard_map/ppermute | solution.py:118
  20.5 0.1 pad_maximum_fusion
  20.7 1.3 %collective-permute-start.2 = (bf16[3,2,640,128]{3,2,1,0:T(8,128)(2,1)S(1)}, bf16[3,2,640,128]{3,2,1,0:T(8,128)(2,1)S(1)}, u32[]{:S(2)}, u32[]{:S(2)}) collective-permute-start(bf16[3,2,640,128]{3,2,1,0:T(8,128)(2,1)S(1)} %pad_maximum_fusion), channel_id=1, source_target_pairs={{1,0},{3,2},{5,4},{7,6},{9,8},{11,10},{13,12},{15,14},{17,16},{19,... | collective-permute-start | bytes 2949128 | tf_op jit(solution)/shard_map/ppermute | solution.py:16
  22.0 3.2 %collective-permute-done.2.refs_3_ = bf16[3,2,640,128]{3,2,1,0:T(8,128)(2,1)S(1)} collective-permute-done((bf16[3,2,640,128]{3,2,1,0:T(8,128)(2,1)S(1)}, bf16[3,2,640,128]{3,2,1,0:T(8,128)(2,1)S(1)}, u32[]{:S(2)}, u32[]{:S(2)}) %collective-permute-start.2) | collective-permute-done | bytes 983072 | tf_op jit(solution)/shard_map/ppermute | solution.py:16
  25.1 0.0 copy-done
  25.1 0.0 copy-done.1
  25.1 0.0 copy-done.2
  25.1 8.9 %shard_map.67 = (bf16[4,640,128]{2,1,0:T(8,128)(2,1)}, f32[9,384,128]{2,1,0:T(8,128)}) custom-call(bf16[4,640,128]{2,1,0:T(8,128)(2,1)S(1)} %bitcast.24, bf16[4,640,128]{2,1,0:T(8,128)(2,1)S(1)} %collective-permute-done.refs_1_, bf16[4,640,128]{2,1,0:T(8,128)(2,1)S(1)} %collective-permute-done.1.refs_2_, ...), custom_call_target="tpu_custom_call" | custom-call | flops 4529848320 | bytes 6914048 | tf_op jit(solution)/shard_map/pallas_call | solution.py:94
  34.1 1.5 %reshape_reshape.3 = f32[128,27,128]{2,1,0:T(8,128)S(1)} reshape(f32[9,384,128]{2,1,0:T(8,128)} %get-tuple-element.6) | data formatting | bytes 3538944 | tf_op jit(solution)/shard_map/reshape;reshape | solution.py:134
  35.6 0.2 pad.4
  35.8 0.2 copy.12
  36.0 5.4 %all_to_all.10 = f32[2,64,32,128]{3,2,1,0:T(8,128)S(1)} all-to-all(f32[2,64,32,128]{3,2,1,0:T(8,128)S(1)} %bitcast.28), channel_id=1, replica_groups=mesh['y'=4,'z'=4,'x'=4,'core'=2] {'core'}, dimensions={0} | all-to-all | bytes 4194304 | tf_op jit(solution)/shard_map/all_to_all | solution.py:157
  41.4 0.3 reduce_sum.20
  41.7 35.6 %all_to_all.11 = f32[64,1,32,128]{3,2,1,0:T(8,128)S(1)} all-to-all(f32[64,1,32,128]{3,2,1,0:T(8,128)S(1)} %bitcast.29), channel_id=1, replica_groups=mesh['y'=4,'z'=4,'x'=4,'core'=2] {'y','z','x'}, dimensions={0} | all-to-all | bytes 2097152 | tf_op jit(solution)/shard_map/all_to_all | solution.py:157
  77.3 0.1 reduce_sum.21
  77.4 0.6 slice_bitcast_fusion.3
  (2 shorter events, 0.0 us)
Async XLA Ops:
  0.6 24.5 %copy-start = (bf16[4,1,640,128]{3,2,1,0:T(8,128)(2,1)S(1)}, bf16[4,1,640,128]{3,2,1,0:T(8,128)(2,1)}, u32[]{:S(2)}) copy-start(bf16[4,1,640,128]{3,2,1,0:T(8,128)(2,1)} %param.5) | copy-start | bytes 1966084
  0.6 24.5 %copy-start.1 = (bf16[3,3,3,128,128]{4,3,2,1,0:T(8,128)(2,1)S(1)}, bf16[3,3,3,128,128]{4,3,2,1,0:T(8,128)(2,1)}, u32[]{:S(2)}) copy-start(bf16[3,3,3,128,128]{4,3,2,1,0:T(8,128)(2,1)} %param.6) | copy-start | bytes 2654212
  0.6 24.5 %copy-start.2 = (bf16[4,1,640,128]{3,2,1,0:T(8,128)(2,1)S(1)}, bf16[4,1,640,128]{3,2,1,0:T(8,128)(2,1)}, u32[]{:S(2)}) copy-start(bf16[4,1,640,128]{3,2,1,0:T(8,128)(2,1)} %param.4) | copy-start | bytes 1966084
  0.7 18.6 %collective-permute-start.1 = (bf16[4,640,128]{2,1,0:T(8,128)(2,1)}, bf16[4,640,128]{2,1,0:T(8,128)(2,1)S(1)}, u32[]{:S(2)}, u32[]{:S(2)}) collective-permute-start(bf16[4,640,128]{2,1,0:T(8,128)(2,1)} %bitcast.21), channel_id=1, source_target_pairs={{2,0},{4,2},{6,4},{8,6},{10,8},{12,10},{14,12},{16,14},{18,16},{20... | collective-permute-start | bytes 1966088 | tf_op jit(solution)/shard_map/ppermute | solution.py:118
  2.1 18.4 %collective-permute-start = (bf16[4,640,128]{2,1,0:T(8,128)(2,1)}, bf16[4,640,128]{2,1,0:T(8,128)(2,1)S(1)}, u32[]{:S(2)}, u32[]{:S(2)}) collective-permute-start(bf16[4,640,128]{2,1,0:T(8,128)(2,1)} %bitcast.22), channel_id=1, source_target_pairs={{0,2},{2,4},{4,6},{6,8},{8,10},{10,12},{12,14},{14,16},{16,18},{18... | collective-permute-start | bytes 1966088 | tf_op jit(solution)/shard_map/ppermute | solution.py:118
  20.7 4.5 %collective-permute-start.2 = (bf16[3,2,640,128]{3,2,1,0:T(8,128)(2,1)S(1)}, bf16[3,2,640,128]{3,2,1,0:T(8,128)(2,1)S(1)}, u32[]{:S(2)}, u32[]{:S(2)}) collective-permute-start(bf16[3,2,640,128]{3,2,1,0:T(8,128)(2,1)S(1)} %pad_maximum_fusion), channel_id=1, source_target_pairs={{1,0},{3,2},{5,4},{7,6},{9,8},{11,10},{13,12},{15,14},{17,16},{19,... | collective-permute-start | bytes 2949128 | tf_op jit(solution)/shard_map/ppermute | solution.py:16

commit v13 on v12

--- a/solution.py
+++ b/solution.py
@@ -29,38 +29,59 @@
     return x
 
 
-def local_kernel(factor, own_ref, up_ref, down_ref, bnd_ref, k_ref, feat_ref, gf_ref, term_ref, z_ref, a_ref, w_ref, cat_ref, acc_ref):
-    frames, breadth, channels = feat_ref.shape
-
+def slab_reader(own_ref, up_ref, down_ref, bnd_ref, frames):
     def slab(frame, row):
         if frame < frames:
             return (up_ref, own_ref, down_ref)[row][frame]
         return bnd_ref[row, frame - frames]
 
-    def block(n):
-        return slice(n * channels, (n + 1) * channels)
-
+    return slab
+
+
+def block(n, channels):
+    return slice(n * channels, (n + 1) * channels)
+
+
+def join_slabs(slab, cat_ref, t, j, channels):
     for i in range(3):
-        for j in range(3):
-            for k in range(3):
-                w_ref[j, block(k), block(i)] = k_ref[(i * 3 + j) * 3 + k]
+        cat_ref[:, block(i, channels)] = slab(t + 2 - i, 2 - j)
+    return cat_ref[...]
+
+
+def term_kernel(factor, own_ref, up_ref, down_ref, bnd_ref, feat_ref, term_ref, a_ref, cat_ref, acc_ref):
+    frames, breadth, channels = feat_ref.shape
+    slab = slab_reader(own_ref, up_ref, down_ref, bnd_ref, frames)
     lanes = lax.broadcasted_iota(jnp.int32, (channels, breadth), 1)
     for t in range(frames):
         values = feat_ref[t].astype(jnp.float32)
         active = (values * jax.nn.sigmoid(values)).astype(jnp.bfloat16).astype(jnp.float32)
         turned = active.T
-        a_ref[t, block(0)] = jnp.where(lanes == 0, 0.0, pltpu.roll(turned, 1, 1)).astype(a_ref.dtype)
-        a_ref[t, block(1)] = turned.astype(a_ref.dtype)
-        a_ref[t, block(2)] = jnp.where(
+        a_ref[t, block(0, channels)] = jnp.where(lanes == 0, 0.0, pltpu.roll(turned, 1, 1)).astype(a_ref.dtype)
+        a_ref[t, block(1, channels)] = turned.astype(a_ref.dtype)
+        a_ref[t, block(2, channels)] = jnp.where(
             lanes == breadth - 1, 0.0, pltpu.roll(turned, breadth - 1, 1)
         ).astype(a_ref.dtype)
     acc_ref[...] = jnp.zeros_like(acc_ref)
+    for t in range(frames):
+        for j in range(3):
+            joined = join_slabs(slab, cat_ref, t, j, channels)
+            acc_ref[j] += jnp.dot(a_ref[t], joined, preferred_element_type=jnp.float32)
+    for i in range(3):
+        for j in range(3):
+            term_ref[i * 3 + j] = acc_ref[j, :, block(i, channels)] * factor
+
+
+def grad_kernel(own_ref, up_ref, down_ref, bnd_ref, k_ref, feat_ref, gf_ref, z_ref, w_ref, cat_ref):
+    frames, breadth, channels = feat_ref.shape
+    slab = slab_reader(own_ref, up_ref, down_ref, bnd_ref, frames)
+    for i in range(3):
+        for j in range(3):
+            for k in range(3):
+                w_ref[j, block(k, channels), block(i, channels)] = k_ref[(i * 3 + j) * 3 + k]
     rows = lax.broadcasted_iota(jnp.int32, (breadth, channels), 0)
     for t in range(frames):
         for j in range(3):
-            for i in range(3):
-                cat_ref[:, block(i)] = slab(t + 2 - i, 2 - j)
-            joined = cat_ref[...]
+            joined = join_slabs(slab, cat_ref, t, j, channels)
             part = lax.dot_general(
                 joined, w_ref[j], (((1,), (1,)), ((), ())), preferred_element_type=jnp.float32
             )
@@ -68,47 +89,58 @@
                 z_ref[...] = part
             else:
                 z_ref[...] += part
-            acc_ref[j] += jnp.dot(a_ref[t], joined, preferred_element_type=jnp.float32)
-        ahead = pltpu.roll(z_ref[:, block(0)], breadth - 1, 0)
-        behind = pltpu.roll(z_ref[:, block(2)], 1, 0)
+        ahead = pltpu.roll(z_ref[:, block(0, channels)], breadth - 1, 0)
+        behind = pltpu.roll(z_ref[:, block(2, channels)], 1, 0)
         grad_input = (
             jnp.where(rows == breadth - 1, 0.0, ahead)
-            + z_ref[:, block(1)]
+            + z_ref[:, block(1, channels)]
             + jnp.where(rows == 0, 0.0, behind)
         )
         values = feat_ref[t].astype(jnp.float32)
         sigmoid_part = jax.nn.sigmoid(values)
         derivative = sigmoid_part * (1.0 + values * (1.0 - sigmoid_part))
         gf_ref[t] = (own_ref[t].astype(jnp.float32) + derivative * grad_input).astype(gf_ref.dtype)
-    for i in range(3):
-        for j in range(3):
-            term_ref[i * 3 + j] = acc_ref[j, :, block(i)] * factor
 
 
 def local_grads(pieces, weights, feat, factor):
     frames, breadth, channels = feat.shape
     vmem = pl.BlockSpec(memory_space=pltpu.VMEM)
-    operands = tuple(pieces) + (weights, feat)
-    flops = 2 * 2 * frames * 9 * breadth * channels * 3 * channels
-    moved = sum(2 * x.size for x in operands) + 2 * feat.size + 4 * 9 * 3 * channels * channels
-    return pl.pallas_call(
-        lambda *refs: local_kernel(factor, *refs),
-        out_shape=(
-            jax.ShapeDtypeStruct((frames, breadth, channels), jnp.bfloat16),
-            jax.ShapeDtypeStruct((9, 3 * channels, channels), jnp.float32),
-        ),
-        in_specs=[vmem] * len(operands),
-        out_specs=(vmem, vmem),
+    params = pltpu.CompilerParams(vmem_limit_bytes=48 * 1024 * 1024)
+    flops = 2 * frames * 9 * breadth * channels * 3 * channels
+    piece_bytes = sum(2 * x.size for x in pieces)
+    term = pl.pallas_call(
+        lambda *refs: term_kernel(factor, *refs),
+        out_shape=jax.ShapeDtypeStruct((9, 3 * channels, channels), jnp.float32),
+        in_specs=[vmem] * (len(pieces) + 1),
+        out_specs=vmem,
         scratch_shapes=[
-            pltpu.VMEM((breadth, 3 * channels), jnp.float32),
             pltpu.VMEM((frames, 3 * channels, breadth), jnp.bfloat16),
-            pltpu.VMEM((3, 3 * channels, 3 * channels), jnp.bfloat16),
             pltpu.VMEM((breadth, 3 * channels), jnp.bfloat16),
             pltpu.VMEM((3, 3 * channels, 3 * channels), jnp.float32),
         ],
-        compiler_params=pltpu.CompilerParams(vmem_limit_bytes=48 * 1024 * 1024),
-        cost_estimate=pl.CostEstimate(flops=flops, bytes_accessed=moved, transcendentals=2 * feat.size),
-    )(*operands)
+        compiler_params=params,
+        cost_estimate=pl.CostEstimate(
+            flops=flops, bytes_accessed=piece_bytes + 2 * feat.size + 4 * 27 * channels * channels,
+            transcendentals=feat.size,
+        ),
+    )(*pieces, feat)
+    grad_features = pl.pallas_call(
+        grad_kernel,
+        out_shape=jax.ShapeDtypeStruct((frames, breadth, channels), jnp.bfloat16),
+        in_specs=[vmem] * (len(pieces) + 2),
+        out_specs=vmem,
+        scratch_shapes=[
+            pltpu.VMEM((breadth, 3 * channels), jnp.float32),
+            pltpu.VMEM((3, 3 * channels, 3 * channels), jnp.bfloat16),
+            pltpu.VMEM((breadth, 3 * channels), jnp.bfloat16),
+        ],
+        compiler_params=params,
+        cost_estimate=pl.CostEstimate(
+            flops=flops, bytes_accessed=piece_bytes + 2 * weights.size + 4 * feat.size,
+            transcendentals=feat.size,
+        ),
+    )(*pieces, weights, feat)
+    return grad_features, term
 
 
 def row_neighbours(x, axis):

time: 78.3 us -> 81.3 us (1.038)
  blocking collectives: 41 us -> 6.29 us
  starting transfers between devices: 7.3 us -> 24.1 us
  waiting for transfers between devices: 16 us -> 27.9 us
  local copies, waits for them, and re-layouts: 3.6 us -> 8.39 us
  other arithmetic: 0.47 us -> 4.42 us
    all_to_all x2 -> x1, blocking collectives: 41 us -> 6.29 us  [reduce_blocks(): part = lax.all_to_all(shaped, axis, 0, 0, tiled=True).sum(0)]
    all_to_all x0 -> x1, starting transfers between devices: none -> 16.8 us  [reduce_blocks(): part = lax.all_to_all(shaped, axis, 0, 0, tiled=True).sum(0)]
    all_to_all x0 -> x1, waiting for transfers between devices: none -> 12 us  [reduce_blocks(): part = lax.all_to_all(shaped, axis, 0, 0, tiled=True).sum(0)]
    reduce_sum x2, other arithmetic: 0.36 us -> 4.31 us  [reduce_blocks(): part = lax.all_to_all(shaped, axis, 0, 0, tiled=True).sum(0)]
    unnamed x6 -> x16, local copies, waits for them, and re-layouts: 0.01 us -> 3.23 us
    pad x1, local copies, waits for them, and re-layouts: 0.18 us -> 1.77 us  [body(): jnp.pad(term.reshape(owners, rows, channels), ((0, 0), (0, padded - rows)...]
    pallas_call x1 -> x2, Pallas kernels: 8.92 us -> 8.92 us  [the longest x1 4.86 us: local_grads(): pl.pallas_call(grad_kernel, out_shape=jax.ShapeDtypeStruct((frames, bread...]
  transfers between devices with their start and end apart: 3 -> 4, of which waited for: 3 -> 4; matrix products, arithmetic and copies ran while one was open for 1% -> 1% of each run, Pallas kernels for 0% -> 6%
where the time goes in v13:
time: 81.3 us; the launch traced here: 80.8 us
  waiting for transfers between devices  27.9 us (34%)
  starting transfers between devices  24.1 us (30%)
  Pallas kernels  8.92 us (11%)
  local copies, waits for them, and re-layouts  8.39 us (10%)
  blocking collectives  6.29 us (8%)
  other arithmetic  4.42 us (5%)
    all_to_all x1, starting transfers between devices, reduce_blocks(): part = lax.all_to_all(shaped, axis, 0, 0, tiled=True).sum(0)  16.8 us
    ppermute x2, waiting for transfers between devices, row_neighbours(): return (lax.ppermute(x, axis, up), lax.ppermute(x, axis, down))  12.8 us
    all_to_all x1, waiting for transfers between devices, reduce_blocks(): part = lax.all_to_all(shaped, axis, 0, 0, tiled=True).sum(0)  12 us
    all_to_all x1, blocking collectives, reduce_blocks(): part = lax.all_to_all(shaped, axis, 0, 0, tiled=True).sum(0)  6.29 us
    ppermute x2, starting transfers between devices, row_neighbours(): return (lax.ppermute(x, axis, up), lax.ppermute(x, axis, down))  6.01 us
    pallas_call x1, Pallas kernels, local_grads(): pl.pallas_call(grad_kernel, out_shape=jax.ShapeDtypeStruct((frames, bread...  4.86 us
    reduce_sum x2, other arithmetic, reduce_blocks(): part = lax.all_to_all(shaped, axis, 0, 0, tiled=True).sum(0)  4.31 us
    pallas_call x1, Pallas kernels, local_grads(): pl.pallas_call(lambda *refs: term_kernel(factor, *refs), out_shape=jax.Sh...  4.06 us
  transfers between devices with their start and end apart: 4, of which 4 were waited for; matrix products, arithmetic and copies ran while one was open for 1% of the time, Pallas kernels for 6%

profile of v13, /device:TPU:0, one launch (start us, length us, event | category | flops | bytes accessed | tf_op | source)
XLA Modules:
  0.0 80.8 jit_solution(5483237806467934651)
XLA Ops:
  0.6 0.0 copy-start
  0.6 0.0 copy-start.6
  0.7 1.4 %collective-permute-start.1 = (bf16[4,640,128]{2,1,0:T(8,128)(2,1)}, bf16[4,640,128]{2,1,0:T(8,128)(2,1)S(1)}, u32[]{:S(2)}, u32[]{:S(2)}) collective-permute-start(bf16[4,640,128]{2,1,0:T(8,128)(2,1)} %bitcast.21), channel_id=1, source_target_pairs={{2,0},{4,2},{6,4},{8,6},{10,8},{12,10},{14,12},{16,14},{18,16},{20... | collective-permute-start | bytes 1966088 | tf_op jit(solution)/shard_map/ppermute | solution.py:150
  2.1 4.6 %collective-permute-start = (bf16[4,640,128]{2,1,0:T(8,128)(2,1)}, bf16[4,640,128]{2,1,0:T(8,128)(2,1)S(1)}, u32[]{:S(2)}, u32[]{:S(2)}) collective-permute-start(bf16[4,640,128]{2,1,0:T(8,128)(2,1)} %bitcast.22), channel_id=1, source_target_pairs={{0,2},{2,4},{4,6},{6,8},{8,10},{10,12},{12,14},{14,16},{16,18},{18... | collective-permute-start | bytes 1966088 | tf_op jit(solution)/shard_map/ppermute | solution.py:150
  6.7 1.0 %slice_bitcast_fusion.1 = bf16[1,2,640,128]{3,2,1,0:T(8,128)(2,1)S(1)} fusion(bf16[4,1,640,128]{3,2,0,1:T(8,128)(2,1)} %bitcast.23), kind=kLoop, calls=%fused_computation.2 | loop fusion | bytes 655360 | tf_op jit(solution)/shard_map/stack | solution.py:157
  7.7 11.5 %collective-permute-done.1.down_ref.refs_2_ = bf16[4,640,128]{2,1,0:T(8,128)(2,1)S(1)} collective-permute-done((bf16[4,640,128]{2,1,0:T(8,128)(2,1)}, bf16[4,640,128]{2,1,0:T(8,128)(2,1)S(1)}, u32[]{:S(2)}, u32[]{:S(2)}) %collective-permute-start.1) | collective-permute-done | bytes 655392 | tf_op jit(solution)/shard_map/ppermute | solution.py:150
  19.3 1.3 %collective-permute-done.up_ref.refs_1_ = bf16[4,640,128]{2,1,0:T(8,128)(2,1)S(1)} collective-permute-done((bf16[4,640,128]{2,1,0:T(8,128)(2,1)}, bf16[4,640,128]{2,1,0:T(8,128)(2,1)S(1)}, u32[]{:S(2)}, u32[]{:S(2)}) %collective-permute-start) | collective-permute-done | bytes 655392 | tf_op jit(solution)/shard_map/ppermute | solution.py:150
  20.5 0.0 copy-start.1
  20.5 0.1 pad_maximum_fusion
  20.7 1.3 %collective-permute-start.2 = (bf16[3,2,640,128]{3,2,1,0:T(8,128)(2,1)S(1)}, bf16[3,2,640,128]{3,2,1,0:T(8,128)(2,1)S(1)}, u32[]{:S(2)}, u32[]{:S(2)}) collective-permute-start(bf16[3,2,640,128]{3,2,1,0:T(8,128)(2,1)S(1)} %pad_maximum_fusion), channel_id=1, source_target_pairs={{1,0},{3,2},{5,4},{7,6},{9,8},{11,10},{13,12},{15,14},{17,16},{19,... | collective-permute-start | bytes 2949128 | tf_op jit(solution)/shard_map/ppermute | solution.py:16
  22.0 3.2 %collective-permute-done.2.bnd_ref.refs_3_ = bf16[3,2,640,128]{3,2,1,0:T(8,128)(2,1)S(1)} collective-permute-done((bf16[3,2,640,128]{3,2,1,0:T(8,128)(2,1)S(1)}, bf16[3,2,640,128]{3,2,1,0:T(8,128)(2,1)S(1)}, u32[]{:S(2)}, u32[]{:S(2)}) %collective-permute-start.2) | collective-permute-done | bytes 983072 | tf_op jit(solution)/shard_map/ppermute | solution.py:16
  25.1 0.0 copy-done.1
  25.1 0.0 copy-done
  25.1 0.0 copy-done.6
  25.1 4.1 %shard_map.68 = f32[9,384,128]{2,1,0:T(8,128)S(1)} custom-call(bf16[4,640,128]{2,1,0:T(8,128)(2,1)S(1)} %bitcast.24, bf16[4,640,128]{2,1,0:T(8,128)(2,1)S(1)} %collective-permute-done.up_ref.refs_1_, bf16[4,640,128]{2,1,0:T(8,128)(2,1)S(1)} %collective-permute-done.1.down_ref.refs_2_, bf16[3,2,640,128]{3,2,1,0:T(8,128)(2,1)S(1)} %collective-permute-done.2.bnd_ref.refs_3_, ...), custom_call_target="tpu_custom_call" | custom-call | flops 2264924160 | bytes 5373952 | tf_op jit(solution)/shard_map/pallas_call | solution.py:111
  29.2 0.0 copy-start.3
  29.2 1.0 %copy-done.3 = bf16[3,2,640,128]{3,2,1,0:T(8,128)(2,1)} copy-done((bf16[3,2,640,128]{3,2,1,0:T(8,128)(2,1)}, bf16[3,2,640,128]{3,2,1,0:T(8,128)(2,1)S(1)}, u32[]{:S(2)}) %copy-start.3) | copy-done | bytes 983064
  30.2 1.5 %reshape_reshape.3 = f32[128,27,128]{2,1,0:T(8,128)} reshape(f32[9,384,128]{2,1,0:T(8,128)S(1)} %shard_map.68) | data formatting | bytes 3538944 | tf_op jit(solution)/shard_map/reshape;reshape | solution.py:166
  31.7 1.8 %pad.4 = f32[128,32,128]{2,1,0:T(8,128)S(1)} pad(f32[128,27,128]{2,1,0:T(8,128)} %reshape_reshape.3, f32[]{:T(128)} %constant.2.clone.1), padding=0_0x0_5x0_0 | pad | bytes 3866628 | tf_op jit(solution)/shard_map/jit(_pad)/pad | solution.py:166
  33.4 0.2 copy.12
  33.7 6.3 %all_to_all.10 = f32[2,64,32,128]{3,2,1,0:T(8,128)} all-to-all(f32[2,64,32,128]{3,2,1,0:T(8,128)S(1)} %bitcast.30), channel_id=1, replica_groups=mesh['y'=4,'z'=4,'x'=4,'core'=2] {'core'}, dimensions={0} | all-to-all | bytes 4194304 | tf_op jit(solution)/shard_map/all_to_all | solution.py:189
  40.0 0.0 copy-start.2
  40.0 0.0 copy-start.4
  40.0 3.0 %reduce_sum.20 = f32[64,32,128]{2,1,0:T(8,128)} reduce(f32[2,64,32,128]{3,2,1,0:T(8,128)} %all_to_all.10, f32[]{:T(128)} %constant.2.clone.1), dimensions={0}, to_apply=%region_0.2 | reduce | flops 262144 | bytes 3145732 | tf_op jit(solution)/shard_map/reduce_sum | solution.py:189
  43.0 16.8 %all-to-all-start.1 = ((f32[64,1,32,128]{3,2,1,0:T(8,128)}), f32[64,1,32,128]{3,2,1,0:T(8,128)}, u32[]{:S(2)}, u32[]{:S(2)}) async-start(f32[64,1,32,128]{3,2,1,0:T(8,128)} %bitcast.31), calls=%async_computation.1 | async-start | bytes 2097152 | tf_op jit(solution)/shard_map/all_to_all | solution.py:189
  59.8 0.0 copy-done.2
  59.8 0.0 copy-done.4
  59.8 0.0 copy-start.5
  59.8 1.2 %copy-done.5 = bf16[3,3,3,128,128]{4,3,2,1,0:T(8,128)(2,1)S(1)} copy-done((bf16[3,3,3,128,128]{4,3,2,1,0:T(8,128)(2,1)S(1)}, bf16[3,3,3,128,128]{4,3,2,1,0:T(8,128)(2,1)}, u32[]{:S(2)}) %copy-start.5) | copy-done | bytes 884760
  60.9 0.0 copy-start.7
  61.0 1.1 %copy-done.7 = bf16[4,1,640,128]{3,2,1,0:T(8,128)(2,1)S(1)} copy-done((bf16[4,1,640,128]{3,2,1,0:T(8,128)(2,1)S(1)}, bf16[4,1,640,128]{3,2,1,0:T(8,128)(2,1)}, u32[]{:S(2)}) %copy-start.7) | copy-done | bytes 655384
  62.0 4.9 %shard_map.67 = bf16[4,640,128]{2,1,0:T(8,128)(2,1)} custom-call(bf16[4,640,128]{2,1,0:T(8,128)(2,1)S(1)} %bitcast.25, bf16[4,640,128]{2,1,0:T(8,128)(2,1)S(1)} %copy-done.2, bf16[4,640,128]{2,1,0:T(8,128)(2,1)S(1)} %collective-permute-done.1.down_ref.refs_2_, bf16[3,2,640,128]{3,2,1,0:T(8,128)(2,1)S(1)} %copy-done.4, bf16[27,128,128]{2,1,0:T(8,128)(2,1)S(1)} %bitcast.26, ...), custom_call_target="tpu_custom_call" | custom-call | flops 2264924160 | bytes 5144576 | tf_op jit(solution)/shard_map/pallas_call | solution.py:127
  66.9 12.0 %all-to-all-done.1 = f32[64,1,32,128]{3,2,1,0:T(8,128)} async-done(((f32[64,1,32,128]{3,2,1,0:T(8,128)}), f32[64,1,32,128]{3,2,1,0:T(8,128)}, u32[]{:S(2)}, u32[]{:S(2)}) %all-to-all-start.1) | async-done | bytes 1048608 | tf_op jit(solution)/shard_map/all_to_all | solution.py:189
  78.8 1.3 %reduce_sum.21 = f32[32,128]{1,0:T(8,128)S(1)} reduce(f32[64,1,32,128]{3,2,1,0:T(8,128)} %all-to-all-done.1, f32[]{:T(128)} %constant.2.clone.1), dimensions={0,1}, to_apply=%region_1.3 | reduce | flops 258048 | bytes 1064964 | tf_op jit(solution)/shard_map/reduce_sum | solution.py:189
  80.2 0.6 slice_bitcast_fusion.3
  (2 shorter events, 0.0 us)
Async XLA Ops:
  0.6 24.5 %copy-start = (bf16[4,1,640,128]{3,2,1,0:T(8,128)(2,1)S(1)}, bf16[4,1,640,128]{3,2,1,0:T(8,128)(2,1)}, u32[]{:S(2)}) copy-start(bf16[4,1,640,128]{3,2,1,0:T(8,128)(2,1)} %param.5) | copy-start | bytes 1966084
  0.6 24.5 %copy-start.6 = (bf16[4,1,640,128]{3,2,1,0:T(8,128)(2,1)S(1)}, bf16[4,1,640,128]{3,2,1,0:T(8,128)(2,1)}, u32[]{:S(2)}) copy-start(bf16[4,1,640,128]{3,2,1,0:T(8,128)(2,1)} %param.4) | copy-start | bytes 1966084
  0.7 18.6 %collective-permute-start.1 = (bf16[4,640,128]{2,1,0:T(8,128)(2,1)}, bf16[4,640,128]{2,1,0:T(8,128)(2,1)S(1)}, u32[]{:S(2)}, u32[]{:S(2)}) collective-permute-start(bf16[4,640,128]{2,1,0:T(8,128)(2,1)} %bitcast.21), channel_id=1, source_target_pairs={{2,0},{4,2},{6,4},{8,6},{10,8},{12,10},{14,12},{16,14},{18,16},{20... | collective-permute-start | bytes 1966088 | tf_op jit(solution)/shard_map/ppermute | solution.py:150
  2.1 18.4 %collective-permute-start = (bf16[4,640,128]{2,1,0:T(8,128)(2,1)}, bf16[4,640,128]{2,1,0:T(8,128)(2,1)S(1)}, u32[]{:S(2)}, u32[]{:S(2)}) collective-permute-start(bf16[4,640,128]{2,1,0:T(8,128)(2,1)} %bitcast.22), channel_id=1, source_target_pairs={{0,2},{2,4},{4,6},{6,8},{8,10},{10,12},{12,14},{14,16},{16,18},{18... | collective-permute-start | bytes 1966088 | tf_op jit(solution)/shard_map/ppermute | solution.py:150
  20.5 4.6 %copy-start.1 = (bf16[4,640,128]{2,1,0:T(8,128)(2,1)}, bf16[4,640,128]{2,1,0:T(8,128)(2,1)S(1)}, u32[]{:S(2)}) copy-start(bf16[4,640,128]{2,1,0:T(8,128)(2,1)S(1)} %collective-permute-done.up_ref.refs_1_) | copy-start | bytes 1966084
  20.7 4.5 %collective-permute-start.2 = (bf16[3,2,640,128]{3,2,1,0:T(8,128)(2,1)S(1)}, bf16[3,2,640,128]{3,2,1,0:T(8,128)(2,1)S(1)}, u32[]{:S(2)}, u32[]{:S(2)}) collective-permute-start(bf16[3,2,640,128]{3,2,1,0:T(8,128)(2,1)S(1)} %pad_maximum_fusion), channel_id=1, source_target_pairs={{1,0},{3,2},{5,4},{7,6},{9,8},{11,10},{13,12},{15,14},{17,16},{19,... | collective-permute-start | bytes 2949128 | tf_op jit(solution)/shard_map/ppermute | solution.py:16
  29.2 1.0 %copy-start.3 = (bf16[3,2,640,128]{3,2,1,0:T(8,128)(2,1)}, bf16[3,2,640,128]{3,2,1,0:T(8,128)(2,1)S(1)}, u32[]{:S(2)}) copy-start(bf16[3,2,640,128]{3,2,1,0:T(8,128)(2,1)S(1)} %collective-permute-done.2.bnd_ref.refs_3_) | copy-start | bytes 2949124
  40.0 19.8 %copy-start.2 = (bf16[4,640,128]{2,1,0:T(8,128)(2,1)S(1)}, bf16[4,640,128]{2,1,0:T(8,128)(2,1)}, u32[]{:S(2)}) copy-start(bf16[4,640,128]{2,1,0:T(8,128)(2,1)} %copy-done.1) | copy-start | bytes 1966084
  40.0 19.8 %copy-start.4 = (bf16[3,2,640,128]{3,2,1,0:T(8,128)(2,1)S(1)}, bf16[3,2,640,128]{3,2,1,0:T(8,128)(2,1)}, u32[]{:S(2)}) copy-start(bf16[3,2,640,128]{3,2,1,0:T(8,128)(2,1)} %copy-done.3) | copy-start | bytes 2949124
  43.0 35.9 %all-to-all-start.1 = ((f32[64,1,32,128]{3,2,1,0:T(8,128)}), f32[64,1,32,128]{3,2,1,0:T(8,128)}, u32[]{:S(2)}, u32[]{:S(2)}) async-start(f32[64,1,32,128]{3,2,1,0:T(8,128)} %bitcast.31), calls=%async_computation.1 | async-start | bytes 2097152 | tf_op jit(solution)/shard_map/all_to_all | solution.py:189
  59.8 1.2 %copy-start.5 = (bf16[3,3,3,128,128]{4,3,2,1,0:T(8,128)(2,1)S(1)}, bf16[3,3,3,128,128]{4,3,2,1,0:T(8,128)(2,1)}, u32[]{:S(2)}) copy-start(bf16[3,3,3,128,128]{4,3,2,1,0:T(8,128)(2,1)} %param.6) | copy-start | bytes 2654212
  60.9 1.1 %copy-start.7 = (bf16[4,1,640,128]{3,2,1,0:T(8,128)(2,1)S(1)}, bf16[4,1,640,128]{3,2,1,0:T(8,128)(2,1)}, u32[]{:S(2)}) copy-start(bf16[4,1,640,128]{3,2,1,0:T(8,128)(2,1)} %param.4) | copy-start | bytes 1966084

commit v14 on v12

--- a/solution.py
+++ b/solution.py
@@ -154,7 +154,13 @@
     for axis in order:
         count = lax.axis_size(axis)
         shaped = part.reshape((count, part.shape[0] // count) + part.shape[1:])
-        part = lax.all_to_all(shaped, axis, 0, 0, tiled=True).sum(0)
+        if count == 2 and not isinstance(axis, tuple):
+            first = lax.axis_index(axis) == 0
+            kept = jnp.where(first, shaped[0], shaped[1])
+            sent = jnp.where(first, shaped[1], shaped[0])
+            part = kept + lax.ppermute(sent, axis, [(0, 1), (1, 0)])
+        else:
+            part = lax.all_to_all(shaped, axis, 0, 0, tiled=True).sum(0)
     return part[0]
 
 

time: 78.3 us -> 79.3 us (1.013)
  blocking collectives: 41 us -> 35.6 us
  waiting for transfers between devices: 16 us -> 18.7 us
  local copies, waits for them, and re-layouts: 3.6 us -> 5.84 us
  other arithmetic: 0.47 us -> 1.72 us
    all_to_all x2 -> x1, blocking collectives: 41 us -> 35.6 us  [reduce_blocks(): part = lax.all_to_all(shaped, axis, 0, 0, tiled=True).sum(0)]
    ppermute x0 -> x1, waiting for transfers between devices: none -> 2.52 us  [reduce_blocks(): part = kept + lax.ppermute(sent, axis, [(0, 1), (1, 0)])]
    unnamed x6, local copies, waits for them, and re-layouts: 0.01 us -> 2.26 us
    another operation x1, other arithmetic: 0.11 us -> 1.07 us  [body(): jnp.stack([above[:2], own[:2], below[:2]])]
  transfers between devices with their start and end apart: 3 -> 4, of which waited for: 3 -> 4; matrix products, arithmetic and copies ran while one was open for 1% -> 1% of each run, Pallas kernels for 0% -> 0%
where the time goes in v14:
time: 79.3 us; the launch traced here: 79 us
  blocking collectives  35.6 us (45%)
  waiting for transfers between devices  18.7 us (24%)
  Pallas kernels  8.93 us (11%)
  starting transfers between devices  7.51 us (9%)
  local copies, waits for them, and re-layouts  5.84 us (7%)
  other arithmetic  1.72 us (2%)
    all_to_all x1, blocking collectives, reduce_blocks(): part = lax.all_to_all(shaped, axis, 0, 0, tiled=True).sum(0)  35.6 us
    ppermute x2, waiting for transfers between devices, row_neighbours(): return (lax.ppermute(x, axis, up), lax.ppermute(x, axis, down))  12.8 us
    pallas_call x1, Pallas kernels, local_grads(): pl.pallas_call(lambda *refs: local_kernel(factor, *refs), out_shape=(jax....  8.93 us
    ppermute x2, starting transfers between devices, row_neighbours(): return (lax.ppermute(x, axis, up), lax.ppermute(x, axis, down))  6.01 us
    ppermute x1, waiting for transfers between devices, passed_along(): return lax.ppermute(block, axis, route)  3.36 us
    ppermute x1, waiting for transfers between devices, reduce_blocks(): part = kept + lax.ppermute(sent, axis, [(0, 1), (1, 0)])  2.52 us
    unnamed x6, local copies, waits for them, and re-layouts  2.26 us
  transfers between devices with their start and end apart: 4, of which 4 were waited for; matrix products, arithmetic and copies ran while one was open for 1% of the time, Pallas kernels for 0%

profile of v14, /device:TPU:0, one launch (start us, length us, event | category | flops | bytes accessed | tf_op | source)
XLA Modules:
  0.0 79.0 jit_solution(14487131491162773100)
XLA Ops:
  0.6 0.0 copy-start
  0.6 1.4 %collective-permute-start.1 = (bf16[4,640,128]{2,1,0:T(8,128)(2,1)}, bf16[4,640,128]{2,1,0:T(8,128)(2,1)S(1)}, u32[]{:S(2)}, u32[]{:S(2)}) collective-permute-start(bf16[4,640,128]{2,1,0:T(8,128)(2,1)} %bitcast.30), channel_id=1, source_target_pairs={{2,0},{4,2},{6,4},{8,6},{10,8},{12,10},{14,12},{16,14},{18,16},{20... | collective-permute-start | bytes 1966088 | tf_op jit(solution)/shard_map/ppermute | solution.py:118
  2.1 4.6 %collective-permute-start = (bf16[4,640,128]{2,1,0:T(8,128)(2,1)}, bf16[4,640,128]{2,1,0:T(8,128)(2,1)S(1)}, u32[]{:S(2)}, u32[]{:S(2)}) collective-permute-start(bf16[4,640,128]{2,1,0:T(8,128)(2,1)} %bitcast.31), channel_id=1, source_target_pairs={{0,2},{2,4},{4,6},{6,8},{8,10},{10,12},{12,14},{14,16},{16,18},{18... | collective-permute-start | bytes 1966088 | tf_op jit(solution)/shard_map/ppermute | solution.py:118
  6.7 1.0 %slice_bitcast_fusion.1 = bf16[1,2,640,128]{3,2,1,0:T(8,128)(2,1)S(1)} fusion(bf16[4,1,640,128]{3,2,0,1:T(8,128)(2,1)} %bitcast.32), kind=kLoop, calls=%fused_computation.5 | loop fusion | bytes 655360 | tf_op jit(solution)/shard_map/stack | solution.py:125
  7.7 11.5 %collective-permute-done.1.refs_2_ = bf16[4,640,128]{2,1,0:T(8,128)(2,1)S(1)} collective-permute-done((bf16[4,640,128]{2,1,0:T(8,128)(2,1)}, bf16[4,640,128]{2,1,0:T(8,128)(2,1)S(1)}, u32[]{:S(2)}, u32[]{:S(2)}) %collective-permute-start.1) | collective-permute-done | bytes 655392 | tf_op jit(solution)/shard_map/ppermute | solution.py:118
  19.2 1.3 %collective-permute-done.refs_1_ = bf16[4,640,128]{2,1,0:T(8,128)(2,1)S(1)} collective-permute-done((bf16[4,640,128]{2,1,0:T(8,128)(2,1)}, bf16[4,640,128]{2,1,0:T(8,128)(2,1)S(1)}, u32[]{:S(2)}, u32[]{:S(2)}) %collective-permute-start) | collective-permute-done | bytes 655392 | tf_op jit(solution)/shard_map/ppermute | solution.py:118
  20.5 1.1 %pad_maximum_fusion = bf16[3,2,640,128]{3,2,1,0:T(8,128)(2,1)} fusion(bf16[1,2,640,128]{3,2,1,0:T(8,128)(2,1)S(1)} %slice_bitcast_fusion, bf16[1,2,640,128]{3,2,1,0:T(8,128)(2,1)S(1)} %slice_bitcast_fusion.1, bf16[1,2,640,128]{3,2,1,0:T(8,128)(2,1)S(1)} %slice_bitcast_fusion.2), kind=kLoop, calls=%fused_computation.3 | loop fusion | flops 983040 | bytes 1966080 | tf_op jit(solution)/shard_map/stack | solution.py:125
  21.6 1.3 %collective-permute-start.2 = (bf16[3,2,640,128]{3,2,1,0:T(8,128)(2,1)}, bf16[3,2,640,128]{3,2,1,0:T(8,128)(2,1)S(1)}, u32[]{:S(2)}, u32[]{:S(2)}) collective-permute-start(bf16[3,2,640,128]{3,2,1,0:T(8,128)(2,1)} %pad_maximum_fusion), channel_id=1, source_target_pairs={{1,0},{3,2},{5,4},{7,6},{9,8},{11,10},{13,12},{15,14},{17,16},{19,... | collective-permute-start | bytes 2949128 | tf_op jit(solution)/shard_map/ppermute | solution.py:16
  22.9 3.4 %collective-permute-done.2.refs_3_ = bf16[3,2,640,128]{3,2,1,0:T(8,128)(2,1)S(1)} collective-permute-done((bf16[3,2,640,128]{3,2,1,0:T(8,128)(2,1)}, bf16[3,2,640,128]{3,2,1,0:T(8,128)(2,1)S(1)}, u32[]{:S(2)}, u32[]{:S(2)}) %collective-permute-start.2) | collective-permute-done | bytes 983072 | tf_op jit(solution)/shard_map/ppermute | solution.py:16
  26.3 0.0 copy-done
  26.3 0.0 copy-start.1
  26.3 1.2 %copy-done.1 = bf16[3,3,3,128,128]{4,3,2,1,0:T(8,128)(2,1)S(1)} copy-done((bf16[3,3,3,128,128]{4,3,2,1,0:T(8,128)(2,1)S(1)}, bf16[3,3,3,128,128]{4,3,2,1,0:T(8,128)(2,1)}, u32[]{:S(2)}) %copy-start.1) | copy-done | bytes 884760
  27.4 0.0 copy-start.2
  27.4 1.1 %copy-done.2 = bf16[4,1,640,128]{3,2,1,0:T(8,128)(2,1)S(1)} copy-done((bf16[4,1,640,128]{3,2,1,0:T(8,128)(2,1)S(1)}, bf16[4,1,640,128]{3,2,1,0:T(8,128)(2,1)}, u32[]{:S(2)}) %copy-start.2) | copy-done | bytes 655384
  28.5 8.9 %shard_map.67 = (bf16[4,640,128]{2,1,0:T(8,128)(2,1)}, f32[9,384,128]{2,1,0:T(8,128)}) custom-call(bf16[4,640,128]{2,1,0:T(8,128)(2,1)S(1)} %bitcast.33, bf16[4,640,128]{2,1,0:T(8,128)(2,1)S(1)} %collective-permute-done.refs_1_, bf16[4,640,128]{2,1,0:T(8,128)(2,1)S(1)} %collective-permute-done.1.refs_2_, ...), custom_call_target="tpu_custom_call" | custom-call | flops 4529848320 | bytes 6914048 | tf_op jit(solution)/shard_map/pallas_call | solution.py:94
  37.4 1.5 %reshape_reshape.3 = f32[128,27,128]{2,1,0:T(8,128)S(1)} reshape(f32[9,384,128]{2,1,0:T(8,128)} %get-tuple-element.6) | data formatting | bytes 3538944 | tf_op jit(solution)/shard_map/reshape;reshape | solution.py:134
  39.0 0.2 pad.4
  39.1 0.2 copy.13
  39.4 0.2 select_bitcast_fusion
  39.6 0.2 collective-permute-start.3
  39.8 2.5 %collective-permute-done.3 = f32[64,32,128]{2,1,0:T(8,128)S(1)} collective-permute-done((f32[64,32,128]{2,1,0:T(8,128)S(1)}, f32[64,32,128]{2,1,0:T(8,128)S(1)}, u32[]{:S(2)}, u32[]{:S(2)}) %collective-permute-start.3) | collective-permute-done | bytes 1048608 | tf_op jit(solution)/shard_map/ppermute | solution.py:161
  42.3 0.3 fusion
  42.7 35.6 %all_to_all.5 = f32[64,1,32,128]{3,2,1,0:T(8,128)S(1)} all-to-all(f32[64,1,32,128]{3,2,1,0:T(8,128)S(1)} %fusion), channel_id=1, replica_groups=mesh['y'=4,'z'=4,'x'=4,'core'=2] {'y','z','x'}, dimensions={0} | all-to-all | bytes 2097152 | tf_op jit(solution)/shard_map/all_to_all | solution.py:163
  78.3 0.1 reduce_sum.11
  78.4 0.6 slice_bitcast_fusion.3
  (2 shorter events, 0.0 us)
Async XLA Ops:
  0.6 25.6 %copy-start = (bf16[4,1,640,128]{3,2,1,0:T(8,128)(2,1)S(1)}, bf16[4,1,640,128]{3,2,1,0:T(8,128)(2,1)}, u32[]{:S(2)}) copy-start(bf16[4,1,640,128]{3,2,1,0:T(8,128)(2,1)} %param.5) | copy-start | bytes 1966084
  0.6 18.6 %collective-permute-start.1 = (bf16[4,640,128]{2,1,0:T(8,128)(2,1)}, bf16[4,640,128]{2,1,0:T(8,128)(2,1)S(1)}, u32[]{:S(2)}, u32[]{:S(2)}) collective-permute-start(bf16[4,640,128]{2,1,0:T(8,128)(2,1)} %bitcast.30), channel_id=1, source_target_pairs={{2,0},{4,2},{6,4},{8,6},{10,8},{12,10},{14,12},{16,14},{18,16},{20... | collective-permute-start | bytes 1966088 | tf_op jit(solution)/shard_map/ppermute | solution.py:118
  2.1 18.4 %collective-permute-start = (bf16[4,640,128]{2,1,0:T(8,128)(2,1)}, bf16[4,640,128]{2,1,0:T(8,128)(2,1)S(1)}, u32[]{:S(2)}, u32[]{:S(2)}) collective-permute-start(bf16[4,640,128]{2,1,0:T(8,128)(2,1)} %bitcast.31), channel_id=1, source_target_pairs={{0,2},{2,4},{4,6},{6,8},{8,10},{10,12},{12,14},{14,16},{16,18},{18... | collective-permute-start | bytes 1966088 | tf_op jit(solution)/shard_map/ppermute | solution.py:118
  21.6 4.7 %collective-permute-start.2 = (bf16[3,2,640,128]{3,2,1,0:T(8,128)(2,1)}, bf16[3,2,640,128]{3,2,1,0:T(8,128)(2,1)S(1)}, u32[]{:S(2)}, u32[]{:S(2)}) collective-permute-start(bf16[3,2,640,128]{3,2,1,0:T(8,128)(2,1)} %pad_maximum_fusion), channel_id=1, source_target_pairs={{1,0},{3,2},{5,4},{7,6},{9,8},{11,10},{13,12},{15,14},{17,16},{19,... | collective-permute-start | bytes 2949128 | tf_op jit(solution)/shard_map/ppermute | solution.py:16
  26.3 1.2 %copy-start.1 = (bf16[3,3,3,128,128]{4,3,2,1,0:T(8,128)(2,1)S(1)}, bf16[3,3,3,128,128]{4,3,2,1,0:T(8,128)(2,1)}, u32[]{:S(2)}) copy-start(bf16[3,3,3,128,128]{4,3,2,1,0:T(8,128)(2,1)} %param.6) | copy-start | bytes 2654212
  27.4 1.1 %copy-start.2 = (bf16[4,1,640,128]{3,2,1,0:T(8,128)(2,1)S(1)}, bf16[4,1,640,128]{3,2,1,0:T(8,128)(2,1)}, u32[]{:S(2)}) copy-start(bf16[4,1,640,128]{3,2,1,0:T(8,128)(2,1)} %param.4) | copy-start | bytes 1966084
  39.6 2.7 %collective-permute-start.3 = (f32[64,32,128]{2,1,0:T(8,128)S(1)}, f32[64,32,128]{2,1,0:T(8,128)S(1)}, u32[]{:S(2)}, u32[]{:S(2)}) collective-permute-start(f32[64,32,128]{2,1,0:T(8,128)S(1)} %select_bitcast_fusion), channel_id=1, source_target_pairs={{0,1},{1,0},{2,3},{3,2},{4,5},{5,4},{6,7},{7,6},{8,9},{9,8},{10,11... | collective-permute-start | bytes 3145736 | tf_op jit(solution)/shard_map/ppermute | solution.py:161

commit v15 on v12

--- a/solution.py
+++ b/solution.py
@@ -132,7 +132,8 @@
     rows = term.shape[0] // owners
     padded = -(-rows // 8) * 8
     term = jnp.pad(term.reshape(owners, rows, channels), ((0, 0), (0, padded - rows), (0, 0)))
-    return (grad_features[:, None], term[None])
+    total = lax.all_to_all(term, ("ha", "ta"), 0, 0, tiled=True).sum(0)
+    return (grad_features[:, None], total[:rows])
 
 
 def physical_mesh(mesh):
@@ -160,47 +161,10 @@
 
 def solution(mesh):
     placed = (P("ta", "ha", None, None), P("ta", "ha", None, None), P())
-    local = jax.shard_map(
+    return jax.shard_map(
         body,
         mesh=mesh,
         in_specs=placed,
-        out_specs=(P("ta", "ha", None, None), P(("ha", "ta"))),
+        out_specs=(P("ta", "ha", None, None), P(("ha", "ta"), None)),
         check_vma=False,
     )
-    grid = physical_mesh(mesh)
-    order = ("core", "y", "z", "x")
-    stages = ("core", PHYSICAL)
-    names = PHYSICAL + ("core",)
-    sizes = [grid.shape[a] for a in names]
-
-    def reorder(term):
-        n, owners, padded, channels = term.shape
-        t = term.reshape((n,) + tuple(sizes) + (padded, channels))
-        perm = [0] + [1 + names.index(a) for a in order] + [5, 6]
-        return t.transpose(perm).reshape(n, owners, padded, channels)
-
-    def reduce_fn(term):
-        rows = 27
-        return reduce_blocks(term, order)
-
-    rows_per = None
-
-    def run(features, cotangent, kernel):
-        grad_features, term = local(features, cotangent, kernel)
-        channels = kernel.shape[-1]
-        owners = term.shape[1]
-        taps_rows = kernel.shape[0] * kernel.shape[1] * kernel.shape[2] * kernel.shape[3]
-        rows = taps_rows // owners
-        term = reorder(term)
-        spec = P(names)
-        part = jax.shard_map(
-            lambda t: reduce_blocks(t, stages)[:rows],
-            mesh=grid,
-            in_specs=spec,
-            out_specs=P(names),
-            check_vma=False,
-        )(term)
-        part = lax.with_sharding_constraint(part, NamedSharding(mesh, P(("ha", "ta"), None)))
-        return grad_features, part
-
-    return run

time: 78.3 us -> 83.6 us (1.068)
  blocking collectives: 41 us -> 46.3 us
  local copies, waits for them, and re-layouts: 3.6 us -> 2.75 us
    all_to_all x2 -> x1, blocking collectives: 41 us -> 46.3 us  [body(): total = lax.all_to_all(term, ('ha', 'ta'), 0, 0, tiled=True).sum(0)]
where the time goes in v15:
time: 83.6 us; the launch traced here: 82.9 us
  blocking collectives  46.3 us (55%)
  waiting for transfers between devices  16 us (19%)
  Pallas kernels  8.94 us (11%)
  starting transfers between devices  7.3 us (9%)
  local copies, waits for them, and re-layouts  2.75 us (3%)
  other arithmetic  0.9 us (1%)
    all_to_all x1, blocking collectives, body(): total = lax.all_to_all(term, ('ha', 'ta'), 0, 0, tiled=True).sum(0)  46.3 us
    ppermute x2, waiting for transfers between devices, row_neighbours(): return (lax.ppermute(x, axis, up), lax.ppermute(x, axis, down))  12.8 us
    pallas_call x1, Pallas kernels, local_grads(): pl.pallas_call(lambda *refs: local_kernel(factor, *refs), out_shape=(jax....  8.94 us
    ppermute x2, starting transfers between devices, row_neighbours(): return (lax.ppermute(x, axis, up), lax.ppermute(x, axis, down))  6.01 us
    ppermute x1, waiting for transfers between devices, passed_along(): return lax.ppermute(block, axis, route)  3.16 us
  transfers between devices with their start and end apart: 3, of which 3 were waited for; matrix products, arithmetic and copies ran while one was open for 1% of the time, Pallas kernels for 0%

profile of v15, /device:TPU:0, one launch (start us, length us, event | category | flops | bytes accessed | tf_op | source)
XLA Modules:
  0.0 82.9 jit_solution(13026414214776434998)
XLA Ops:
  0.6 0.0 copy-start
  0.6 0.0 copy-start.1
  0.6 0.0 copy-start.2
  0.7 1.4 %collective-permute-start.1 = (bf16[4,640,128]{2,1,0:T(8,128)(2,1)}, bf16[4,640,128]{2,1,0:T(8,128)(2,1)S(1)}, u32[]{:S(2)}, u32[]{:S(2)}) collective-permute-start(bf16[4,640,128]{2,1,0:T(8,128)(2,1)} %bitcast.14), channel_id=1, source_target_pairs={{2,0},{4,2},{6,4},{8,6},{10,8},{12,10},{14,12},{16,14},{18,16},{20... | collective-permute-start | bytes 1966088 | tf_op jit(solution)/shard_map/ppermute | solution.py:118
  2.1 4.6 %collective-permute-start = (bf16[4,640,128]{2,1,0:T(8,128)(2,1)}, bf16[4,640,128]{2,1,0:T(8,128)(2,1)S(1)}, u32[]{:S(2)}, u32[]{:S(2)}) collective-permute-start(bf16[4,640,128]{2,1,0:T(8,128)(2,1)} %bitcast.15), channel_id=1, source_target_pairs={{0,2},{2,4},{4,6},{6,8},{8,10},{10,12},{12,14},{14,16},{16,18},{18... | collective-permute-start | bytes 1966088 | tf_op jit(solution)/shard_map/ppermute | solution.py:118
  6.7 1.0 %slice_bitcast_fusion.1 = bf16[1,2,640,128]{3,2,1,0:T(8,128)(2,1)S(1)} fusion(bf16[4,1,640,128]{3,2,0,1:T(8,128)(2,1)} %bitcast.16), kind=kLoop, calls=%fused_computation.2 | loop fusion | bytes 655360 | tf_op jit(solution)/shard_map/stack | solution.py:125
  7.7 11.5 %collective-permute-done.1.refs_2_ = bf16[4,640,128]{2,1,0:T(8,128)(2,1)S(1)} collective-permute-done((bf16[4,640,128]{2,1,0:T(8,128)(2,1)}, bf16[4,640,128]{2,1,0:T(8,128)(2,1)S(1)}, u32[]{:S(2)}, u32[]{:S(2)}) %collective-permute-start.1) | collective-permute-done | bytes 655392 | tf_op jit(solution)/shard_map/ppermute | solution.py:118
  19.3 1.3 %collective-permute-done.refs_1_ = bf16[4,640,128]{2,1,0:T(8,128)(2,1)S(1)} collective-permute-done((bf16[4,640,128]{2,1,0:T(8,128)(2,1)}, bf16[4,640,128]{2,1,0:T(8,128)(2,1)S(1)}, u32[]{:S(2)}, u32[]{:S(2)}) %collective-permute-start) | collective-permute-done | bytes 655392 | tf_op jit(solution)/shard_map/ppermute | solution.py:118
  20.5 0.1 pad_maximum_fusion
  20.7 1.3 %collective-permute-start.2 = (bf16[3,2,640,128]{3,2,1,0:T(8,128)(2,1)S(1)}, bf16[3,2,640,128]{3,2,1,0:T(8,128)(2,1)S(1)}, u32[]{:S(2)}, u32[]{:S(2)}) collective-permute-start(bf16[3,2,640,128]{3,2,1,0:T(8,128)(2,1)S(1)} %pad_maximum_fusion), channel_id=1, source_target_pairs={{1,0},{3,2},{5,4},{7,6},{9,8},{11,10},{13,12},{15,14},{17,16},{19,... | collective-permute-start | bytes 2949128 | tf_op jit(solution)/shard_map/ppermute | solution.py:16
  22.0 3.2 %collective-permute-done.2.refs_3_ = bf16[3,2,640,128]{3,2,1,0:T(8,128)(2,1)S(1)} collective-permute-done((bf16[3,2,640,128]{3,2,1,0:T(8,128)(2,1)S(1)}, bf16[3,2,640,128]{3,2,1,0:T(8,128)(2,1)S(1)}, u32[]{:S(2)}, u32[]{:S(2)}) %collective-permute-start.2) | collective-permute-done | bytes 983072 | tf_op jit(solution)/shard_map/ppermute | solution.py:16
  25.1 0.0 copy-done
  25.1 0.0 copy-done.1
  25.1 0.0 copy-done.2
  25.1 8.9 %shard_map.50 = (bf16[4,640,128]{2,1,0:T(8,128)(2,1)}, f32[9,384,128]{2,1,0:T(8,128)}) custom-call(bf16[4,640,128]{2,1,0:T(8,128)(2,1)S(1)} %bitcast.17, bf16[4,640,128]{2,1,0:T(8,128)(2,1)S(1)} %collective-permute-done.refs_1_, bf16[4,640,128]{2,1,0:T(8,128)(2,1)S(1)} %collective-permute-done.1.refs_2_, ...), custom_call_target="tpu_custom_call" | custom-call | flops 4529848320 | bytes 6914048 | tf_op jit(solution)/shard_map/pallas_call | solution.py:94
  34.1 1.5 %reshape_reshape.3 = f32[128,27,128]{2,1,0:T(8,128)S(1)} reshape(f32[9,384,128]{2,1,0:T(8,128)} %get-tuple-element.5) | data formatting | bytes 3538944 | tf_op jit(solution)/shard_map/reshape;reshape | solution.py:134
  35.6 0.2 pad.4
  35.8 46.3 %all_to_all.5 = f32[128,32,128]{2,1,0:T(8,128)S(1)} all-to-all(f32[128,32,128]{2,1,0:T(8,128)S(1)} %pad.4), channel_id=1, replica_groups=mesh['ha'=64,'ta'=2] {'ha','ta'}, dimensions={0} | all-to-all | bytes 4194304 | tf_op jit(solution)/shard_map/all_to_all | solution.py:135
  82.1 0.8 reduce_sum.9
  (2 shorter events, 0.0 us)
Async XLA Ops:
  0.6 24.5 %copy-start = (bf16[4,1,640,128]{3,2,1,0:T(8,128)(2,1)S(1)}, bf16[4,1,640,128]{3,2,1,0:T(8,128)(2,1)}, u32[]{:S(2)}) copy-start(bf16[4,1,640,128]{3,2,1,0:T(8,128)(2,1)} %param.4) | copy-start | bytes 1966084
  0.6 24.5 %copy-start.1 = (bf16[3,3,3,128,128]{4,3,2,1,0:T(8,128)(2,1)S(1)}, bf16[3,3,3,128,128]{4,3,2,1,0:T(8,128)(2,1)}, u32[]{:S(2)}) copy-start(bf16[3,3,3,128,128]{4,3,2,1,0:T(8,128)(2,1)} %param.5) | copy-start | bytes 2654212
  0.6 24.5 %copy-start.2 = (bf16[4,1,640,128]{3,2,1,0:T(8,128)(2,1)S(1)}, bf16[4,1,640,128]{3,2,1,0:T(8,128)(2,1)}, u32[]{:S(2)}) copy-start(bf16[4,1,640,128]{3,2,1,0:T(8,128)(2,1)} %param.3) | copy-start | bytes 1966084
  0.7 18.6 %collective-permute-start.1 = (bf16[4,640,128]{2,1,0:T(8,128)(2,1)}, bf16[4,640,128]{2,1,0:T(8,128)(2,1)S(1)}, u32[]{:S(2)}, u32[]{:S(2)}) collective-permute-start(bf16[4,640,128]{2,1,0:T(8,128)(2,1)} %bitcast.14), channel_id=1, source_target_pairs={{2,0},{4,2},{6,4},{8,6},{10,8},{12,10},{14,12},{16,14},{18,16},{20... | collective-permute-start | bytes 1966088 | tf_op jit(solution)/shard_map/ppermute | solution.py:118
  2.1 18.4 %collective-permute-start = (bf16[4,640,128]{2,1,0:T(8,128)(2,1)}, bf16[4,640,128]{2,1,0:T(8,128)(2,1)S(1)}, u32[]{:S(2)}, u32[]{:S(2)}) collective-permute-start(bf16[4,640,128]{2,1,0:T(8,128)(2,1)} %bitcast.15), channel_id=1, source_target_pairs={{0,2},{2,4},{4,6},{6,8},{8,10},{10,12},{12,14},{14,16},{16,18},{18... | collective-permute-start | bytes 1966088 | tf_op jit(solution)/shard_map/ppermute | solution.py:118
  20.7 4.5 %collective-permute-start.2 = (bf16[3,2,640,128]{3,2,1,0:T(8,128)(2,1)S(1)}, bf16[3,2,640,128]{3,2,1,0:T(8,128)(2,1)S(1)}, u32[]{:S(2)}, u32[]{:S(2)}) collective-permute-start(bf16[3,2,640,128]{3,2,1,0:T(8,128)(2,1)S(1)} %pad_maximum_fusion), channel_id=1, source_target_pairs={{1,0},{3,2},{5,4},{7,6},{9,8},{11,10},{13,12},{15,14},{17,16},{19,... | collective-permute-start | bytes 2949128 | tf_op jit(solution)/shard_map/ppermute | solution.py:16

commit v16 on v14

--- a/solution.py
+++ b/solution.py
@@ -29,8 +29,13 @@
     return x
 
 
-def local_kernel(factor, own_ref, up_ref, down_ref, bnd_ref, k_ref, feat_ref, gf_ref, term_ref, z_ref, a_ref, w_ref, cat_ref, acc_ref):
+def local_kernel(factor, own_ref, up_ref, down_ref, bnd_ref, k_hbm, feat_hbm, gf_ref, term_ref, z_ref, a_ref, w_ref, cat_ref, acc_ref, k_ref, feat_ref, sems):
     frames, breadth, channels = feat_ref.shape
+    feat_copy = pltpu.make_async_copy(feat_hbm, feat_ref, sems.at[0])
+    k_copy = pltpu.make_async_copy(k_hbm, k_ref, sems.at[1])
+    feat_copy.start()
+    k_copy.start()
+    feat_copy.wait()
 
     def slab(frame, row):
         if frame < frames:
@@ -40,10 +45,6 @@
     def block(n):
         return slice(n * channels, (n + 1) * channels)
 
-    for i in range(3):
-        for j in range(3):
-            for k in range(3):
-                w_ref[j, block(k), block(i)] = k_ref[(i * 3 + j) * 3 + k]
     lanes = lax.broadcasted_iota(jnp.int32, (channels, breadth), 1)
     for t in range(frames):
         values = feat_ref[t].astype(jnp.float32)
@@ -54,6 +55,11 @@
         a_ref[t, block(2)] = jnp.where(
             lanes == breadth - 1, 0.0, pltpu.roll(turned, breadth - 1, 1)
         ).astype(a_ref.dtype)
+    k_copy.wait()
+    for i in range(3):
+        for j in range(3):
+            for k in range(3):
+                w_ref[j, block(k), block(i)] = k_ref[(i * 3 + j) * 3 + k]
     acc_ref[...] = jnp.zeros_like(acc_ref)
     rows = lax.broadcasted_iota(jnp.int32, (breadth, channels), 0)
     for t in range(frames):
@@ -97,7 +103,7 @@
             jax.ShapeDtypeStruct((frames, breadth, channels), jnp.bfloat16),
             jax.ShapeDtypeStruct((9, 3 * channels, channels), jnp.float32),
         ),
-        in_specs=[vmem] * len(operands),
+        in_specs=[vmem] * len(pieces) + [pl.BlockSpec(memory_space=pl.ANY)] * 2,
         out_specs=(vmem, vmem),
         scratch_shapes=[
             pltpu.VMEM((breadth, 3 * channels), jnp.float32),
@@ -105,6 +111,9 @@
             pltpu.VMEM((3, 3 * channels, 3 * channels), jnp.bfloat16),
             pltpu.VMEM((breadth, 3 * channels), jnp.bfloat16),
             pltpu.VMEM((3, 3 * channels, 3 * channels), jnp.float32),
+            pltpu.VMEM(weights.shape, weights.dtype),
+            pltpu.VMEM(feat.shape, feat.dtype),
+            pltpu.SemaphoreType.DMA((2,)),
         ],
         compiler_params=pltpu.CompilerParams(vmem_limit_bytes=48 * 1024 * 1024),
         cost_estimate=pl.CostEstimate(flops=flops, bytes_accessed=moved, transcendentals=2 * feat.size),

time: 79.3 us -> 80.1 us (1.010)
  no operation moved by 1% of the time
where the time goes in v16:
time: 80.1 us; the launch traced here: 79.8 us
  blocking collectives  35.6 us (44%)
  waiting for transfers between devices  18.7 us (23%)
  Pallas kernels  9.71 us (12%)
  starting transfers between devices  7.51 us (9%)
  local copies, waits for them, and re-layouts  5.85 us (7%)
  other arithmetic  1.72 us (2%)
    all_to_all x1, blocking collectives, reduce_blocks(): part = lax.all_to_all(shaped, axis, 0, 0, tiled=True).sum(0)  35.6 us
    ppermute x2, waiting for transfers between devices, row_neighbours(): return (lax.ppermute(x, axis, up), lax.ppermute(x, axis, down))  12.8 us
    pallas_call x1, Pallas kernels, local_grads(): pl.pallas_call(lambda *refs: local_kernel(factor, *refs), out_shape=(jax....  9.71 us
    ppermute x2, starting transfers between devices, row_neighbours(): return (lax.ppermute(x, axis, up), lax.ppermute(x, axis, down))  6.01 us
    ppermute x1, waiting for transfers between devices, passed_along(): return lax.ppermute(block, axis, route)  3.36 us
    ppermute x1, waiting for transfers between devices, reduce_blocks(): part = kept + lax.ppermute(sent, axis, [(0, 1), (1, 0)])  2.52 us
    unnamed x6, local copies, waits for them, and re-layouts  2.26 us
  transfers between devices with their start and end apart: 4, of which 4 were waited for; matrix products, arithmetic and copies ran while one was open for 1% of the time, Pallas kernels for 0%

profile of v16, /device:TPU:0, one launch (start us, length us, event | category | flops | bytes accessed | tf_op | source)
XLA Modules:
  0.0 79.8 jit_solution(6365483119150895711)
XLA Ops:
  0.6 0.0 copy-start
  0.6 1.4 %collective-permute-start.1 = (bf16[4,640,128]{2,1,0:T(8,128)(2,1)}, bf16[4,640,128]{2,1,0:T(8,128)(2,1)S(1)}, u32[]{:S(2)}, u32[]{:S(2)}) collective-permute-start(bf16[4,640,128]{2,1,0:T(8,128)(2,1)} %bitcast.30), channel_id=1, source_target_pairs={{2,0},{4,2},{6,4},{8,6},{10,8},{12,10},{14,12},{16,14},{18,16},{20... | collective-permute-start | bytes 1966088 | tf_op jit(solution)/shard_map/ppermute | solution.py:127
  2.1 4.6 %collective-permute-start = (bf16[4,640,128]{2,1,0:T(8,128)(2,1)}, bf16[4,640,128]{2,1,0:T(8,128)(2,1)S(1)}, u32[]{:S(2)}, u32[]{:S(2)}) collective-permute-start(bf16[4,640,128]{2,1,0:T(8,128)(2,1)} %bitcast.31), channel_id=1, source_target_pairs={{0,2},{2,4},{4,6},{6,8},{8,10},{10,12},{12,14},{14,16},{16,18},{18... | collective-permute-start | bytes 1966088 | tf_op jit(solution)/shard_map/ppermute | solution.py:127
  6.7 1.0 %slice_bitcast_fusion.1 = bf16[1,2,640,128]{3,2,1,0:T(8,128)(2,1)S(1)} fusion(bf16[4,1,640,128]{3,2,0,1:T(8,128)(2,1)} %bitcast.32), kind=kLoop, calls=%fused_computation.5 | loop fusion | bytes 655360 | tf_op jit(solution)/shard_map/stack | solution.py:134
  7.7 11.5 %collective-permute-done.1.refs_2_ = bf16[4,640,128]{2,1,0:T(8,128)(2,1)S(1)} collective-permute-done((bf16[4,640,128]{2,1,0:T(8,128)(2,1)}, bf16[4,640,128]{2,1,0:T(8,128)(2,1)S(1)}, u32[]{:S(2)}, u32[]{:S(2)}) %collective-permute-start.1) | collective-permute-done | bytes 655392 | tf_op jit(solution)/shard_map/ppermute | solution.py:127
  19.2 1.3 %collective-permute-done.refs_1_ = bf16[4,640,128]{2,1,0:T(8,128)(2,1)S(1)} collective-permute-done((bf16[4,640,128]{2,1,0:T(8,128)(2,1)}, bf16[4,640,128]{2,1,0:T(8,128)(2,1)S(1)}, u32[]{:S(2)}, u32[]{:S(2)}) %collective-permute-start) | collective-permute-done | bytes 655392 | tf_op jit(solution)/shard_map/ppermute | solution.py:127
  20.5 1.1 %pad_maximum_fusion = bf16[3,2,640,128]{3,2,1,0:T(8,128)(2,1)} fusion(bf16[1,2,640,128]{3,2,1,0:T(8,128)(2,1)S(1)} %slice_bitcast_fusion, bf16[1,2,640,128]{3,2,1,0:T(8,128)(2,1)S(1)} %slice_bitcast_fusion.1, bf16[1,2,640,128]{3,2,1,0:T(8,128)(2,1)S(1)} %slice_bitcast_fusion.2), kind=kLoop, calls=%fused_computation.3 | loop fusion | flops 983040 | bytes 1966080 | tf_op jit(solution)/shard_map/stack | solution.py:134
  21.6 1.3 %collective-permute-start.2 = (bf16[3,2,640,128]{3,2,1,0:T(8,128)(2,1)}, bf16[3,2,640,128]{3,2,1,0:T(8,128)(2,1)S(1)}, u32[]{:S(2)}, u32[]{:S(2)}) collective-permute-start(bf16[3,2,640,128]{3,2,1,0:T(8,128)(2,1)} %pad_maximum_fusion), channel_id=1, source_target_pairs={{1,0},{3,2},{5,4},{7,6},{9,8},{11,10},{13,12},{15,14},{17,16},{19,... | collective-permute-start | bytes 2949128 | tf_op jit(solution)/shard_map/ppermute | solution.py:16
  22.9 3.4 %collective-permute-done.2.refs_3_ = bf16[3,2,640,128]{3,2,1,0:T(8,128)(2,1)S(1)} collective-permute-done((bf16[3,2,640,128]{3,2,1,0:T(8,128)(2,1)}, bf16[3,2,640,128]{3,2,1,0:T(8,128)(2,1)S(1)}, u32[]{:S(2)}, u32[]{:S(2)}) %collective-permute-start.2) | collective-permute-done | bytes 983072 | tf_op jit(solution)/shard_map/ppermute | solution.py:16
  26.3 0.0 copy-done
  26.3 0.0 copy-start.1
  26.3 1.2 %copy-done.1 = bf16[3,3,3,128,128]{4,3,2,1,0:T(8,128)(2,1)S(1)} copy-done((bf16[3,3,3,128,128]{4,3,2,1,0:T(8,128)(2,1)S(1)}, bf16[3,3,3,128,128]{4,3,2,1,0:T(8,128)(2,1)}, u32[]{:S(2)}) %copy-start.1) | copy-done | bytes 884760
  27.4 0.0 copy-start.2
  27.4 1.1 %copy-done.2 = bf16[4,1,640,128]{3,2,1,0:T(8,128)(2,1)S(1)} copy-done((bf16[4,1,640,128]{3,2,1,0:T(8,128)(2,1)S(1)}, bf16[4,1,640,128]{3,2,1,0:T(8,128)(2,1)}, u32[]{:S(2)}) %copy-start.2) | copy-done | bytes 655384
  28.5 9.7 %shard_map.67 = (bf16[4,640,128]{2,1,0:T(8,128)(2,1)}, f32[9,384,128]{2,1,0:T(8,128)}) custom-call(bf16[4,640,128]{2,1,0:T(8,128)(2,1)S(1)} %bitcast.33, bf16[4,640,128]{2,1,0:T(8,128)(2,1)S(1)} %collective-permute-done.refs_1_, bf16[4,640,128]{2,1,0:T(8,128)(2,1)S(1)} %collective-permute-done.1.refs_2_, ...), custom_call_target="tpu_custom_call" | custom-call | flops 4529848320 | bytes 6914048 | tf_op jit(solution)/shard_map/pallas_call | solution.py:100
  38.2 1.5 %reshape_reshape.3 = f32[128,27,128]{2,1,0:T(8,128)S(1)} reshape(f32[9,384,128]{2,1,0:T(8,128)} %get-tuple-element.6) | data formatting | bytes 3538944 | tf_op jit(solution)/shard_map/reshape;reshape | solution.py:143
  39.8 0.2 pad.4
  39.9 0.2 copy.13
  40.2 0.2 select_bitcast_fusion
  40.4 0.2 collective-permute-start.3
  40.6 2.5 %collective-permute-done.3 = f32[64,32,128]{2,1,0:T(8,128)S(1)} collective-permute-done((f32[64,32,128]{2,1,0:T(8,128)S(1)}, f32[64,32,128]{2,1,0:T(8,128)S(1)}, u32[]{:S(2)}, u32[]{:S(2)}) %collective-permute-start.3) | collective-permute-done | bytes 1048608 | tf_op jit(solution)/shard_map/ppermute | solution.py:170
  43.1 0.3 fusion
  43.5 35.6 %all_to_all.5 = f32[64,1,32,128]{3,2,1,0:T(8,128)S(1)} all-to-all(f32[64,1,32,128]{3,2,1,0:T(8,128)S(1)} %fusion), channel_id=1, replica_groups=mesh['y'=4,'z'=4,'x'=4,'core'=2] {'y','z','x'}, dimensions={0} | all-to-all | bytes 2097152 | tf_op jit(solution)/shard_map/all_to_all | solution.py:172
  79.1 0.1 reduce_sum.11
  79.2 0.6 slice_bitcast_fusion.3
  (2 shorter events, 0.0 us)
Async XLA Ops:
  0.6 25.6 %copy-start = (bf16[4,1,640,128]{3,2,1,0:T(8,128)(2,1)S(1)}, bf16[4,1,640,128]{3,2,1,0:T(8,128)(2,1)}, u32[]{:S(2)}) copy-start(bf16[4,1,640,128]{3,2,1,0:T(8,128)(2,1)} %param.5) | copy-start | bytes 1966084
  0.6 18.6 %collective-permute-start.1 = (bf16[4,640,128]{2,1,0:T(8,128)(2,1)}, bf16[4,640,128]{2,1,0:T(8,128)(2,1)S(1)}, u32[]{:S(2)}, u32[]{:S(2)}) collective-permute-start(bf16[4,640,128]{2,1,0:T(8,128)(2,1)} %bitcast.30), channel_id=1, source_target_pairs={{2,0},{4,2},{6,4},{8,6},{10,8},{12,10},{14,12},{16,14},{18,16},{20... | collective-permute-start | bytes 1966088 | tf_op jit(solution)/shard_map/ppermute | solution.py:127
  2.1 18.4 %collective-permute-start = (bf16[4,640,128]{2,1,0:T(8,128)(2,1)}, bf16[4,640,128]{2,1,0:T(8,128)(2,1)S(1)}, u32[]{:S(2)}, u32[]{:S(2)}) collective-permute-start(bf16[4,640,128]{2,1,0:T(8,128)(2,1)} %bitcast.31), channel_id=1, source_target_pairs={{0,2},{2,4},{4,6},{6,8},{8,10},{10,12},{12,14},{14,16},{16,18},{18... | collective-permute-start | bytes 1966088 | tf_op jit(solution)/shard_map/ppermute | solution.py:127
  21.6 4.7 %collective-permute-start.2 = (bf16[3,2,640,128]{3,2,1,0:T(8,128)(2,1)}, bf16[3,2,640,128]{3,2,1,0:T(8,128)(2,1)S(1)}, u32[]{:S(2)}, u32[]{:S(2)}) collective-permute-start(bf16[3,2,640,128]{3,2,1,0:T(8,128)(2,1)} %pad_maximum_fusion), channel_id=1, source_target_pairs={{1,0},{3,2},{5,4},{7,6},{9,8},{11,10},{13,12},{15,14},{17,16},{19,... | collective-permute-start | bytes 2949128 | tf_op jit(solution)/shard_map/ppermute | solution.py:16
  26.3 1.2 %copy-start.1 = (bf16[3,3,3,128,128]{4,3,2,1,0:T(8,128)(2,1)S(1)}, bf16[3,3,3,128,128]{4,3,2,1,0:T(8,128)(2,1)}, u32[]{:S(2)}) copy-start(bf16[3,3,3,128,128]{4,3,2,1,0:T(8,128)(2,1)} %param.6) | copy-start | bytes 2654212
  27.4 1.1 %copy-start.2 = (bf16[4,1,640,128]{3,2,1,0:T(8,128)(2,1)S(1)}, bf16[4,1,640,128]{3,2,1,0:T(8,128)(2,1)}, u32[]{:S(2)}) copy-start(bf16[4,1,640,128]{3,2,1,0:T(8,128)(2,1)} %param.4) | copy-start | bytes 1966084
  40.4 2.7 %collective-permute-start.3 = (f32[64,32,128]{2,1,0:T(8,128)S(1)}, f32[64,32,128]{2,1,0:T(8,128)S(1)}, u32[]{:S(2)}, u32[]{:S(2)}) collective-permute-start(f32[64,32,128]{2,1,0:T(8,128)S(1)} %select_bitcast_fusion), channel_id=1, source_target_pairs={{0,1},{1,0},{2,3},{3,2},{4,5},{5,4},{6,7},{7,6},{8,9},{9,8},{10,11... | collective-permute-start | bytes 3145736 | tf_op jit(solution)/shard_map/ppermute | solution.py:170

commit v17 on v12

--- a/solution.py
+++ b/solution.py
@@ -130,9 +130,7 @@
     term = term.reshape(-1, channels)
     owners = lax.axis_size("ha") * lax.axis_size("ta")
     rows = term.shape[0] // owners
-    padded = -(-rows // 8) * 8
-    term = jnp.pad(term.reshape(owners, rows, channels), ((0, 0), (0, padded - rows), (0, 0)))
-    return (grad_features[:, None], term[None])
+    return (grad_features[:, None], term.reshape(owners, rows * channels)[None])
 
 
 def physical_mesh(mesh):
@@ -174,10 +172,10 @@
     sizes = [grid.shape[a] for a in names]
 
     def reorder(term):
-        n, owners, padded, channels = term.shape
-        t = term.reshape((n,) + tuple(sizes) + (padded, channels))
-        perm = [0] + [1 + names.index(a) for a in order] + [5, 6]
-        return t.transpose(perm).reshape(n, owners, padded, channels)
+        n, owners = term.shape[:2]
+        t = term.reshape((n,) + tuple(sizes) + term.shape[2:])
+        perm = [0] + [1 + names.index(a) for a in order] + list(range(5, t.ndim))
+        return t.transpose(perm).reshape(term.shape)
 
     def reduce_fn(term):
         rows = 27
@@ -194,7 +192,7 @@
         term = reorder(term)
         spec = P(names)
         part = jax.shard_map(
-            lambda t: reduce_blocks(t, stages)[:rows],
+            lambda t: reduce_blocks(t, stages).reshape(rows, channels),
             mesh=grid,
             in_specs=spec,
             out_specs=P(names),

time: 78.3 us -> 77.6 us (level)
  blocking collectives: 41 us -> 39 us
  other arithmetic: 0.47 us -> 1.56 us
    reshape x0 -> x2, local copies, waits for them, and re-layouts: none -> 2.85 us  [the longest x1 2.24 us: reorder(): t = term.reshape((n,) + tuple(sizes) + term.shape[2:])]
    all_to_all x2, blocking collectives: 41 us -> 39 us  [reduce_blocks(): part = lax.all_to_all(shaped, axis, 0, 0, tiled=True).sum(0)]
    another operation x1, local copies, waits for them, and re-layouts: 1.51 us -> 0.12 us  [reduce_blocks(): shaped = part.reshape((count, part.shape[0] // count) + part.shape[1:])]
    reduce_sum x2, other arithmetic: 0.36 us -> 1.45 us  [reduce_blocks(): part = lax.all_to_all(shaped, axis, 0, 0, tiled=True).sum(0)]
where the time goes in v17:
time: 77.6 us; the launch traced here: 77.3 us
  blocking collectives  39 us (50%)
  waiting for transfers between devices  15.9 us (20%)
  Pallas kernels  8.92 us (11%)
  starting transfers between devices  7.18 us (9%)
  local copies, waits for them, and re-layouts  4.03 us (5%)
  other arithmetic  1.56 us (2%)
    all_to_all x2, blocking collectives, reduce_blocks(): part = lax.all_to_all(shaped, axis, 0, 0, tiled=True).sum(0)  39 us
    ppermute x2, waiting for transfers between devices, row_neighbours(): return (lax.ppermute(x, axis, up), lax.ppermute(x, axis, down))  12.8 us
    pallas_call x1, Pallas kernels, local_grads(): pl.pallas_call(lambda *refs: local_kernel(factor, *refs), out_shape=(jax....  8.92 us
    ppermute x2, starting transfers between devices, row_neighbours(): return (lax.ppermute(x, axis, up), lax.ppermute(x, axis, down))  5.88 us
    ppermute x1, waiting for transfers between devices, passed_along(): return lax.ppermute(block, axis, route)  3.16 us
    reshape x1, local copies, waits for them, and re-layouts, reorder(): t = term.reshape((n,) + tuple(sizes) + term.shape[2:])  2.24 us
  transfers between devices with their start and end apart: 3, of which 3 were waited for; matrix products, arithmetic and copies ran while one was open for 1% of the time, Pallas kernels for 0%

profile of v17, /device:TPU:0, one launch (start us, length us, event | category | flops | bytes accessed | tf_op | source)
XLA Modules:
  0.0 77.3 jit_solution(5078425278881861349)
XLA Ops:
  0.6 1.3 %collective-permute-start.1 = (bf16[4,640,128]{2,1,0:T(8,128)(2,1)}, bf16[4,640,128]{2,1,0:T(8,128)(2,1)S(1)}, u32[]{:S(2)}, u32[]{:S(2)}) collective-permute-start(bf16[4,640,128]{2,1,0:T(8,128)(2,1)} %bitcast.17), channel_id=1, source_target_pairs={{2,0},{4,2},{6,4},{8,6},{10,8},{12,10},{14,12},{16,14},{18,16},{20... | collective-permute-start | bytes 1966088 | tf_op jit(solution)/shard_map/ppermute | solution.py:118
  1.9 4.6 %collective-permute-start = (bf16[4,640,128]{2,1,0:T(8,128)(2,1)}, bf16[4,640,128]{2,1,0:T(8,128)(2,1)S(1)}, u32[]{:S(2)}, u32[]{:S(2)}) collective-permute-start(bf16[4,640,128]{2,1,0:T(8,128)(2,1)} %bitcast.18), channel_id=1, source_target_pairs={{0,2},{2,4},{4,6},{6,8},{8,10},{10,12},{12,14},{14,16},{16,18},{18... | collective-permute-start | bytes 1966088 | tf_op jit(solution)/shard_map/ppermute | solution.py:118
  6.5 1.0 %slice_bitcast_fusion.1 = bf16[1,2,640,128]{3,2,1,0:T(8,128)(2,1)S(1)} fusion(bf16[4,1,640,128]{3,2,0,1:T(8,128)(2,1)} %bitcast.19), kind=kLoop, calls=%fused_computation.2 | loop fusion | bytes 655360 | tf_op jit(solution)/shard_map/stack | solution.py:125
  7.5 0.0 copy-start
  7.6 0.0 copy-start.1
  7.6 0.0 copy-start.2
  7.6 11.5 %collective-permute-done.1.refs_2_ = bf16[4,640,128]{2,1,0:T(8,128)(2,1)S(1)} collective-permute-done((bf16[4,640,128]{2,1,0:T(8,128)(2,1)}, bf16[4,640,128]{2,1,0:T(8,128)(2,1)S(1)}, u32[]{:S(2)}, u32[]{:S(2)}) %collective-permute-start.1) | collective-permute-done | bytes 655392 | tf_op jit(solution)/shard_map/ppermute | solution.py:118
  19.1 1.3 %collective-permute-done.refs_1_ = bf16[4,640,128]{2,1,0:T(8,128)(2,1)S(1)} collective-permute-done((bf16[4,640,128]{2,1,0:T(8,128)(2,1)}, bf16[4,640,128]{2,1,0:T(8,128)(2,1)S(1)}, u32[]{:S(2)}, u32[]{:S(2)}) %collective-permute-start) | collective-permute-done | bytes 655392 | tf_op jit(solution)/shard_map/ppermute | solution.py:118
  20.4 0.1 pad_maximum_fusion
  20.5 1.3 %collective-permute-start.2 = (bf16[3,2,640,128]{3,2,1,0:T(8,128)(2,1)S(1)}, bf16[3,2,640,128]{3,2,1,0:T(8,128)(2,1)S(1)}, u32[]{:S(2)}, u32[]{:S(2)}) collective-permute-start(bf16[3,2,640,128]{3,2,1,0:T(8,128)(2,1)S(1)} %pad_maximum_fusion), channel_id=1, source_target_pairs={{1,0},{3,2},{5,4},{7,6},{9,8},{11,10},{13,12},{15,14},{17,16},{19,... | collective-permute-start | bytes 2949128 | tf_op jit(solution)/shard_map/ppermute | solution.py:16
  21.8 3.2 %collective-permute-done.2.refs_3_ = bf16[3,2,640,128]{3,2,1,0:T(8,128)(2,1)S(1)} collective-permute-done((bf16[3,2,640,128]{3,2,1,0:T(8,128)(2,1)S(1)}, bf16[3,2,640,128]{3,2,1,0:T(8,128)(2,1)S(1)}, u32[]{:S(2)}, u32[]{:S(2)}) %collective-permute-start.2) | collective-permute-done | bytes 983072 | tf_op jit(solution)/shard_map/ppermute | solution.py:16
  25.0 0.0 copy-done
  25.0 0.0 copy-done.1
  25.0 0.0 copy-done.2
  25.0 8.9 %shard_map.67 = (bf16[4,640,128]{2,1,0:T(8,128)(2,1)}, f32[9,384,128]{2,1,0:T(8,128)}) custom-call(bf16[4,640,128]{2,1,0:T(8,128)(2,1)S(1)} %bitcast.20, bf16[4,640,128]{2,1,0:T(8,128)(2,1)S(1)} %collective-permute-done.refs_1_, bf16[4,640,128]{2,1,0:T(8,128)(2,1)S(1)} %collective-permute-done.1.refs_2_, ...), custom_call_target="tpu_custom_call" | custom-call | flops 4529848320 | bytes 6914048 | tf_op jit(solution)/shard_map/pallas_call | solution.py:94
  33.9 2.2 %reshape.20 = f32[1,4,4,4,2,3456]{5,4,3,2,1,0:T(2,128)S(1)} reshape(f32[9,384,128]{2,1,0:T(8,128)} %get-tuple-element.6) | data formatting | bytes 3538944 | tf_op jit(solution)/reshape | solution.py:176
  36.1 0.1 copy.12
  36.3 5.2 %all_to_all.10 = f32[2,64,3456]{2,1,0:T(8,128)S(1)} all-to-all(f32[2,64,3456]{2,1,0:T(8,128)S(1)} %copy.12), channel_id=1, replica_groups=mesh['y'=4,'z'=4,'x'=4,'core'=2] {'core'}, dimensions={0} | all-to-all | bytes 3538944 | tf_op jit(solution)/shard_map/all_to_all | solution.py:155
  41.4 0.2 reduce_sum.18
  41.6 0.6 reshape.23
  42.2 33.8 %all_to_all.11 = f32[64,1,3456]{2,1,0:T(1,128)S(1)} all-to-all(f32[64,1,3456]{2,1,0:T(1,128)S(1)} %reshape.23), channel_id=1, replica_groups=mesh['y'=4,'z'=4,'x'=4,'core'=2] {'y','z','x'}, dimensions={0} | all-to-all | bytes 1769472 | tf_op jit(solution)/shard_map/all_to_all | solution.py:155
  76.1 1.3 %reduce_sum.19 = f32[3456]{0:T(1024)} reduce(f32[64,1,3456]{2,1,0:T(1,128)S(1)} %all_to_all.11, f32[]{:T(128)} %constant.0.clone.1), dimensions={0,1}, to_apply=%region_1.0 | reduce | flops 217728 | bytes 898564 | tf_op jit(solution)/shard_map/reduce_sum | solution.py:155
  (2 shorter events, 0.0 us)
Async XLA Ops:
  0.6 18.4 %collective-permute-start.1 = (bf16[4,640,128]{2,1,0:T(8,128)(2,1)}, bf16[4,640,128]{2,1,0:T(8,128)(2,1)S(1)}, u32[]{:S(2)}, u32[]{:S(2)}) collective-permute-start(bf16[4,640,128]{2,1,0:T(8,128)(2,1)} %bitcast.17), channel_id=1, source_target_pairs={{2,0},{4,2},{6,4},{8,6},{10,8},{12,10},{14,12},{16,14},{18,16},{20... | collective-permute-start | bytes 1966088 | tf_op jit(solution)/shard_map/ppermute | solution.py:118
  1.9 18.4 %collective-permute-start = (bf16[4,640,128]{2,1,0:T(8,128)(2,1)}, bf16[4,640,128]{2,1,0:T(8,128)(2,1)S(1)}, u32[]{:S(2)}, u32[]{:S(2)}) collective-permute-start(bf16[4,640,128]{2,1,0:T(8,128)(2,1)} %bitcast.18), channel_id=1, source_target_pairs={{0,2},{2,4},{4,6},{6,8},{8,10},{10,12},{12,14},{14,16},{16,18},{18... | collective-permute-start | bytes 1966088 | tf_op jit(solution)/shard_map/ppermute | solution.py:118
  7.5 17.4 %copy-start = (bf16[4,1,640,128]{3,2,1,0:T(8,128)(2,1)S(1)}, bf16[4,1,640,128]{3,2,1,0:T(8,128)(2,1)}, u32[]{:S(2)}) copy-start(bf16[4,1,640,128]{3,2,1,0:T(8,128)(2,1)} %param.5) | copy-start | bytes 1966084
  7.6 17.4 %copy-start.1 = (bf16[3,3,3,128,128]{4,3,2,1,0:T(8,128)(2,1)S(1)}, bf16[3,3,3,128,128]{4,3,2,1,0:T(8,128)(2,1)}, u32[]{:S(2)}) copy-start(bf16[3,3,3,128,128]{4,3,2,1,0:T(8,128)(2,1)} %param.6) | copy-start | bytes 2654212
  7.6 17.4 %copy-start.2 = (bf16[4,1,640,128]{3,2,1,0:T(8,128)(2,1)S(1)}, bf16[4,1,640,128]{3,2,1,0:T(8,128)(2,1)}, u32[]{:S(2)}) copy-start(bf16[4,1,640,128]{3,2,1,0:T(8,128)(2,1)} %param.4) | copy-start | bytes 1966084
  20.5 4.5 %collective-permute-start.2 = (bf16[3,2,640,128]{3,2,1,0:T(8,128)(2,1)S(1)}, bf16[3,2,640,128]{3,2,1,0:T(8,128)(2,1)S(1)}, u32[]{:S(2)}, u32[]{:S(2)}) collective-permute-start(bf16[3,2,640,128]{3,2,1,0:T(8,128)(2,1)S(1)} %pad_maximum_fusion), channel_id=1, source_target_pairs={{1,0},{3,2},{5,4},{7,6},{9,8},{11,10},{13,12},{15,14},{17,16},{19,... | collective-permute-start | bytes 2949128 | tf_op jit(solution)/shard_map/ppermute | solution.py:16

commit v18 on v17

--- a/solution.py
+++ b/solution.py
@@ -29,13 +29,13 @@
     return x
 
 
-def local_kernel(factor, own_ref, up_ref, down_ref, bnd_ref, k_ref, feat_ref, gf_ref, term_ref, z_ref, a_ref, w_ref, cat_ref, acc_ref):
+def local_kernel(factor, own_ref, up_ref, down_ref, late_up_ref, late_own_ref, late_down_ref, k_ref, feat_ref, gf_ref, term_ref, z_ref, a_ref, w_ref, cat_ref, acc_ref):
     frames, breadth, channels = feat_ref.shape
 
     def slab(frame, row):
         if frame < frames:
             return (up_ref, own_ref, down_ref)[row][frame]
-        return bnd_ref[row, frame - frames]
+        return (late_up_ref, late_own_ref, late_down_ref)[row][frame - frames]
 
     def block(n):
         return slice(n * channels, (n + 1) * channels)
@@ -122,11 +122,16 @@
     frames, height, breadth, channels = features.shape
     own = cotangent[:, 0]
     above, below = row_neighbours(own, "ha")
-    boundary = passed_along(jnp.stack([above[:2], own[:2], below[:2]]), "ta", -1)
+    early = own[:2]
+    joint = ("ha", "ta")
+    rows_count, cores = lax.axis_size("ha"), lax.axis_size("ta")
+    late_up = lax.ppermute(early, joint, [((h - 1) * cores + 1, h * cores) for h in range(1, rows_count)])
+    late_down = lax.ppermute(early, joint, [((h + 1) * cores + 1, h * cores) for h in range(rows_count - 1)])
+    late_own = passed_along(early, "ta", -1)
     total_cells = frames * height * breadth * lax.axis_size("ha") * lax.axis_size("ta")
     factor = float(total_cells) ** (-0.5)
     weights = kernel.reshape(-1, channels, channels)
-    grad_features, term = local_grads((own, above, below, boundary), weights, features[:, 0], factor)
+    grad_features, term = local_grads((own, above, below, late_up, late_own, late_down), weights, features[:, 0], factor)
     term = term.reshape(-1, channels)
     owners = lax.axis_size("ha") * lax.axis_size("ta")
     rows = term.shape[0] // owners

time: 77.6 us -> 80 us (1.031)
  waiting for transfers between devices: 15.9 us -> 11.8 us
  local copies, waits for them, and re-layouts: 4.03 us -> 7.31 us
  starting transfers between devices: 7.18 us -> 9.15 us
  blocking collectives: 39 us -> 40.3 us
    ppermute x2, waiting for transfers between devices: 12.8 us -> 0.01 us  [row_neighbours(): return (lax.ppermute(x, axis, up), lax.ppermute(x, axis, down))]
    ppermute x0 -> x2, waiting for transfers between devices: none -> 11.8 us  [the longest x1 11.8 us: body(): lax.ppermute(early, joint, [((h + 1) * cores + 1, h * cores) for h in ran...]
    unnamed x6, local copies, waits for them, and re-layouts: 0.02 us -> 3.34 us
    ppermute x1, waiting for transfers between devices: 3.16 us -> 0.01 us  [passed_along(): return lax.ppermute(block, axis, route)]
    ppermute x0 -> x2, starting transfers between devices: none -> 1.97 us  [the longest x1 1.29 us: body(): lax.ppermute(early, joint, [((h + 1) * cores + 1, h * cores) for h in ran...]
    all_to_all x2, blocking collectives: 39 us -> 40.3 us  [reduce_blocks(): part = lax.all_to_all(shaped, axis, 0, 0, tiled=True).sum(0)]
    another operation x3 -> x0, local copies, waits for them, and re-layouts: 1.05 us -> none  [body(): jnp.stack([above[:2], own[:2], below[:2]])]
    slice x0 -> x1, local copies, waits for them, and re-layouts: none -> 1.01 us  [body(): early = own[:2]]
  transfers between devices with their start and end apart: 3 -> 5, of which waited for: 3 -> 1; matrix products, arithmetic and copies ran while one was open for 1% -> 1% of each run, Pallas kernels for 0% -> 0%
where the time goes in v18:
time: 80 us; the launch traced here: 79.6 us
  blocking collectives  40.3 us (50%)
  waiting for transfers between devices  11.8 us (15%)
  starting transfers between devices  9.15 us (11%)
  Pallas kernels  8.93 us (11%)
  local copies, waits for them, and re-layouts  7.31 us (9%)
  other arithmetic  1.45 us (2%)
    all_to_all x2, blocking collectives, reduce_blocks(): part = lax.all_to_all(shaped, axis, 0, 0, tiled=True).sum(0)  40.3 us
    ppermute x1, waiting for transfers between devices, body(): lax.ppermute(early, joint, [((h + 1) * cores + 1, h * cores) for h in ran...  11.8 us
    pallas_call x1, Pallas kernels, local_grads(): pl.pallas_call(lambda *refs: local_kernel(factor, *refs), out_shape=(jax....  8.93 us
    ppermute x2, starting transfers between devices, row_neighbours(): return (lax.ppermute(x, axis, up), lax.ppermute(x, axis, down))  5.88 us
    unnamed x6, local copies, waits for them, and re-layouts  3.34 us
    reshape x1, local copies, waits for them, and re-layouts, reorder(): t = term.reshape((n,) + tuple(sizes) + term.shape[2:])  2.24 us
  transfers between devices with their start and end apart: 5, of which 1 were waited for; matrix products, arithmetic and copies ran while one was open for 1% of the time, Pallas kernels for 0%

profile of v18, /device:TPU:0, one launch (start us, length us, event | category | flops | bytes accessed | tf_op | source)
XLA Modules:
  0.0 79.6 jit_solution(15082820769719676261)
XLA Ops:
  0.6 1.3 %collective-permute-start.1 = (bf16[4,640,128]{2,1,0:T(8,128)(2,1)}, bf16[4,640,128]{2,1,0:T(8,128)(2,1)S(1)}, u32[]{:S(2)}, u32[]{:S(2)}) collective-permute-start(bf16[4,640,128]{2,1,0:T(8,128)(2,1)} %bitcast.13), channel_id=1, source_target_pairs={{2,0},{4,2},{6,4},{8,6},{10,8},{12,10},{14,12},{16,14},{18,16},{20... | collective-permute-start | bytes 1966088 | tf_op jit(solution)/shard_map/ppermute | solution.py:118
  1.9 4.6 %collective-permute-start = (bf16[4,640,128]{2,1,0:T(8,128)(2,1)}, bf16[4,640,128]{2,1,0:T(8,128)(2,1)S(1)}, u32[]{:S(2)}, u32[]{:S(2)}) collective-permute-start(bf16[4,640,128]{2,1,0:T(8,128)(2,1)} %bitcast.14), channel_id=1, source_target_pairs={{0,2},{2,4},{4,6},{6,8},{8,10},{10,12},{12,14},{14,16},{16,18},{18... | collective-permute-start | bytes 1966088 | tf_op jit(solution)/shard_map/ppermute | solution.py:118
  6.5 1.0 %slice_bitcast_fusion = bf16[2,640,128]{2,1,0:T(8,128)(2,1)S(1)} fusion(bf16[4,1,640,128]{3,2,0,1:T(8,128)(2,1)} %bitcast.15), kind=kLoop, calls=%fused_computation | loop fusion | bytes 655360 | tf_op jit(solution)/shard_map/slice | solution.py:125
  7.5 1.3 %collective-permute-start.4 = (bf16[2,640,128]{2,1,0:T(8,128)(2,1)S(1)}, bf16[2,640,128]{2,1,0:T(8,128)(2,1)S(1)}, u32[]{:S(2)}, u32[]{:S(2)}) collective-permute-start(bf16[2,640,128]{2,1,0:T(8,128)(2,1)S(1)} %slice_bitcast_fusion), channel_id=1, source_target_pairs={{3,0},{5,2},{7,4},{9,6},{11,8},{13,10},{15,12},{17,14},{19,16},{21... | collective-permute-start | bytes 983048 | tf_op jit(solution)/shard_map/ppermute | solution.py:129
  8.8 1.3 %collective-permute-start.3 = (bf16[2,640,128]{2,1,0:T(8,128)(2,1)S(1)}, bf16[2,640,128]{2,1,0:T(8,128)(2,1)S(1)}, u32[]{:S(2)}, u32[]{:S(2)}) collective-permute-start(bf16[2,640,128]{2,1,0:T(8,128)(2,1)S(1)} %slice_bitcast_fusion), channel_id=1, source_target_pairs={{1,0},{3,2},{5,4},{7,6},{9,8},{11,10},{13,12},{15,14},{17,16},{19,... | collective-permute-start | bytes 983048 | tf_op jit(solution)/shard_map/ppermute | solution.py:16
  10.1 0.7 collective-permute-start.2
  10.8 11.8 %collective-permute-done.4.refs_5_ = bf16[2,640,128]{2,1,0:T(8,128)(2,1)S(1)} collective-permute-done((bf16[2,640,128]{2,1,0:T(8,128)(2,1)S(1)}, bf16[2,640,128]{2,1,0:T(8,128)(2,1)S(1)}, u32[]{:S(2)}, u32[]{:S(2)}) %collective-permute-start.4) | collective-permute-done | bytes 327712 | tf_op jit(solution)/shard_map/ppermute | solution.py:129
  22.6 0.0 collective-permute-done.3.refs_4_
  22.6 0.0 collective-permute-done.2.refs_3_
  22.6 0.0 collective-permute-done.1.refs_2_
  22.6 0.0 collective-permute-done.refs_1_
  22.6 0.0 copy-start
  22.6 1.1 %copy-done = bf16[4,1,640,128]{3,2,1,0:T(8,128)(2,1)S(1)} copy-done((bf16[4,1,640,128]{3,2,1,0:T(8,128)(2,1)S(1)}, bf16[4,1,640,128]{3,2,1,0:T(8,128)(2,1)}, u32[]{:S(2)}) %copy-start) | copy-done | bytes 655384
  23.7 0.0 copy-start.1
  23.7 1.2 %copy-done.1 = bf16[3,3,3,128,128]{4,3,2,1,0:T(8,128)(2,1)S(1)} copy-done((bf16[3,3,3,128,128]{4,3,2,1,0:T(8,128)(2,1)S(1)}, bf16[3,3,3,128,128]{4,3,2,1,0:T(8,128)(2,1)}, u32[]{:S(2)}) %copy-start.1) | copy-done | bytes 884760
  24.9 0.0 copy-start.2
  24.9 1.1 %copy-done.2 = bf16[4,1,640,128]{3,2,1,0:T(8,128)(2,1)S(1)} copy-done((bf16[4,1,640,128]{3,2,1,0:T(8,128)(2,1)S(1)}, bf16[4,1,640,128]{3,2,1,0:T(8,128)(2,1)}, u32[]{:S(2)}) %copy-start.2) | copy-done | bytes 655384
  26.0 8.9 %shard_map.67 = (bf16[4,640,128]{2,1,0:T(8,128)(2,1)}, f32[9,384,128]{2,1,0:T(8,128)}) custom-call(bf16[4,640,128]{2,1,0:T(8,128)(2,1)S(1)} %bitcast.16, bf16[4,640,128]{2,1,0:T(8,128)(2,1)S(1)} %collective-permute-done.refs_1_, bf16[4,640,128]{2,1,0:T(8,128)(2,1)S(1)} %collective-permute-done.1.refs_2_, ...), custom_call_target="tpu_custom_call" | custom-call | flops 4529848320 | bytes 6914048 | tf_op jit(solution)/shard_map/pallas_call | solution.py:94
  34.9 2.2 %reshape.19 = f32[1,4,4,4,2,3456]{5,4,3,2,1,0:T(2,128)S(1)} reshape(f32[9,384,128]{2,1,0:T(8,128)} %get-tuple-element.6) | data formatting | bytes 3538944 | tf_op jit(solution)/reshape | solution.py:181
  37.1 0.1 copy.12
  37.3 5.9 %all_to_all.10 = f32[2,64,3456]{2,1,0:T(8,128)S(1)} all-to-all(f32[2,64,3456]{2,1,0:T(8,128)S(1)} %copy.12), channel_id=1, replica_groups=mesh['y'=4,'z'=4,'x'=4,'core'=2] {'core'}, dimensions={0} | all-to-all | bytes 3538944 | tf_op jit(solution)/shard_map/all_to_all | solution.py:160
  43.2 0.2 reduce_sum.18
  43.4 0.6 reshape.22
  44.0 34.3 %all_to_all.11 = f32[64,1,3456]{2,1,0:T(1,128)S(1)} all-to-all(f32[64,1,3456]{2,1,0:T(1,128)S(1)} %reshape.22), channel_id=1, replica_groups=mesh['y'=4,'z'=4,'x'=4,'core'=2] {'y','z','x'}, dimensions={0} | all-to-all | bytes 1769472 | tf_op jit(solution)/shard_map/all_to_all | solution.py:160
  78.3 1.3 %reduce_sum.19 = f32[3456]{0:T(1024)} reduce(f32[64,1,3456]{2,1,0:T(1,128)S(1)} %all_to_all.11, f32[]{:T(128)} %constant.0.clone.1), dimensions={0,1}, to_apply=%region_1.0 | reduce | flops 217728 | bytes 898564 | tf_op jit(solution)/shard_map/reduce_sum | solution.py:160
Async XLA Ops:
  0.6 22.0 %collective-permute-start.1 = (bf16[4,640,128]{2,1,0:T(8,128)(2,1)}, bf16[4,640,128]{2,1,0:T(8,128)(2,1)S(1)}, u32[]{:S(2)}, u32[]{:S(2)}) collective-permute-start(bf16[4,640,128]{2,1,0:T(8,128)(2,1)} %bitcast.13), channel_id=1, source_target_pairs={{2,0},{4,2},{6,4},{8,6},{10,8},{12,10},{14,12},{16,14},{18,16},{20... | collective-permute-start | bytes 1966088 | tf_op jit(solution)/shard_map/ppermute | solution.py:118
  1.9 20.7 %collective-permute-start = (bf16[4,640,128]{2,1,0:T(8,128)(2,1)}, bf16[4,640,128]{2,1,0:T(8,128)(2,1)S(1)}, u32[]{:S(2)}, u32[]{:S(2)}) collective-permute-start(bf16[4,640,128]{2,1,0:T(8,128)(2,1)} %bitcast.14), channel_id=1, source_target_pairs={{0,2},{2,4},{4,6},{6,8},{8,10},{10,12},{12,14},{14,16},{16,18},{18... | collective-permute-start | bytes 1966088 | tf_op jit(solution)/shard_map/ppermute | solution.py:118
  7.5 15.0 %collective-permute-start.4 = (bf16[2,640,128]{2,1,0:T(8,128)(2,1)S(1)}, bf16[2,640,128]{2,1,0:T(8,128)(2,1)S(1)}, u32[]{:S(2)}, u32[]{:S(2)}) collective-permute-start(bf16[2,640,128]{2,1,0:T(8,128)(2,1)S(1)} %slice_bitcast_fusion), channel_id=1, source_target_pairs={{3,0},{5,2},{7,4},{9,6},{11,8},{13,10},{15,12},{17,14},{19,16},{21... | collective-permute-start | bytes 983048 | tf_op jit(solution)/shard_map/ppermute | solution.py:129
  8.8 13.8 %collective-permute-start.3 = (bf16[2,640,128]{2,1,0:T(8,128)(2,1)S(1)}, bf16[2,640,128]{2,1,0:T(8,128)(2,1)S(1)}, u32[]{:S(2)}, u32[]{:S(2)}) collective-permute-start(bf16[2,640,128]{2,1,0:T(8,128)(2,1)S(1)} %slice_bitcast_fusion), channel_id=1, source_target_pairs={{1,0},{3,2},{5,4},{7,6},{9,8},{11,10},{13,12},{15,14},{17,16},{19,... | collective-permute-start | bytes 983048 | tf_op jit(solution)/shard_map/ppermute | solution.py:16
  10.1 12.5 %collective-permute-start.2 = (bf16[2,640,128]{2,1,0:T(8,128)(2,1)S(1)}, bf16[2,640,128]{2,1,0:T(8,128)(2,1)S(1)}, u32[]{:S(2)}, u32[]{:S(2)}) collective-permute-start(bf16[2,640,128]{2,1,0:T(8,128)(2,1)S(1)} %slice_bitcast_fusion), channel_id=1, source_target_pairs={{1,2},{3,4},{5,6},{7,8},{9,10},{11,12},{13,14},{15,16},{17,18},{19... | collective-permute-start | bytes 983048 | tf_op jit(solution)/shard_map/ppermute | solution.py:128
  22.6 1.1 %copy-start = (bf16[4,1,640,128]{3,2,1,0:T(8,128)(2,1)S(1)}, bf16[4,1,640,128]{3,2,1,0:T(8,128)(2,1)}, u32[]{:S(2)}) copy-start(bf16[4,1,640,128]{3,2,1,0:T(8,128)(2,1)} %param.5) | copy-start | bytes 1966084
  23.7 1.2 %copy-start.1 = (bf16[3,3,3,128,128]{4,3,2,1,0:T(8,128)(2,1)S(1)}, bf16[3,3,3,128,128]{4,3,2,1,0:T(8,128)(2,1)}, u32[]{:S(2)}) copy-start(bf16[3,3,3,128,128]{4,3,2,1,0:T(8,128)(2,1)} %param.6) | copy-start | bytes 2654212
  24.9 1.1 %copy-start.2 = (bf16[4,1,640,128]{3,2,1,0:T(8,128)(2,1)S(1)}, bf16[4,1,640,128]{3,2,1,0:T(8,128)(2,1)}, u32[]{:S(2)}) copy-start(bf16[4,1,640,128]{3,2,1,0:T(8,128)(2,1)} %param.4) | copy-start | bytes 1966084

commit v19 on v18

--- a/solution.py
+++ b/solution.py
@@ -106,7 +106,7 @@
             pltpu.VMEM((breadth, 3 * channels), jnp.bfloat16),
             pltpu.VMEM((3, 3 * channels, 3 * channels), jnp.float32),
         ],
-        compiler_params=pltpu.CompilerParams(vmem_limit_bytes=48 * 1024 * 1024),
+        compiler_params=pltpu.CompilerParams(vmem_limit_bytes=60 * 1024 * 1024),
         cost_estimate=pl.CostEstimate(flops=flops, bytes_accessed=moved, transcendentals=2 * feat.size),
     )(*operands)
 

time: 80 us -> 79.9 us (level)
  Pallas kernels: 8.93 us -> 11.1 us
  local copies, waits for them, and re-layouts: 7.31 us -> 5.29 us
    pallas_call x1, Pallas kernels: 8.93 us -> 11.1 us  [local_grads(): pl.pallas_call(lambda *refs: local_kernel(factor, *refs), out_shape=(jax....]
    unnamed x6 -> x10, local copies, waits for them, and re-layouts: 3.34 us -> 1.31 us
where the time goes in v19:
time: 79.9 us; the launch traced here: 79.6 us
  blocking collectives  40.1 us (50%)
  waiting for transfers between devices  11.8 us (15%)
  Pallas kernels  11.1 us (14%)
  starting transfers between devices  9.15 us (11%)
  local copies, waits for them, and re-layouts  5.29 us (7%)
  other arithmetic  1.45 us (2%)
    all_to_all x2, blocking collectives, reduce_blocks(): part = lax.all_to_all(shaped, axis, 0, 0, tiled=True).sum(0)  40.1 us
    ppermute x1, waiting for transfers between devices, body(): lax.ppermute(early, joint, [((h + 1) * cores + 1, h * cores) for h in ran...  11.8 us
    pallas_call x1, Pallas kernels, local_grads(): pl.pallas_call(lambda *refs: local_kernel(factor, *refs), out_shape=(jax....  11.1 us
    ppermute x2, starting transfers between devices, row_neighbours(): return (lax.ppermute(x, axis, up), lax.ppermute(x, axis, down))  5.88 us
    reshape x1, local copies, waits for them, and re-layouts, reorder(): t = term.reshape((n,) + tuple(sizes) + term.shape[2:])  2.24 us
  transfers between devices with their start and end apart: 5, of which 1 were waited for; matrix products, arithmetic and copies ran while one was open for 1% of the time, Pallas kernels for 0%

profile of v19, /device:TPU:0, one launch (start us, length us, event | category | flops | bytes accessed | tf_op | source)
XLA Modules:
  0.0 79.6 jit_solution(11978746102437165603)
XLA Ops:
  0.6 1.3 %collective-permute-start.1 = (bf16[4,640,128]{2,1,0:T(8,128)(2,1)}, bf16[4,640,128]{2,1,0:T(8,128)(2,1)S(1)}, u32[]{:S(2)}, u32[]{:S(2)}) collective-permute-start(bf16[4,640,128]{2,1,0:T(8,128)(2,1)} %bitcast.14), channel_id=1, source_target_pairs={{2,0},{4,2},{6,4},{8,6},{10,8},{12,10},{14,12},{16,14},{18,16},{20... | collective-permute-start | bytes 1966088 | tf_op jit(solution)/shard_map/ppermute | solution.py:118
  1.9 4.6 %collective-permute-start = (bf16[4,640,128]{2,1,0:T(8,128)(2,1)}, bf16[4,640,128]{2,1,0:T(8,128)(2,1)S(1)}, u32[]{:S(2)}, u32[]{:S(2)}) collective-permute-start(bf16[4,640,128]{2,1,0:T(8,128)(2,1)} %bitcast.15), channel_id=1, source_target_pairs={{0,2},{2,4},{4,6},{6,8},{8,10},{10,12},{12,14},{14,16},{16,18},{18... | collective-permute-start | bytes 1966088 | tf_op jit(solution)/shard_map/ppermute | solution.py:118
  6.5 1.0 %slice_bitcast_fusion = bf16[2,640,128]{2,1,0:T(8,128)(2,1)S(1)} fusion(bf16[4,1,640,128]{3,2,0,1:T(8,128)(2,1)} %bitcast.16), kind=kLoop, calls=%fused_computation | loop fusion | bytes 655360 | tf_op jit(solution)/shard_map/slice | solution.py:125
  7.5 1.3 %collective-permute-start.4 = (bf16[2,640,128]{2,1,0:T(8,128)(2,1)S(1)}, bf16[2,640,128]{2,1,0:T(8,128)(2,1)S(1)}, u32[]{:S(2)}, u32[]{:S(2)}) collective-permute-start(bf16[2,640,128]{2,1,0:T(8,128)(2,1)S(1)} %slice_bitcast_fusion), channel_id=1, source_target_pairs={{3,0},{5,2},{7,4},{9,6},{11,8},{13,10},{15,12},{17,14},{19,16},{21... | collective-permute-start | bytes 983048 | tf_op jit(solution)/shard_map/ppermute | solution.py:129
  8.8 1.3 %collective-permute-start.3 = (bf16[2,640,128]{2,1,0:T(8,128)(2,1)S(1)}, bf16[2,640,128]{2,1,0:T(8,128)(2,1)S(1)}, u32[]{:S(2)}, u32[]{:S(2)}) collective-permute-start(bf16[2,640,128]{2,1,0:T(8,128)(2,1)S(1)} %slice_bitcast_fusion), channel_id=1, source_target_pairs={{1,0},{3,2},{5,4},{7,6},{9,8},{11,10},{13,12},{15,14},{17,16},{19,... | collective-permute-start | bytes 983048 | tf_op jit(solution)/shard_map/ppermute | solution.py:16
  10.1 0.7 collective-permute-start.2
  10.8 11.8 %collective-permute-done.4.refs_5_ = bf16[2,640,128]{2,1,0:T(8,128)(2,1)S(1)} collective-permute-done((bf16[2,640,128]{2,1,0:T(8,128)(2,1)S(1)}, bf16[2,640,128]{2,1,0:T(8,128)(2,1)S(1)}, u32[]{:S(2)}, u32[]{:S(2)}) %collective-permute-start.4) | collective-permute-done | bytes 327712 | tf_op jit(solution)/shard_map/ppermute | solution.py:129
  22.6 0.0 copy-start.2
  22.6 0.0 collective-permute-done.3.refs_4_
  22.6 0.0 copy-start.3
  22.6 0.0 collective-permute-done.2.refs_3_
  22.6 0.0 copy-start.4
  22.6 0.0 collective-permute-done.1.refs_2_
  22.6 0.0 copy-start
  22.6 0.0 collective-permute-done.refs_1_
  22.6 0.0 copy-start.1
  22.7 0.7 copy-done.2
  23.3 0.1 copy-done.3
  23.4 0.1 copy-done.4
  23.5 0.2 copy-done
  23.7 0.2 copy-done.1
  24.0 11.1 %shard_map.67 = (bf16[4,640,128]{2,1,0:T(8,128)(2,1)}, f32[9,384,128]{2,1,0:T(8,128)}) custom-call(bf16[4,640,128]{2,1,0:T(8,128)(2,1)} %bitcast.17, bf16[4,640,128]{2,1,0:T(8,128)(2,1)} %copy-done.1, bf16[4,640,128]{2,1,0:T(8,128)(2,1)} %copy-done, bf16[2,640,128]{2,1,0:T(8,128)(2,1)} %copy-done.4, bf16[2,640,128]{2,1,0:T(8,128)(2,1)} %copy-done.3, ...), custom_call_target="tpu_custom_call" | custom-call | flops 4529848320 | bytes 6914048 | tf_op jit(solution)/shard_map/pallas_call | solution.py:94
  35.1 2.2 %reshape.19 = f32[1,4,4,4,2,3456]{5,4,3,2,1,0:T(2,128)S(1)} reshape(f32[9,384,128]{2,1,0:T(8,128)} %get-tuple-element.6) | data formatting | bytes 3538944 | tf_op jit(solution)/reshape | solution.py:181
  37.3 0.1 copy.12
  37.5 5.8 %all_to_all.10 = f32[2,64,3456]{2,1,0:T(8,128)S(1)} all-to-all(f32[2,64,3456]{2,1,0:T(8,128)S(1)} %copy.12), channel_id=1, replica_groups=mesh['y'=4,'z'=4,'x'=4,'core'=2] {'core'}, dimensions={0} | all-to-all | bytes 3538944 | tf_op jit(solution)/shard_map/all_to_all | solution.py:160
  43.2 0.2 reduce_sum.18
  43.4 0.6 reshape.22
  44.0 34.3 %all_to_all.11 = f32[64,1,3456]{2,1,0:T(1,128)S(1)} all-to-all(f32[64,1,3456]{2,1,0:T(1,128)S(1)} %reshape.22), channel_id=1, replica_groups=mesh['y'=4,'z'=4,'x'=4,'core'=2] {'y','z','x'}, dimensions={0} | all-to-all | bytes 1769472 | tf_op jit(solution)/shard_map/all_to_all | solution.py:160
  78.3 1.3 %reduce_sum.19 = f32[3456]{0:T(1024)} reduce(f32[64,1,3456]{2,1,0:T(1,128)S(1)} %all_to_all.11, f32[]{:T(128)} %constant.0.clone.1), dimensions={0,1}, to_apply=%region_1.0 | reduce | flops 217728 | bytes 898564 | tf_op jit(solution)/shard_map/reduce_sum | solution.py:160
Async XLA Ops:
  0.6 22.0 %collective-permute-start.1 = (bf16[4,640,128]{2,1,0:T(8,128)(2,1)}, bf16[4,640,128]{2,1,0:T(8,128)(2,1)S(1)}, u32[]{:S(2)}, u32[]{:S(2)}) collective-permute-start(bf16[4,640,128]{2,1,0:T(8,128)(2,1)} %bitcast.14), channel_id=1, source_target_pairs={{2,0},{4,2},{6,4},{8,6},{10,8},{12,10},{14,12},{16,14},{18,16},{20... | collective-permute-start | bytes 1966088 | tf_op jit(solution)/shard_map/ppermute | solution.py:118
  1.9 20.7 %collective-permute-start = (bf16[4,640,128]{2,1,0:T(8,128)(2,1)}, bf16[4,640,128]{2,1,0:T(8,128)(2,1)S(1)}, u32[]{:S(2)}, u32[]{:S(2)}) collective-permute-start(bf16[4,640,128]{2,1,0:T(8,128)(2,1)} %bitcast.15), channel_id=1, source_target_pairs={{0,2},{2,4},{4,6},{6,8},{8,10},{10,12},{12,14},{14,16},{16,18},{18... | collective-permute-start | bytes 1966088 | tf_op jit(solution)/shard_map/ppermute | solution.py:118
  7.5 15.0 %collective-permute-start.4 = (bf16[2,640,128]{2,1,0:T(8,128)(2,1)S(1)}, bf16[2,640,128]{2,1,0:T(8,128)(2,1)S(1)}, u32[]{:S(2)}, u32[]{:S(2)}) collective-permute-start(bf16[2,640,128]{2,1,0:T(8,128)(2,1)S(1)} %slice_bitcast_fusion), channel_id=1, source_target_pairs={{3,0},{5,2},{7,4},{9,6},{11,8},{13,10},{15,12},{17,14},{19,16},{21... | collective-permute-start | bytes 983048 | tf_op jit(solution)/shard_map/ppermute | solution.py:129
  8.8 13.8 %collective-permute-start.3 = (bf16[2,640,128]{2,1,0:T(8,128)(2,1)S(1)}, bf16[2,640,128]{2,1,0:T(8,128)(2,1)S(1)}, u32[]{:S(2)}, u32[]{:S(2)}) collective-permute-start(bf16[2,640,128]{2,1,0:T(8,128)(2,1)S(1)} %slice_bitcast_fusion), channel_id=1, source_target_pairs={{1,0},{3,2},{5,4},{7,6},{9,8},{11,10},{13,12},{15,14},{17,16},{19,... | collective-permute-start | bytes 983048 | tf_op jit(solution)/shard_map/ppermute | solution.py:16
  10.1 12.5 %collective-permute-start.2 = (bf16[2,640,128]{2,1,0:T(8,128)(2,1)S(1)}, bf16[2,640,128]{2,1,0:T(8,128)(2,1)S(1)}, u32[]{:S(2)}, u32[]{:S(2)}) collective-permute-start(bf16[2,640,128]{2,1,0:T(8,128)(2,1)S(1)} %slice_bitcast_fusion), channel_id=1, source_target_pairs={{1,2},{3,4},{5,6},{7,8},{9,10},{11,12},{13,14},{15,16},{17,18},{19... | collective-permute-start | bytes 983048 | tf_op jit(solution)/shard_map/ppermute | solution.py:128
  22.6 0.7 copy-start.2
  22.6 0.9 %copy-start.3 = (bf16[2,640,128]{2,1,0:T(8,128)(2,1)}, bf16[2,640,128]{2,1,0:T(8,128)(2,1)S(1)}, u32[]{:S(2)}) copy-start(bf16[2,640,128]{2,1,0:T(8,128)(2,1)S(1)} %collective-permute-done.3.refs_4_) | copy-start | bytes 983044
  22.6 0.9 %copy-start.4 = (bf16[2,640,128]{2,1,0:T(8,128)(2,1)}, bf16[2,640,128]{2,1,0:T(8,128)(2,1)S(1)}, u32[]{:S(2)}) copy-start(bf16[2,640,128]{2,1,0:T(8,128)(2,1)S(1)} %collective-permute-done.2.refs_3_) | copy-start | bytes 983044
  22.6 1.1 %copy-start = (bf16[4,640,128]{2,1,0:T(8,128)(2,1)}, bf16[4,640,128]{2,1,0:T(8,128)(2,1)S(1)}, u32[]{:S(2)}) copy-start(bf16[4,640,128]{2,1,0:T(8,128)(2,1)S(1)} %collective-permute-done.1.refs_2_) | copy-start | bytes 1966084
  22.6 1.3 %copy-start.1 = (bf16[4,640,128]{2,1,0:T(8,128)(2,1)}, bf16[4,640,128]{2,1,0:T(8,128)(2,1)S(1)}, u32[]{:S(2)}) copy-start(bf16[4,640,128]{2,1,0:T(8,128)(2,1)S(1)} %collective-permute-done.refs_1_) | copy-start | bytes 1966084

commit v20 on v17

--- a/solution.py
+++ b/solution.py
@@ -29,7 +29,7 @@
     return x
 
 
-def local_kernel(factor, own_ref, up_ref, down_ref, bnd_ref, k_ref, feat_ref, gf_ref, term_ref, z_ref, a_ref, w_ref, cat_ref, acc_ref):
+def local_kernel(factor, own_ref, up_ref, down_ref, bnd_ref, k_ref, feat_ref, gf_ref, term_ref, z_ref, a_ref, w_ref, cat_ref, acc_ref, s_ref):
     frames, breadth, channels = feat_ref.shape
 
     def slab(frame, row):
@@ -47,7 +47,8 @@
     lanes = lax.broadcasted_iota(jnp.int32, (channels, breadth), 1)
     for t in range(frames):
         values = feat_ref[t].astype(jnp.float32)
-        active = (values * jax.nn.sigmoid(values)).astype(jnp.bfloat16).astype(jnp.float32)
+        s_ref[t] = jax.nn.sigmoid(values)
+        active = (values * s_ref[t]).astype(jnp.bfloat16).astype(jnp.float32)
         turned = active.T
         a_ref[t, block(0)] = jnp.where(lanes == 0, 0.0, pltpu.roll(turned, 1, 1)).astype(a_ref.dtype)
         a_ref[t, block(1)] = turned.astype(a_ref.dtype)
@@ -77,7 +78,7 @@
             + jnp.where(rows == 0, 0.0, behind)
         )
         values = feat_ref[t].astype(jnp.float32)
-        sigmoid_part = jax.nn.sigmoid(values)
+        sigmoid_part = s_ref[t]
         derivative = sigmoid_part * (1.0 + values * (1.0 - sigmoid_part))
         gf_ref[t] = (own_ref[t].astype(jnp.float32) + derivative * grad_input).astype(gf_ref.dtype)
     for i in range(3):
@@ -105,6 +106,7 @@
             pltpu.VMEM((3, 3 * channels, 3 * channels), jnp.bfloat16),
             pltpu.VMEM((breadth, 3 * channels), jnp.bfloat16),
             pltpu.VMEM((3, 3 * channels, 3 * channels), jnp.float32),
+            pltpu.VMEM((frames, breadth, channels), jnp.float32),
         ],
         compiler_params=pltpu.CompilerParams(vmem_limit_bytes=48 * 1024 * 1024),
         cost_estimate=pl.CostEstimate(flops=flops, bytes_accessed=moved, transcendentals=2 * feat.size),

time: 77.6 us -> 77.6 us (level)
  no operation moved by 1% of the time
where the time goes in v20:
time: 77.6 us; the launch traced here: 77.3 us
  blocking collectives  39 us (50%)
  waiting for transfers between devices  15.9 us (20%)
  Pallas kernels  8.89 us (11%)
  starting transfers between devices  7.18 us (9%)
  local copies, waits for them, and re-layouts  4.03 us (5%)
  other arithmetic  1.56 us (2%)
    all_to_all x2, blocking collectives, reduce_blocks(): part = lax.all_to_all(shaped, axis, 0, 0, tiled=True).sum(0)  39 us
    ppermute x2, waiting for transfers between devices, row_neighbours(): return (lax.ppermute(x, axis, up), lax.ppermute(x, axis, down))  12.8 us
    pallas_call x1, Pallas kernels, local_grads(): pl.pallas_call(lambda *refs: local_kernel(factor, *refs), out_shape=(jax....  8.89 us
    ppermute x2, starting transfers between devices, row_neighbours(): return (lax.ppermute(x, axis, up), lax.ppermute(x, axis, down))  5.88 us
    ppermute x1, waiting for transfers between devices, passed_along(): return lax.ppermute(block, axis, route)  3.16 us
    reshape x1, local copies, waits for them, and re-layouts, reorder(): t = term.reshape((n,) + tuple(sizes) + term.shape[2:])  2.24 us
  transfers between devices with their start and end apart: 3, of which 3 were waited for; matrix products, arithmetic and copies ran while one was open for 1% of the time, Pallas kernels for 0%

profile of v20, /device:TPU:0, one launch (start us, length us, event | category | flops | bytes accessed | tf_op | source)
XLA Modules:
  0.0 77.3 jit_solution(15336887453628752063)
XLA Ops:
  0.6 1.3 %collective-permute-start.1 = (bf16[4,640,128]{2,1,0:T(8,128)(2,1)}, bf16[4,640,128]{2,1,0:T(8,128)(2,1)S(1)}, u32[]{:S(2)}, u32[]{:S(2)}) collective-permute-start(bf16[4,640,128]{2,1,0:T(8,128)(2,1)} %bitcast.17), channel_id=1, source_target_pairs={{2,0},{4,2},{6,4},{8,6},{10,8},{12,10},{14,12},{16,14},{18,16},{20... | collective-permute-start | bytes 1966088 | tf_op jit(solution)/shard_map/ppermute | solution.py:120
  1.9 4.6 %collective-permute-start = (bf16[4,640,128]{2,1,0:T(8,128)(2,1)}, bf16[4,640,128]{2,1,0:T(8,128)(2,1)S(1)}, u32[]{:S(2)}, u32[]{:S(2)}) collective-permute-start(bf16[4,640,128]{2,1,0:T(8,128)(2,1)} %bitcast.18), channel_id=1, source_target_pairs={{0,2},{2,4},{4,6},{6,8},{8,10},{10,12},{12,14},{14,16},{16,18},{18... | collective-permute-start | bytes 1966088 | tf_op jit(solution)/shard_map/ppermute | solution.py:120
  6.5 1.0 %slice_bitcast_fusion.1 = bf16[1,2,640,128]{3,2,1,0:T(8,128)(2,1)S(1)} fusion(bf16[4,1,640,128]{3,2,0,1:T(8,128)(2,1)} %bitcast.19), kind=kLoop, calls=%fused_computation.2 | loop fusion | bytes 655360 | tf_op jit(solution)/shard_map/stack | solution.py:127
  7.5 0.0 copy-start
  7.6 0.0 copy-start.1
  7.6 0.0 copy-start.2
  7.6 11.5 %collective-permute-done.1.refs_2_ = bf16[4,640,128]{2,1,0:T(8,128)(2,1)S(1)} collective-permute-done((bf16[4,640,128]{2,1,0:T(8,128)(2,1)}, bf16[4,640,128]{2,1,0:T(8,128)(2,1)S(1)}, u32[]{:S(2)}, u32[]{:S(2)}) %collective-permute-start.1) | collective-permute-done | bytes 655392 | tf_op jit(solution)/shard_map/ppermute | solution.py:120
  19.1 1.3 %collective-permute-done.refs_1_ = bf16[4,640,128]{2,1,0:T(8,128)(2,1)S(1)} collective-permute-done((bf16[4,640,128]{2,1,0:T(8,128)(2,1)}, bf16[4,640,128]{2,1,0:T(8,128)(2,1)S(1)}, u32[]{:S(2)}, u32[]{:S(2)}) %collective-permute-start) | collective-permute-done | bytes 655392 | tf_op jit(solution)/shard_map/ppermute | solution.py:120
  20.4 0.1 pad_maximum_fusion
  20.5 1.3 %collective-permute-start.2 = (bf16[3,2,640,128]{3,2,1,0:T(8,128)(2,1)S(1)}, bf16[3,2,640,128]{3,2,1,0:T(8,128)(2,1)S(1)}, u32[]{:S(2)}, u32[]{:S(2)}) collective-permute-start(bf16[3,2,640,128]{3,2,1,0:T(8,128)(2,1)S(1)} %pad_maximum_fusion), channel_id=1, source_target_pairs={{1,0},{3,2},{5,4},{7,6},{9,8},{11,10},{13,12},{15,14},{17,16},{19,... | collective-permute-start | bytes 2949128 | tf_op jit(solution)/shard_map/ppermute | solution.py:16
  21.8 3.2 %collective-permute-done.2.refs_3_ = bf16[3,2,640,128]{3,2,1,0:T(8,128)(2,1)S(1)} collective-permute-done((bf16[3,2,640,128]{3,2,1,0:T(8,128)(2,1)S(1)}, bf16[3,2,640,128]{3,2,1,0:T(8,128)(2,1)S(1)}, u32[]{:S(2)}, u32[]{:S(2)}) %collective-permute-start.2) | collective-permute-done | bytes 983072 | tf_op jit(solution)/shard_map/ppermute | solution.py:16
  25.0 0.0 copy-done
  25.0 0.0 copy-done.1
  25.0 0.0 copy-done.2
  25.0 8.9 %shard_map.67 = (bf16[4,640,128]{2,1,0:T(8,128)(2,1)}, f32[9,384,128]{2,1,0:T(8,128)}) custom-call(bf16[4,640,128]{2,1,0:T(8,128)(2,1)S(1)} %bitcast.20, bf16[4,640,128]{2,1,0:T(8,128)(2,1)S(1)} %collective-permute-done.refs_1_, bf16[4,640,128]{2,1,0:T(8,128)(2,1)S(1)} %collective-permute-done.1.refs_2_, ...), custom_call_target="tpu_custom_call" | custom-call | flops 4529848320 | bytes 6914048 | tf_op jit(solution)/shard_map/pallas_call | solution.py:95
  33.9 2.2 %reshape.20 = f32[1,4,4,4,2,3456]{5,4,3,2,1,0:T(2,128)S(1)} reshape(f32[9,384,128]{2,1,0:T(8,128)} %get-tuple-element.6) | data formatting | bytes 3538944 | tf_op jit(solution)/reshape | solution.py:178
  36.1 0.1 copy.12
  36.2 5.2 %all_to_all.10 = f32[2,64,3456]{2,1,0:T(8,128)S(1)} all-to-all(f32[2,64,3456]{2,1,0:T(8,128)S(1)} %copy.12), channel_id=1, replica_groups=mesh['y'=4,'z'=4,'x'=4,'core'=2] {'core'}, dimensions={0} | all-to-all | bytes 3538944 | tf_op jit(solution)/shard_map/all_to_all | solution.py:157
  41.4 0.2 reduce_sum.18
  41.6 0.6 reshape.23
  42.2 33.8 %all_to_all.11 = f32[64,1,3456]{2,1,0:T(1,128)S(1)} all-to-all(f32[64,1,3456]{2,1,0:T(1,128)S(1)} %reshape.23), channel_id=1, replica_groups=mesh['y'=4,'z'=4,'x'=4,'core'=2] {'y','z','x'}, dimensions={0} | all-to-all | bytes 1769472 | tf_op jit(solution)/shard_map/all_to_all | solution.py:157
  76.0 1.3 %reduce_sum.19 = f32[3456]{0:T(1024)} reduce(f32[64,1,3456]{2,1,0:T(1,128)S(1)} %all_to_all.11, f32[]{:T(128)} %constant.0.clone.1), dimensions={0,1}, to_apply=%region_1.0 | reduce | flops 217728 | bytes 898564 | tf_op jit(solution)/shard_map/reduce_sum | solution.py:157
  (2 shorter events, 0.0 us)
Async XLA Ops:
  0.6 18.4 %collective-permute-start.1 = (bf16[4,640,128]{2,1,0:T(8,128)(2,1)}, bf16[4,640,128]{2,1,0:T(8,128)(2,1)S(1)}, u32[]{:S(2)}, u32[]{:S(2)}) collective-permute-start(bf16[4,640,128]{2,1,0:T(8,128)(2,1)} %bitcast.17), channel_id=1, source_target_pairs={{2,0},{4,2},{6,4},{8,6},{10,8},{12,10},{14,12},{16,14},{18,16},{20... | collective-permute-start | bytes 1966088 | tf_op jit(solution)/shard_map/ppermute | solution.py:120
  1.9 18.4 %collective-permute-start = (bf16[4,640,128]{2,1,0:T(8,128)(2,1)}, bf16[4,640,128]{2,1,0:T(8,128)(2,1)S(1)}, u32[]{:S(2)}, u32[]{:S(2)}) collective-permute-start(bf16[4,640,128]{2,1,0:T(8,128)(2,1)} %bitcast.18), channel_id=1, source_target_pairs={{0,2},{2,4},{4,6},{6,8},{8,10},{10,12},{12,14},{14,16},{16,18},{18... | collective-permute-start | bytes 1966088 | tf_op jit(solution)/shard_map/ppermute | solution.py:120
  7.5 17.4 %copy-start = (bf16[4,1,640,128]{3,2,1,0:T(8,128)(2,1)S(1)}, bf16[4,1,640,128]{3,2,1,0:T(8,128)(2,1)}, u32[]{:S(2)}) copy-start(bf16[4,1,640,128]{3,2,1,0:T(8,128)(2,1)} %param.5) | copy-start | bytes 1966084
  7.6 17.4 %copy-start.1 = (bf16[3,3,3,128,128]{4,3,2,1,0:T(8,128)(2,1)S(1)}, bf16[3,3,3,128,128]{4,3,2,1,0:T(8,128)(2,1)}, u32[]{:S(2)}) copy-start(bf16[3,3,3,128,128]{4,3,2,1,0:T(8,128)(2,1)} %param.6) | copy-start | bytes 2654212
  7.6 17.4 %copy-start.2 = (bf16[4,1,640,128]{3,2,1,0:T(8,128)(2,1)S(1)}, bf16[4,1,640,128]{3,2,1,0:T(8,128)(2,1)}, u32[]{:S(2)}) copy-start(bf16[4,1,640,128]{3,2,1,0:T(8,128)(2,1)} %param.4) | copy-start | bytes 1966084
  20.5 4.5 %collective-permute-start.2 = (bf16[3,2,640,128]{3,2,1,0:T(8,128)(2,1)S(1)}, bf16[3,2,640,128]{3,2,1,0:T(8,128)(2,1)S(1)}, u32[]{:S(2)}, u32[]{:S(2)}) collective-permute-start(bf16[3,2,640,128]{3,2,1,0:T(8,128)(2,1)S(1)} %pad_maximum_fusion), channel_id=1, source_target_pairs={{1,0},{3,2},{5,4},{7,6},{9,8},{11,10},{13,12},{15,14},{17,16},{19,... | collective-permute-start | bytes 2949128 | tf_op jit(solution)/shard_map/ppermute | solution.py:16

commit v21 on v17

--- a/solution.py
+++ b/solution.py
@@ -29,13 +29,8 @@
     return x
 
 
-def local_kernel(factor, own_ref, up_ref, down_ref, bnd_ref, k_ref, feat_ref, gf_ref, term_ref, z_ref, a_ref, w_ref, cat_ref, acc_ref):
+def prep_kernel(k_ref, feat_ref, a_ref, w_ref):
     frames, breadth, channels = feat_ref.shape
-
-    def slab(frame, row):
-        if frame < frames:
-            return (up_ref, own_ref, down_ref)[row][frame]
-        return bnd_ref[row, frame - frames]
 
     def block(n):
         return slice(n * channels, (n + 1) * channels)
@@ -54,6 +49,19 @@
         a_ref[t, block(2)] = jnp.where(
             lanes == breadth - 1, 0.0, pltpu.roll(turned, breadth - 1, 1)
         ).astype(a_ref.dtype)
+
+
+def local_kernel(factor, own_ref, up_ref, down_ref, bnd_ref, a_ref, w_ref, feat_ref, gf_ref, term_ref, z_ref, cat_ref, acc_ref):
+    frames, breadth, channels = feat_ref.shape
+
+    def slab(frame, row):
+        if frame < frames:
+            return (up_ref, own_ref, down_ref)[row][frame]
+        return bnd_ref[row, frame - frames]
+
+    def block(n):
+        return slice(n * channels, (n + 1) * channels)
+
     acc_ref[...] = jnp.zeros_like(acc_ref)
     rows = lax.broadcasted_iota(jnp.int32, (breadth, channels), 0)
     for t in range(frames):
@@ -88,7 +96,21 @@
 def local_grads(pieces, weights, feat, factor):
     frames, breadth, channels = feat.shape
     vmem = pl.BlockSpec(memory_space=pltpu.VMEM)
-    operands = tuple(pieces) + (weights, feat)
+    params = pltpu.CompilerParams(vmem_limit_bytes=48 * 1024 * 1024)
+    a, w = pl.pallas_call(
+        prep_kernel,
+        out_shape=(
+            jax.ShapeDtypeStruct((frames, 3 * channels, breadth), jnp.bfloat16),
+            jax.ShapeDtypeStruct((3, 3 * channels, 3 * channels), jnp.bfloat16),
+        ),
+        in_specs=[vmem] * 2,
+        out_specs=(vmem, vmem),
+        compiler_params=params,
+        cost_estimate=pl.CostEstimate(
+            flops=8 * feat.size, bytes_accessed=4 * weights.size + 8 * feat.size, transcendentals=feat.size
+        ),
+    )(weights, feat)
+    operands = tuple(pieces) + (a, w, feat)
     flops = 2 * 2 * frames * 9 * breadth * channels * 3 * channels
     moved = sum(2 * x.size for x in operands) + 2 * feat.size + 4 * 9 * 3 * channels * channels
     return pl.pallas_call(
@@ -101,13 +123,11 @@
         out_specs=(vmem, vmem),
         scratch_shapes=[
             pltpu.VMEM((breadth, 3 * channels), jnp.float32),
-            pltpu.VMEM((frames, 3 * channels, breadth), jnp.bfloat16),
-            pltpu.VMEM((3, 3 * channels, 3 * channels), jnp.bfloat16),
             pltpu.VMEM((breadth, 3 * channels), jnp.bfloat16),
             pltpu.VMEM((3, 3 * channels, 3 * channels), jnp.float32),
         ],
-        compiler_params=pltpu.CompilerParams(vmem_limit_bytes=48 * 1024 * 1024),
-        cost_estimate=pl.CostEstimate(flops=flops, bytes_accessed=moved, transcendentals=2 * feat.size),
+        compiler_params=params,
+        cost_estimate=pl.CostEstimate(flops=flops, bytes_accessed=moved, transcendentals=feat.size),
     )(*operands)
 
 

time: 77.6 us -> 79 us (1.018)
  waiting for transfers between devices: 15.9 us -> 13.8 us
  Pallas kernels: 8.92 us -> 10.9 us
  local copies, waits for them, and re-layouts: 4.03 us -> 5.32 us
    ppermute x1, waiting for transfers between devices: 3.16 us -> 1.01 us  [passed_along(): return lax.ppermute(block, axis, route)]
    unnamed x6 -> x8, local copies, waits for them, and re-layouts: 0.02 us -> 1.31 us
    pallas_call x1, Pallas kernels: 8.92 us -> 10.1 us  [local_grads(): pl.pallas_call(lambda *refs: local_kernel(factor, *refs), out_shape=(jax....]
    pallas_call x0 -> x1, Pallas kernels: none -> 0.83 us  [local_grads(): pl.pallas_call(prep_kernel, out_shape=(jax.ShapeDtypeStruct((frames, 3 *...]
  transfers between devices with their start and end apart: 3 -> 3, of which waited for: 3 -> 3; matrix products, arithmetic and copies ran while one was open for 1% -> 1% of each run, Pallas kernels for 0% -> 1%
where the time goes in v21:
time: 79 us; the launch traced here: 78.6 us
  blocking collectives  39 us (49%)
  waiting for transfers between devices  13.8 us (17%)
  Pallas kernels  10.9 us (14%)
  starting transfers between devices  7.31 us (9%)
  local copies, waits for them, and re-layouts  5.32 us (7%)
  other arithmetic  1.56 us (2%)
    all_to_all x2, blocking collectives, reduce_blocks(): part = lax.all_to_all(shaped, axis, 0, 0, tiled=True).sum(0)  39 us
    ppermute x2, waiting for transfers between devices, row_neighbours(): return (lax.ppermute(x, axis, up), lax.ppermute(x, axis, down))  12.8 us
    pallas_call x1, Pallas kernels, local_grads(): pl.pallas_call(lambda *refs: local_kernel(factor, *refs), out_shape=(jax....  10.1 us
    ppermute x2, starting transfers between devices, row_neighbours(): return (lax.ppermute(x, axis, up), lax.ppermute(x, axis, down))  5.88 us
    reshape x1, local copies, waits for them, and re-layouts, reorder(): t = term.reshape((n,) + tuple(sizes) + term.shape[2:])  2.24 us
  transfers between devices with their start and end apart: 3, of which 3 were waited for; matrix products, arithmetic and copies ran while one was open for 1% of the time, Pallas kernels for 1%

profile of v21, /device:TPU:0, one launch (start us, length us, event | category | flops | bytes accessed | tf_op | source)
XLA Modules:
  0.0 78.6 jit_solution(13427274314446344424)
XLA Ops:
  0.6 1.3 %collective-permute-start.1 = (bf16[4,640,128]{2,1,0:T(8,128)(2,1)}, bf16[4,640,128]{2,1,0:T(8,128)(2,1)S(1)}, u32[]{:S(2)}, u32[]{:S(2)}) collective-permute-start(bf16[4,640,128]{2,1,0:T(8,128)(2,1)} %bitcast.20), channel_id=1, source_target_pairs={{2,0},{4,2},{6,4},{8,6},{10,8},{12,10},{14,12},{16,14},{18,16},{20... | collective-permute-start | bytes 1966088 | tf_op jit(solution)/shard_map/ppermute | solution.py:138
  1.9 4.6 %collective-permute-start = (bf16[4,640,128]{2,1,0:T(8,128)(2,1)}, bf16[4,640,128]{2,1,0:T(8,128)(2,1)S(1)}, u32[]{:S(2)}, u32[]{:S(2)}) collective-permute-start(bf16[4,640,128]{2,1,0:T(8,128)(2,1)} %bitcast.21), channel_id=1, source_target_pairs={{0,2},{2,4},{4,6},{6,8},{8,10},{10,12},{12,14},{14,16},{16,18},{18... | collective-permute-start | bytes 1966088 | tf_op jit(solution)/shard_map/ppermute | solution.py:138
  6.5 1.0 %slice_bitcast_fusion.1 = bf16[1,2,640,128]{3,2,1,0:T(8,128)(2,1)S(1)} fusion(bf16[4,1,640,128]{3,2,0,1:T(8,128)(2,1)} %bitcast.22), kind=kLoop, calls=%fused_computation.2 | loop fusion | bytes 655360 | tf_op jit(solution)/shard_map/stack | solution.py:145
  7.5 0.0 copy-start
  7.6 0.0 copy-start.1
  7.6 11.5 %collective-permute-done.1.refs_2_ = bf16[4,640,128]{2,1,0:T(8,128)(2,1)S(1)} collective-permute-done((bf16[4,640,128]{2,1,0:T(8,128)(2,1)}, bf16[4,640,128]{2,1,0:T(8,128)(2,1)S(1)}, u32[]{:S(2)}, u32[]{:S(2)}) %collective-permute-start.1) | collective-permute-done | bytes 655392 | tf_op jit(solution)/shard_map/ppermute | solution.py:138
  19.1 1.3 %collective-permute-done.refs_1_ = bf16[4,640,128]{2,1,0:T(8,128)(2,1)S(1)} collective-permute-done((bf16[4,640,128]{2,1,0:T(8,128)(2,1)}, bf16[4,640,128]{2,1,0:T(8,128)(2,1)S(1)}, u32[]{:S(2)}, u32[]{:S(2)}) %collective-permute-start) | collective-permute-done | bytes 655392 | tf_op jit(solution)/shard_map/ppermute | solution.py:138
  20.4 0.0 copy-start.2
  20.4 0.1 pad_maximum_fusion
  20.5 1.4 %collective-permute-start.2 = (bf16[3,2,640,128]{3,2,1,0:T(8,128)(2,1)S(1)}, bf16[3,2,640,128]{3,2,1,0:T(8,128)(2,1)S(1)}, u32[]{:S(2)}, u32[]{:S(2)}) collective-permute-start(bf16[3,2,640,128]{3,2,1,0:T(8,128)(2,1)S(1)} %pad_maximum_fusion), channel_id=1, source_target_pairs={{1,0},{3,2},{5,4},{7,6},{9,8},{11,10},{13,12},{15,14},{17,16},{19,... | collective-permute-start | bytes 2949128 | tf_op jit(solution)/shard_map/ppermute | solution.py:16
  22.0 0.0 copy-done
  22.0 0.0 copy-done.1
  22.0 0.8 %shard_map.67 = (bf16[4,384,640]{2,1,0:T(8,128)(2,1)S(1)}, bf16[3,384,384]{2,1,0:T(8,128)(2,1)S(1)}) custom-call(bf16[27,128,128]{2,1,0:T(8,128)(2,1)S(1)} %bitcast.17, bf16[4,640,128]{2,1,0:T(8,128)(2,1)S(1)} %bitcast.18), custom_call_target="tpu_custom_call" | custom-call | flops 2621440 | bytes 4390912 | tf_op jit(solution)/shard_map/pallas_call | solution.py:100
  22.8 0.0 copy-start.3
  22.8 1.3 %copy-done.3 = bf16[4,384,640]{2,1,0:T(8,128)(2,1)} copy-done((bf16[4,384,640]{2,1,0:T(8,128)(2,1)}, bf16[4,384,640]{2,1,0:T(8,128)(2,1)S(1)}, u32[]{:S(2)}) %copy-start.3) | copy-done | bytes 1966104
  24.1 1.0 %collective-permute-done.2.refs_3_ = bf16[3,2,640,128]{3,2,1,0:T(8,128)(2,1)S(1)} collective-permute-done((bf16[3,2,640,128]{3,2,1,0:T(8,128)(2,1)S(1)}, bf16[3,2,640,128]{3,2,1,0:T(8,128)(2,1)S(1)}, u32[]{:S(2)}, u32[]{:S(2)}) %collective-permute-start.2) | collective-permute-done | bytes 983072 | tf_op jit(solution)/shard_map/ppermute | solution.py:16
  25.1 0.0 copy-done.2
  25.1 10.1 %shard_map.68 = (bf16[4,640,128]{2,1,0:T(8,128)(2,1)}, f32[9,384,128]{2,1,0:T(8,128)}) custom-call(bf16[4,640,128]{2,1,0:T(8,128)(2,1)S(1)} %bitcast.23, bf16[4,640,128]{2,1,0:T(8,128)(2,1)S(1)} %collective-permute-done.refs_1_, bf16[4,640,128]{2,1,0:T(8,128)(2,1)S(1)} %collective-permute-done.1.refs_2_, ...), custom_call_target="tpu_custom_call" | custom-call | flops 4529848320 | bytes 8880128 | tf_op jit(solution)/shard_map/pallas_call | solution.py:116
  35.2 2.2 %reshape.20 = f32[1,4,4,4,2,3456]{5,4,3,2,1,0:T(2,128)S(1)} reshape(f32[9,384,128]{2,1,0:T(8,128)} %get-tuple-element.10) | data formatting | bytes 3538944 | tf_op jit(solution)/reshape | solution.py:196
  37.4 0.1 copy.12
  37.6 5.2 %all_to_all.10 = f32[2,64,3456]{2,1,0:T(8,128)S(1)} all-to-all(f32[2,64,3456]{2,1,0:T(8,128)S(1)} %copy.12), channel_id=1, replica_groups=mesh['y'=4,'z'=4,'x'=4,'core'=2] {'core'}, dimensions={0} | all-to-all | bytes 3538944 | tf_op jit(solution)/shard_map/all_to_all | solution.py:175
  42.7 0.2 reduce_sum.18
  42.9 0.6 reshape.23
  43.5 33.8 %all_to_all.11 = f32[64,1,3456]{2,1,0:T(1,128)S(1)} all-to-all(f32[64,1,3456]{2,1,0:T(1,128)S(1)} %reshape.23), channel_id=1, replica_groups=mesh['y'=4,'z'=4,'x'=4,'core'=2] {'y','z','x'}, dimensions={0} | all-to-all | bytes 1769472 | tf_op jit(solution)/shard_map/all_to_all | solution.py:175
  77.4 1.3 %reduce_sum.19 = f32[3456]{0:T(1024)} reduce(f32[64,1,3456]{2,1,0:T(1,128)S(1)} %all_to_all.11, f32[]{:T(128)} %constant.0.clone.1), dimensions={0,1}, to_apply=%region_1.0 | reduce | flops 217728 | bytes 898564 | tf_op jit(solution)/shard_map/reduce_sum | solution.py:175
  (2 shorter events, 0.0 us)
Async XLA Ops:
  0.6 18.4 %collective-permute-start.1 = (bf16[4,640,128]{2,1,0:T(8,128)(2,1)}, bf16[4,640,128]{2,1,0:T(8,128)(2,1)S(1)}, u32[]{:S(2)}, u32[]{:S(2)}) collective-permute-start(bf16[4,640,128]{2,1,0:T(8,128)(2,1)} %bitcast.20), channel_id=1, source_target_pairs={{2,0},{4,2},{6,4},{8,6},{10,8},{12,10},{14,12},{16,14},{18,16},{20... | collective-permute-start | bytes 1966088 | tf_op jit(solution)/shard_map/ppermute | solution.py:138
  1.9 18.4 %collective-permute-start = (bf16[4,640,128]{2,1,0:T(8,128)(2,1)}, bf16[4,640,128]{2,1,0:T(8,128)(2,1)S(1)}, u32[]{:S(2)}, u32[]{:S(2)}) collective-permute-start(bf16[4,640,128]{2,1,0:T(8,128)(2,1)} %bitcast.21), channel_id=1, source_target_pairs={{0,2},{2,4},{4,6},{6,8},{8,10},{10,12},{12,14},{14,16},{16,18},{18... | collective-permute-start | bytes 1966088 | tf_op jit(solution)/shard_map/ppermute | solution.py:138
  7.5 14.4 %copy-start = (bf16[3,3,3,128,128]{4,3,2,1,0:T(8,128)(2,1)S(1)}, bf16[3,3,3,128,128]{4,3,2,1,0:T(8,128)(2,1)}, u32[]{:S(2)}) copy-start(bf16[3,3,3,128,128]{4,3,2,1,0:T(8,128)(2,1)} %param.6) | copy-start | bytes 2654212
  7.6 14.4 %copy-start.1 = (bf16[4,1,640,128]{3,2,1,0:T(8,128)(2,1)S(1)}, bf16[4,1,640,128]{3,2,1,0:T(8,128)(2,1)}, u32[]{:S(2)}) copy-start(bf16[4,1,640,128]{3,2,1,0:T(8,128)(2,1)} %param.4) | copy-start | bytes 1966084
  20.4 4.7 %copy-start.2 = (bf16[4,1,640,128]{3,2,1,0:T(8,128)(2,1)S(1)}, bf16[4,1,640,128]{3,2,1,0:T(8,128)(2,1)}, u32[]{:S(2)}) copy-start(bf16[4,1,640,128]{3,2,1,0:T(8,128)(2,1)} %param.5) | copy-start | bytes 1966084
  20.5 4.6 %collective-permute-start.2 = (bf16[3,2,640,128]{3,2,1,0:T(8,128)(2,1)S(1)}, bf16[3,2,640,128]{3,2,1,0:T(8,128)(2,1)S(1)}, u32[]{:S(2)}, u32[]{:S(2)}) collective-permute-start(bf16[3,2,640,128]{3,2,1,0:T(8,128)(2,1)S(1)} %pad_maximum_fusion), channel_id=1, source_target_pairs={{1,0},{3,2},{5,4},{7,6},{9,8},{11,10},{13,12},{15,14},{17,16},{19,... | collective-permute-start | bytes 2949128 | tf_op jit(solution)/shard_map/ppermute | solution.py:16
  22.8 1.3 %copy-start.3 = (bf16[4,384,640]{2,1,0:T(8,128)(2,1)}, bf16[4,384,640]{2,1,0:T(8,128)(2,1)S(1)}, u32[]{:S(2)}) copy-start(bf16[4,384,640]{2,1,0:T(8,128)(2,1)S(1)} %get-tuple-element.7.refs_4_) | copy-start | bytes 5898244
